TPU v7x, 32 devices: a whole 2x2x4 slice. The times are simulated.
32 devices in a mesh: grp: 2 (over y), frame: 4 (over x, core), coil: 4 (over z).
Axes of the slice: x: 2, y: 2, z: 4, core: 2. Of those that a mesh axis runs over, the one named last changes fastest.
Arguments:
- images: bfloat16 [8, 2, 384, 384], P(('grp', 'frame')), parts along dimension 0, may hold values from -6 to 6
- coil_maps: bfloat16 [8, 2, 384, 384], P(('grp', 'coil')), parts along dimension 0, may hold values from -3 to 3
- kspace_data: float32 [8, 4, 2, 6, 128], P(('grp', 'frame'), 'coil'), parts along dimension 0, may hold values from -6 to 6
- spoke_angle: int32 [8, 6], P(('grp', 'frame')), parts along dimension 0, may hold values from 0 to 15
- band_row: int32 [8, 6], P(('grp', 'frame')), parts along dimension 0, may hold values from 0 to 256
- band_col: int32 [8, 6], P(('grp', 'frame')), parts along dimension 0, may hold values from 0 to 256
- kernel_rows: bfloat16 [16, 128, 128], replicated, may hold values from -0.5 to 0.5
- kernel_cols: bfloat16 [16, 128, 128], replicated, may hold values from -0.5 to 0.5
Outputs:
- updated: float32 [8, 2, 384, 384], P(('grp', 'frame')), parts along dimension 0
There are 2 independent parts, one for each index of `grp`. A program takes and returns all parts, laid end to end along the dimension named above; an argument that names none is the same for every part. Nothing has to cross between parts.
All inputs are finite; a program needn't handle non-finite values.
Results may differ from a plain program's by a relative error of at most 0.0014.
Values may be sent and summed in bfloat16 or wider, within the bound.
No kernel may reach another device: no remote copies, remote signals or barrier semaphores. Data moves between devices by JAX's collectives and lax.ppermute only.
A program may use at most 64 MiB of HBM per device.

v0:
```python
import math

import jax
import ml_dtypes
import numpy as np
import jax.numpy as jnp
from jax import lax
from jax.sharding import PartitionSpec as P


SMOOTHING = 0.05
STEP_SIZE = 1.0
TV_WEIGHT = 0.2


def padded(cells, sides, width):
    for axis, dim in sides:
        count = lax.axis_size(axis)
        ends = count - 1
        head = lax.slice_in_dim(cells, 0, width, axis=dim)
        tail = lax.slice_in_dim(cells, cells.shape[dim] - width, cells.shape[dim], axis=dim)
        cells = jnp.concatenate(
            [
                lax.ppermute(tail, axis, [(i, (i + 1) % count) for i in range(ends)]),
                cells,
                lax.ppermute(head, axis, [((i + 1) % count, i) for i in range(ends)]),
            ],
            axis=dim,
        )
    return cells


def transform_table(extent):
    indices = np.arange(extent, dtype=np.int64)
    phases = (indices[:, None] * indices[None, :] % extent).astype(np.float32)
    angle_values = np.float32(2.0 * math.pi / extent) * phases
    scaling = np.float32(1.0 / math.sqrt(extent))
    table = np.stack([np.cos(angle_values) * scaling, np.sin(angle_values) * scaling])
    return jnp.asarray(table.astype(ml_dtypes.bfloat16))


def combine_parts(products, direction):
    real_part = products[0, 0] + direction * products[1, 1]
    imaginary = products[0, 1] - direction * products[1, 0]
    return jnp.stack([real_part, imaginary])


def rotated(block, coil_count, shift):
    return lax.ppermute(block, "coil", [(i, (i + shift) % coil_count) for i in range(coil_count)])


def exchange_rows(coil_map, rows, coil_count, coil_index):
    received = [lax.dynamic_slice_in_dim(coil_map, coil_index * rows, rows, axis=1)]
    for shift in range(1, coil_count):
        target = (coil_index + shift) % coil_count
        block = lax.dynamic_slice_in_dim(coil_map, target * rows, rows, axis=1)
        received.append(rotated(block, coil_count, shift))
    return jnp.stack(received)


def selector(first_index, extent, patch_side):
    positions = jnp.arange(extent, dtype=jnp.int32)
    offsets = jnp.arange(patch_side, dtype=jnp.int32)
    wanted = first_index[:, None, None] + offsets[None, None, :]
    return (positions[None, :, None] == wanted).astype(jnp.bfloat16)


def pick_kernels(kernels, angle_ids):
    choice = (angle_ids[:, None] == jnp.arange(kernels.shape[0], dtype=jnp.int32)[None, :])
    flat = kernels.reshape(kernels.shape[0], -1)
    picked = jnp.dot(choice.astype(kernels.dtype), flat, preferred_element_type=jnp.float32)
    return picked.astype(kernels.dtype).reshape((angle_ids.shape[0],) + kernels.shape[1:])


def forward_residual(transform, frame_image, coil_map, measured, row_placed, col_placed):
    map_planes = coil_map.astype(jnp.float32)
    image_planes = frame_image.astype(jnp.float32)
    coil_image = jnp.stack(
        [
            map_planes[0] * image_planes[0] - map_planes[1] * image_planes[1],
            map_planes[0] * image_planes[1] + map_planes[1] * image_planes[0],
        ]
    ).astype(jnp.bfloat16)
    products = jnp.einsum(
        "bij,ajk->abik", coil_image, transform, preferred_element_type=jnp.float32
    )
    half_done = combine_parts(products, 1.0).astype(jnp.bfloat16)
    products = jnp.einsum("aij,bjk->abik", transform, half_done, preferred_element_type=jnp.float32)
    kspace = combine_parts(products, 1.0).astype(jnp.bfloat16)
    contracted = jnp.einsum("pik,gjk->pgij", kspace, col_placed, preferred_element_type=jnp.float32)
    predicted = jnp.sum(contracted * row_placed.astype(jnp.float32)[None], axis=2)
    return predicted - measured


def backward_rows(transform, residuals, map_rows, row_select, row_w, col_placed, coil_index):
    rows = map_rows.shape[2]
    spread = (row_w.astype(jnp.float32)[None, None] * residuals[:, :, :, None, :]).astype(jnp.bfloat16)
    placed = jnp.einsum(
        "cpgrj,gjk->cpgrk", spread, col_placed, preferred_element_type=jnp.float32
    ).astype(jnp.bfloat16)
    row_table = lax.dynamic_slice_in_dim(transform, coil_index * rows, rows, axis=1)
    table_at = jnp.einsum(
        "aij,gjr->aigr", row_table, row_select, preferred_element_type=jnp.float32
    ).astype(jnp.bfloat16)
    products = jnp.einsum("aigr,cbgrk->abcik", table_at, placed, preferred_element_type=jnp.float32)
    half_back = combine_parts(products, -1.0).astype(jnp.bfloat16)
    products = jnp.einsum("bcij,ajk->abcik", half_back, transform, preferred_element_type=jnp.float32)
    coil_back = combine_parts(products, -1.0)
    maps = map_rows.astype(jnp.float32)
    real_part = jnp.sum(maps[:, 0] * coil_back[0] + maps[:, 1] * coil_back[1], axis=0)
    imaginary = jnp.sum(maps[:, 0] * coil_back[1] - maps[:, 1] * coil_back[0], axis=0)
    return jnp.stack([real_part, imaginary])


def tv_term(extended, first_frame, frame_total):
    widened = extended.astype(jnp.float32)
    change = widened[1:] - widened[:-1]
    position = first_frame - 1 + jnp.arange(change.shape[0], dtype=jnp.int32)
    inside = ((position >= 0) & (position <= frame_total - 2)).astype(jnp.float32)
    normed = inside[:, None, None, None] * (
        change / jnp.sqrt(jnp.sum(change * change, axis=1, keepdims=True) + SMOOTHING)
    )
    return normed[:-1] - normed[1:]


def normed_change(later, earlier, valid):
    change = later.astype(jnp.float32) - earlier.astype(jnp.float32)
    scale = jnp.sqrt(change[0] * change[0] + change[1] * change[1] + SMOOTHING)
    return valid * (change / scale)


def tv_single(images, frame_index, frame_total):
    count = lax.axis_size("frame")
    image = images[0]
    earlier = lax.ppermute(image, "frame", [(i, i + 1) for i in range(count - 1)])
    later = lax.ppermute(image, "frame", [(i + 1, i) for i in range(count - 1)])
    has_earlier = (frame_index >= 1).astype(jnp.float32)
    has_later = (frame_index <= frame_total - 2).astype(jnp.float32)
    return (normed_change(image, earlier, has_earlier) - normed_change(later, image, has_later))[None]


def body(
    images, coil_maps, kspace_data, spoke_angle, band_row, band_col, kernel_rows, kernel_cols
):
    frame_count = images.shape[0]
    extent = images.shape[-1]
    patch_side = kernel_cols.shape[-1]
    coil_count = lax.axis_size("coil")
    coil_index = lax.axis_index("coil")
    rows = extent // coil_count
    transform = transform_table(extent)
    map_rows = exchange_rows(coil_maps[0], rows, coil_count, coil_index)
    first_frame = lax.axis_index("frame") * frame_count
    frame_total = lax.axis_size("frame") * frame_count
    if frame_count == 1:
        tv_grad = tv_single(images, first_frame, frame_total)
    else:
        tv_grad = tv_term(padded(images, (("frame", 0),), 1), first_frame, frame_total)
    row_w = pick_kernels(kernel_rows, spoke_angle[0])
    col_w = pick_kernels(kernel_cols, spoke_angle[0])
    row_select = selector(band_row[0], extent, patch_side)
    col_select = selector(band_col[0], extent, patch_side)
    exact = dict(preferred_element_type=jnp.float32)
    col_placed = jnp.einsum("gjq,gkq->gjk", col_w, col_select, **exact).astype(jnp.bfloat16)
    row_placed = jnp.einsum("grj,gir->gij", row_w, row_select, **exact).astype(jnp.bfloat16)
    residual = forward_residual(
        transform, images[0], coil_maps[0], kspace_data[0, 0], row_placed, col_placed
    )
    residuals = jnp.stack(
        [residual] + [rotated(residual, coil_count, shift) for shift in range(1, coil_count)]
    )
    grad_rows = backward_rows(
        transform, residuals, map_rows, row_select, row_w, col_placed, coil_index
    )
    tv_grad, grad_rows = lax.optimization_barrier((tv_grad, grad_rows.astype(jnp.bfloat16)))
    data_grad = lax.all_gather(grad_rows, "coil", axis=1, tiled=True).astype(jnp.float32)[None]
    return images.astype(jnp.float32) - STEP_SIZE * (data_grad + TV_WEIGHT * tv_grad)


def solution(mesh):
    in_specs = (
        P(("grp", "frame"), None, None, None),
        P(("grp", "coil"), None, None, None),
        P(("grp", "frame"), "coil", None, None, None),
        P(("grp", "frame"), None),
        P(("grp", "frame"), None),
        P(("grp", "frame"), None),
        P(),
        P(),
    )
    out_specs = P(("grp", "frame"), None, None, None)
    return jax.shard_map(body, mesh=mesh, in_specs=in_specs, out_specs=out_specs, check_vma=False)
```

profile of v0, /device:TPU:0, one launch (start us, length us, event | category | flops | bytes accessed | tf_op | source)
XLA Modules:
  0.0 59.4 jit_solution(14672326287005543459)
XLA Ops:
  0.0 1.2 %bitcast_convert_fusion.1 = f32[2,384,384]{2,1,0:T(8,128)S(1)} fusion(bf16[1,2,384,384]{3,2,1,0:T(8,128)(2,1)} %param.9), kind=kLoop, calls=%fused_computation.131 | loop fusion | flops 294912 | bytes 1769472 | tf_op jit(solution)/shard_map/convert_element_type | solution.py:127
  1.5 0.9 %copy-done.1 = bf16[2,384,384,1]{2,1,0,3:T(8,128)(2,1)S(1)} copy-done((bf16[2,384,384,1]{2,1,0,3:T(8,128)(2,1)S(1)}, bf16[2,384,384,1]{2,1,0,3:T(8,128)(2,1)}, u32[]{:S(2)}) %copy-start.1) | copy-done | bytes 589848
  2.4 0.8 %convolution_bitcast_fusion.2 = f32[2,2,384,384]{3,2,0,1:T(8,128)S(1)} fusion(bf16[2,384,384,1]{2,1,0,3:T(8,128)(2,1)S(1)} %copy-done.1, bf16[1,384,384]{2,1,0:T(8,128)(2,1)S(1)} %get-tuple-element.12, bf16[1,384,384]{2,1,0:T(8,128)(2,1)S(1)} %get-tuple-element.11), kind=kOutput, calls=%fused_computation.12 | convolution fusion | flops 454164480 | bytes 3538944 | tf_op jit(solution)/shard_map/bij,ajk->abik/dot_general | solution.py:84
  3.3 0.8 %convolution_bitcast_fusion.1 = f32[2,2,384,384]{2,3,0,1:T(8,128)S(1)} fusion(bf16[2,384,384,1]{2,1,0,3:T(8,128)(2,1)S(1)} %copy-done.1, bf16[1,384,384]{2,1,0:T(8,128)(2,1)S(1)} %fusion.64, bf16[1,384,384]{2,1,0:T(8,128)(2,1)S(1)} %fusion.63), kind=kOutput, calls=%fused_computation.11 | convolution fusion | flops 454164480 | bytes 3538944 | tf_op jit(solution)/shard_map/aij,bjk->abik/dot_general | solution.py:88
  4.2 0.8 %fusion.66 = bf16[1,384,384]{1,2,0:T(8,128)(2,1)} fusion(f32[2,2,384,384]{2,3,0,1:T(8,128)S(1)} %convolution_bitcast_fusion.1), kind=kLoop, calls=%fused_computation.101 | loop fusion | flops 294912 | bytes 1474560 | tf_op jit(solution)/shard_map/sub | solution.py:44
  5.2 0.4 fusion.21
  5.6 0.3 fusion.13
  5.9 1.4 %copy.17 = f32[6,384,128]{1,2,0:T(8,128)} copy(f32[6,384,128]{2,1,0:T(8,128)S(1)} %fusion.13) | data formatting | bytes 2359296 | tf_op jit(solution)/shard_map/convert_element_type | solution.py:91
  7.3 0.4 fusion.20
  7.8 0.4 convolution_convert_fusion.3
  8.2 0.4 copy-done.3
  8.6 0.9 %fusion.5 = f32[2,6,128]{2,0,1:T(2,128)S(1)} fusion(f32[6,384,128]{1,2,0:T(8,128)S(1)} %copy-done.3, bf16[1,384,384]{1,2,0:T(8,128)(2,1)S(1)} %copy-done.8, bf16[1,384,384]{1,2,0:T(8,128)(2,1)S(1)} %fusion.65, bf16[6,128,384]{2,1,0:T(8,128)(2,1)S(1)} %convolution_convert_fusion.3), kind=kOutput, calls=%fused_computation.8 | convolution fusion | flops 455342592 | bytes 2365440 | tf_op jit(solution)/shard_map/pik,gjk->pgij/dot_general | solution.py:90
  9.5 3.1 %collective-permute-start.5 = (f32[2,6,128]{2,0,1:T(2,128)S(1)}, f32[2,6,128]{2,0,1:T(2,128)S(1)}, u32[]{:S(2)}, u32[]{:S(2)}) collective-permute-start(f32[2,6,128]{2,0,1:T(2,128)S(1)} %bitcast_subtract_fusion), channel_id=1, source_target_pairs={{0,1},{1,2},{2,3},{3,0},{4,5},{5,6},{6,7},{7,4},{8,9},{9,10},{10,1... | collective-permute-start | bytes 18440 | tf_op jit(solution)/shard_map/ppermute | solution.py:49
  12.6 2.6 %collective-permute-start.6 = (f32[2,6,128]{2,0,1:T(2,128)S(1)}, f32[2,6,128]{2,0,1:T(2,128)S(1)}, u32[]{:S(2)}, u32[]{:S(2)}) collective-permute-start(f32[2,6,128]{2,0,1:T(2,128)S(1)} %bitcast_subtract_fusion), channel_id=1, source_target_pairs={{0,2},{1,3},{2,0},{3,1},{4,6},{5,7},{6,4},{7,5},{8,10},{9,11},{10,... | collective-permute-start | bytes 18440 | tf_op jit(solution)/shard_map/ppermute | solution.py:49
  15.2 1.3 %collective-permute-start.7 = (f32[2,6,128]{2,0,1:T(2,128)S(1)}, f32[2,6,128]{2,0,1:T(2,128)S(1)}, u32[]{:S(2)}, u32[]{:S(2)}) collective-permute-start(f32[2,6,128]{2,0,1:T(2,128)S(1)} %bitcast_subtract_fusion), channel_id=1, source_target_pairs={{0,3},{1,0},{2,1},{3,2},{4,7},{5,4},{6,5},{7,6},{8,11},{9,8},{10,9... | collective-permute-start | bytes 18440 | tf_op jit(solution)/shard_map/ppermute | solution.py:49
  16.6 1.3 %collective-permute-start = (bf16[2,384,384]{2,1,0:T(8,128)(2,1)S(1)}, bf16[2,384,384]{2,1,0:T(8,128)(2,1)S(1)}, u32[]{:S(2)}, u32[]{:S(2)}) collective-permute-start(bf16[2,384,384]{2,1,0:T(8,128)(2,1)S(1)} %bitcast.233), channel_id=1, source_target_pairs={{0,4},{4,8},{8,12},{1,5},{5,9},{9,13},{2,6},{6,10},{10,14},{3,7},{... | collective-permute-start | bytes 1769480 | tf_op jit(solution)/shard_map/ppermute | solution.py:135
  17.9 1.3 %collective-permute-start.1 = (bf16[2,384,384]{2,1,0:T(8,128)(2,1)S(1)}, bf16[2,384,384]{2,1,0:T(8,128)(2,1)S(1)}, u32[]{:S(2)}, u32[]{:S(2)}) collective-permute-start(bf16[2,384,384]{2,1,0:T(8,128)(2,1)S(1)} %bitcast.234), channel_id=1, source_target_pairs={{4,0},{8,4},{12,8},{5,1},{9,5},{13,9},{6,2},{10,6},{14,10},{7,3},{... | collective-permute-start | bytes 1769480 | tf_op jit(solution)/shard_map/ppermute | solution.py:136
  19.2 0.8 %bitcast_convert_fusion = f32[6,128,128]{2,1,0:T(8,128)} fusion(bf16[1,6,128,128]{3,1,2,0:T(8,128)(2,1)S(1)} %fusion.21), kind=kLoop, calls=%fused_computation.105 | loop fusion | flops 98304 | bytes 589824 | tf_op jit(solution)/shard_map/convert_element_type | solution.py:97
  20.0 2.1 %fusion.17 = bf16[2,96,6,128,1,1]{3,1,2,0,5,4:T(8,128)(2,1)} fusion(s32[6,128]{1,0:T(8,128)S(1)} %iota_add_fusion, bf16[2,384,384]{2,1,0:T(8,128)(2,1)} %constant.52.clone, s32[]{:T(128)S(6)} %select_n.28), kind=kOutput, calls=%fused_computation.27 | convolution fusion | flops 113688576 | bytes 445444 | tf_op jit(solution)/shard_map/aij,gjr->aigr/dot_general | solution.py:102
  22.0 0.8 %dynamic-slice_bitcast_fusion.2 = (bf16[2,96,384]{2,1,0:T(8,128)(2,1)}, bf16[2,96,384]{2,1,0:T(8,128)(2,1)}, bf16[2,96,384]{2,1,0:T(8,128)(2,1)}) fusion(bf16[1,2,384,384]{3,2,1,0:T(8,128)(2,1)S(1)} %copy-done.2, s32[]{:T(128)S(6)} %select_n.30, s32[]{:T(128)S(6)} %select_n.32, s32[]{:T(128)S(6)} %select_n.34), kind=kLoop, calls=%fused_computation.113 | loop fusion | bytes 884748 | tf_op jit(solution)/shard_map/dynamic_slice | solution.py:56
  22.9 0.5 collective-permute-start.4
  23.4 1.6 %collective-permute-start.2 = (bf16[2,96,384]{2,1,0:T(8,128)(2,1)}, bf16[2,96,384]{2,1,0:T(8,128)(2,1)}, u32[]{:S(2)}, u32[]{:S(2)}) collective-permute-start(bf16[2,96,384]{2,1,0:T(8,128)(2,1)} %get-tuple-element.13), channel_id=1, source_target_pairs={{0,1},{1,2},{2,3},{3,0},{4,5},{5,6},{6,7},{7,4},{8,9},{9,10},{10,1... | collective-permute-start | bytes 442376 | tf_op jit(solution)/shard_map/ppermute | solution.py:49
  25.2 4.7 %fusion.6 = f32[2,2,4,96,384]{4,3,0,1,2:T(8,128)} fusion(bf16[2,96,6,128,1,1]{3,1,2,0,5,4:T(8,128)(2,1)} %fusion.17, f32[4,2,6,128]{3,2,1,0:T(8,128)S(1)} %copy.18, f32[6,128,128]{2,1,0:T(8,128)S(1)} %copy-done.7, bf16[6,128,384]{2,1,0:T(8,128)(2,1)S(1)} %convolution_convert_fusion.3), kind=kOutput, calls=%fused_computation.9 | convolution fusion | flops 1513881600 | bytes 3661824 | tf_op jit(solution)/shard_map/aigr,cbgrk->abcik/dot_general | solution.py:105
  29.9 1.4 %fusion.67 = bf16[1,4,96,384]{3,2,1,0:T(8,128)(2,1)S(1)} fusion(f32[2,2,4,96,384]{4,3,0,1,2:T(8,128)} %fusion.6), kind=kLoop, calls=%fused_computation.102 | loop fusion | flops 442368 | bytes 1474560 | tf_op jit(solution)/shard_map/add | solution.py:43
  31.3 1.3 %fusion.68 = bf16[1,4,96,384]{3,2,1,0:T(8,128)(2,1)S(1)} fusion(f32[2,2,4,96,384]{4,3,0,1,2:T(8,128)} %fusion.6), kind=kLoop, calls=%fused_computation.103 | loop fusion | flops 442368 | bytes 1474560 | tf_op jit(solution)/shard_map/sub | solution.py:44
  32.6 0.8 %convolution_bitcast_fusion = f32[2,2,4,96,384]{4,3,2,1,0:T(8,128)S(1)} fusion(bf16[2,384,384,1,1]{2,1,4,3,0:T(8,128)(2,1)S(1)} %copy-done.4, bf16[1,4,96,384]{3,2,1,0:T(8,128)(2,1)S(1)} %fusion.68, bf16[1,4,96,384]{3,2,1,0:T(8,128)(2,1)S(1)} %fusion.67), kind=kOutput, calls=%fused_computation.10 | convolution fusion | flops 454164480 | bytes 3538944 | tf_op jit(solution)/shard_map/bcij,ajk->abcik/dot_general | solution.py:107
  33.4 5.5 %collective-permute-done.3 = bf16[2,96,384]{2,1,0:T(8,128)(2,1)} collective-permute-done((bf16[2,96,384]{2,1,0:T(8,128)(2,1)}, bf16[2,96,384]{2,1,0:T(8,128)(2,1)}, u32[]{:S(2)}, u32[]{:S(2)}) %collective-permute-start.3) | collective-permute-done | bytes 147488 | tf_op jit(solution)/shard_map/ppermute | solution.py:49
  38.9 1.2 %maximum_convert_fusion = f32[4,2,96,384]{3,2,0,1:T(8,128)S(1)} fusion(bf16[1,2,96,384]{3,2,0,1:T(8,128)(2,1)} %bitcast.10, bf16[1,2,96,384]{3,2,0,1:T(8,128)(2,1)} %bitcast.8, bf16[1,2,96,384]{3,2,0,1:T(8,128)(2,1)} %bitcast.6, bf16[1,2,96,384]{3,2,0,1:T(8,128)(2,1)S(1)} %constant_dynamic-slice_fusion), kind=kLoop, calls=%fused_computation.72 | loop fusion | flops 1179648 | bytes 1769472 | tf_op jit(solution)/shard_map/convert_element_type | solution.py:109
  40.6 0.4 fusion.40
  41.0 0.5 subtract_bitcast_fusion
  41.5 16.7 %all_gather.3 = bf16[2,384,384]{2,1,0:T(8,128)(2,1)S(1)} all-gather(bf16[2,96,384]{2,1,0:T(8,128)(2,1)S(1)} %pad_maximum_fusion), channel_id=1, replica_groups=mesh['grp'=2,'frame'=4,'coil'=4] {'coil'}, dimensions={1}, use_global_device_ids=true | all-gather | bytes 737280 | tf_op jit(solution)/shard_map/all_gather | solution.py:176
  58.1 1.3 %fusion.14 = f32[1,2,384,384]{3,2,1,0:T(8,128)} fusion(f32[1,2,384,384]{3,2,1,0:T(8,128)S(1)} %subtract_bitcast_fusion, bf16[1,2,384,384]{3,2,1,0:T(8,128)(2,1)S(1)} %copy-done, bf16[2,384,384]{2,1,0:T(8,128)(2,1)S(1)} %all_gather.3), kind=kLoop, calls=%fused_computation.20 | loop fusion | flops 1474560 | bytes 3538944 | tf_op jit(solution)/shard_map/sub | solution.py:177
  (47 shorter events, 1.6 us)
Async XLA Ops:
  0.0 1.2 %copy-start.2 = (bf16[1,2,384,384]{3,2,1,0:T(8,128)(2,1)S(1)}, bf16[1,2,384,384]{3,2,1,0:T(8,128)(2,1)}, u32[]{:S(2)}) copy-start(bf16[1,2,384,384]{3,2,1,0:T(8,128)(2,1)} %param.10) | copy-start | bytes 1769476
  1.3 1.1 %copy-start.1 = (bf16[2,384,384,1]{2,1,0,3:T(8,128)(2,1)S(1)}, bf16[2,384,384,1]{2,1,0,3:T(8,128)(2,1)}, u32[]{:S(2)}) copy-start(bf16[2,384,384,1]{2,1,0,3:T(8,128)(2,1)} %constant.59) | copy-start | bytes 1769476
  4.1 0.9 %copy-start.11 = (s32[1,6]{1,0:T(1,128)S(1)}, s32[1,6]{1,0:T(1,128)}, u32[]{:S(2)}) copy-start(s32[1,6]{1,0:T(1,128)} %param.13) | copy-start | bytes 76
  4.1 1.0 %copy-start.5 = (bf16[16,128,128]{2,1,0:T(8,128)(2,1)S(1)}, bf16[16,128,128]{2,1,0:T(8,128)(2,1)}, u32[]{:S(2)}) copy-start(bf16[16,128,128]{2,1,0:T(8,128)(2,1)} %param.15) | copy-start | bytes 1572868
  4.1 1.0 %copy-start.10 = (s32[1,6]{1,0:T(1,128)S(1)}, s32[1,6]{1,0:T(1,128)}, u32[]{:S(2)}) copy-start(s32[1,6]{1,0:T(1,128)} %param.12) | copy-start | bytes 76
  5.9 1.4 %copy-start.6 = (bf16[16,128,128]{2,1,0:T(8,128)(2,1)S(1)}, bf16[16,128,128]{2,1,0:T(8,128)(2,1)}, u32[]{:S(2)}) copy-start(bf16[16,128,128]{2,1,0:T(8,128)(2,1)} %param.16) | copy-start | bytes 1572868
  5.9 1.8 %copy-start.12 = (s32[1,6]{1,0:T(1,128)S(1)}, s32[1,6]{1,0:T(1,128)}, u32[]{:S(2)}) copy-start(s32[1,6]{1,0:T(1,128)} %param.14) | copy-start | bytes 76
  7.3 1.3 %copy-start.3 = (f32[6,384,128]{1,2,0:T(8,128)S(1)}, f32[6,384,128]{1,2,0:T(8,128)}, u32[]{:S(2)}) copy-start(f32[6,384,128]{1,2,0:T(8,128)} %copy.17) | copy-start | bytes 3538948
  7.3 1.3 %copy-start.8 = (bf16[1,384,384]{1,2,0:T(8,128)(2,1)S(1)}, bf16[1,384,384]{1,2,0:T(8,128)(2,1)}, u32[]{:S(2)}) copy-start(bf16[1,384,384]{1,2,0:T(8,128)(2,1)} %fusion.66) | copy-start | bytes 884740
  8.6 0.9 %copy-start.9 = (f32[1,1,2,6,128]{4,2,3,1,0:T(2,128)S(1)}, f32[1,1,2,6,128]{4,2,3,1,0:T(2,128)}, u32[]{:S(2)}) copy-start(f32[1,1,2,6,128]{4,2,3,1,0:T(2,128)} %param.11) | copy-start | bytes 18436
  8.6 7.9 %copy-start = (bf16[1,2,384,384]{3,2,1,0:T(8,128)(2,1)S(1)}, bf16[1,2,384,384]{3,2,1,0:T(8,128)(2,1)}, u32[]{:S(2)}) copy-start(bf16[1,2,384,384]{3,2,1,0:T(8,128)(2,1)} %param.9) | copy-start | bytes 1769476
  9.5 13.3 %collective-permute-start.5 = (f32[2,6,128]{2,0,1:T(2,128)S(1)}, f32[2,6,128]{2,0,1:T(2,128)S(1)}, u32[]{:S(2)}, u32[]{:S(2)}) collective-permute-start(f32[2,6,128]{2,0,1:T(2,128)S(1)} %bitcast_subtract_fusion), channel_id=1, source_target_pairs={{0,1},{1,2},{2,3},{3,0},{4,5},{5,6},{6,7},{7,4},{8,9},{9,10},{10,1... | collective-permute-start | bytes 18440 | tf_op jit(solution)/shard_map/ppermute | solution.py:49
  12.6 10.7 %collective-permute-start.6 = (f32[2,6,128]{2,0,1:T(2,128)S(1)}, f32[2,6,128]{2,0,1:T(2,128)S(1)}, u32[]{:S(2)}, u32[]{:S(2)}) collective-permute-start(f32[2,6,128]{2,0,1:T(2,128)S(1)} %bitcast_subtract_fusion), channel_id=1, source_target_pairs={{0,2},{1,3},{2,0},{3,1},{4,6},{5,7},{6,4},{7,5},{8,10},{9,11},{10,... | collective-permute-start | bytes 18440 | tf_op jit(solution)/shard_map/ppermute | solution.py:49
  15.2 9.7 %collective-permute-start.7 = (f32[2,6,128]{2,0,1:T(2,128)S(1)}, f32[2,6,128]{2,0,1:T(2,128)S(1)}, u32[]{:S(2)}, u32[]{:S(2)}) collective-permute-start(f32[2,6,128]{2,0,1:T(2,128)S(1)} %bitcast_subtract_fusion), channel_id=1, source_target_pairs={{0,3},{1,0},{2,1},{3,2},{4,7},{5,4},{6,5},{7,6},{8,11},{9,8},{10,9... | collective-permute-start | bytes 18440 | tf_op jit(solution)/shard_map/ppermute | solution.py:49
  16.6 23.8 %collective-permute-start = (bf16[2,384,384]{2,1,0:T(8,128)(2,1)S(1)}, bf16[2,384,384]{2,1,0:T(8,128)(2,1)S(1)}, u32[]{:S(2)}, u32[]{:S(2)}) collective-permute-start(bf16[2,384,384]{2,1,0:T(8,128)(2,1)S(1)} %bitcast.233), channel_id=1, source_target_pairs={{0,4},{4,8},{8,12},{1,5},{5,9},{9,13},{2,6},{6,10},{10,14},{3,7},{... | collective-permute-start | bytes 1769480 | tf_op jit(solution)/shard_map/ppermute | solution.py:135
  17.9 22.5 %collective-permute-start.1 = (bf16[2,384,384]{2,1,0:T(8,128)(2,1)S(1)}, bf16[2,384,384]{2,1,0:T(8,128)(2,1)S(1)}, u32[]{:S(2)}, u32[]{:S(2)}) collective-permute-start(bf16[2,384,384]{2,1,0:T(8,128)(2,1)S(1)} %bitcast.234), channel_id=1, source_target_pairs={{4,0},{8,4},{12,8},{5,1},{9,5},{13,9},{6,2},{10,6},{14,10},{7,3},{... | collective-permute-start | bytes 1769480 | tf_op jit(solution)/shard_map/ppermute | solution.py:136
  20.0 5.2 %copy-start.7 = (f32[6,128,128]{2,1,0:T(8,128)S(1)}, f32[6,128,128]{2,1,0:T(8,128)}, u32[]{:S(2)}) copy-start(f32[6,128,128]{2,1,0:T(8,128)} %bitcast_convert_fusion) | copy-start | bytes 1179652
  22.9 10.5 %collective-permute-start.4 = (bf16[2,96,384]{2,1,0:T(8,128)(2,1)}, bf16[2,96,384]{2,1,0:T(8,128)(2,1)}, u32[]{:S(2)}, u32[]{:S(2)}) collective-permute-start(bf16[2,96,384]{2,1,0:T(8,128)(2,1)} %get-tuple-element.15), channel_id=1, source_target_pairs={{0,3},{1,0},{2,1},{3,2},{4,7},{5,4},{6,5},{7,6},{8,11},{9,8},{10,9... | collective-permute-start | bytes 442376 | tf_op jit(solution)/shard_map/ppermute | solution.py:49
  23.4 10.0 %collective-permute-start.2 = (bf16[2,96,384]{2,1,0:T(8,128)(2,1)}, bf16[2,96,384]{2,1,0:T(8,128)(2,1)}, u32[]{:S(2)}, u32[]{:S(2)}) collective-permute-start(bf16[2,96,384]{2,1,0:T(8,128)(2,1)} %get-tuple-element.13), channel_id=1, source_target_pairs={{0,1},{1,2},{2,3},{3,0},{4,5},{5,6},{6,7},{7,4},{8,9},{9,10},{10,1... | collective-permute-start | bytes 442376 | tf_op jit(solution)/shard_map/ppermute | solution.py:49
  25.0 13.9 %collective-permute-start.3 = (bf16[2,96,384]{2,1,0:T(8,128)(2,1)}, bf16[2,96,384]{2,1,0:T(8,128)(2,1)}, u32[]{:S(2)}, u32[]{:S(2)}) collective-permute-start(bf16[2,96,384]{2,1,0:T(8,128)(2,1)} %get-tuple-element.14), channel_id=1, source_target_pairs={{0,2},{1,3},{2,0},{3,1},{4,6},{5,7},{6,4},{7,5},{8,10},{9,11},{10,... | collective-permute-start | bytes 442376 | tf_op jit(solution)/shard_map/ppermute | solution.py:49
  29.9 2.7 %copy-start.4 = (bf16[2,384,384,1,1]{2,1,4,3,0:T(8,128)(2,1)S(1)}, bf16[2,384,384,1,1]{2,1,4,3,0:T(8,128)(2,1)}, u32[]{:S(2)}) copy-start(bf16[2,384,384,1,1]{2,1,4,3,0:T(8,128)(2,1)} %constant.60) | copy-start | bytes 1769476
where the time goes:
time: 59.8 us; the launch traced here: 59.4 us
  blocking collectives  16.7 us (28%)
  starting transfers between devices  11.9 us (20%)
  matrix products  11.5 us (19%)
  other arithmetic  9.84 us (16%)
  waiting for transfers between devices  5.49 us (9%)
  local copies, waits for them, and re-layouts  3.69 us (6%)
    all_gather x1, blocking collectives, body(): lax.all_gather(grad_rows, 'coil', axis=1, tiled=True).astype(jnp.float32)  16.7 us
    ppermute x6, starting transfers between devices, rotated(): lax.ppermute(block, 'coil', [(i, (i + shift) % coil_count) for i in range...  9.31 us
    ppermute x6, waiting for transfers between devices, rotated(): lax.ppermute(block, 'coil', [(i, (i + shift) % coil_count) for i in range...  5.48 us
    dot_general x1, matrix products, backward_rows(): jnp.einsum('aigr,cbgrk->abcik', table_at, placed, preferred_element_type=...  4.72 us
    sub x3, other arithmetic, combine_parts(): imaginary = products[0, 1] - direction * products[1, 0]  2.14 us
    dot_general x1, matrix products, backward_rows(): jnp.einsum('aij,gjr->aigr', row_table, row_select, preferred_element_type...  2.06 us
    unnamed x26, local copies, waits for them, and re-layouts  1.51 us
    add x3, other arithmetic, combine_parts(): real_part = products[0, 0] + direction * products[1, 1]  1.49 us
  transfers between devices with their start and end apart: 8, of which 1 were waited for; matrix products, arithmetic and copies ran while one was open for 22% of the time, Pallas kernels for 0%

commit v1 on v0

--- a/solution.py
+++ b/solution.py
@@ -93,22 +93,30 @@
 
 
 def backward_rows(transform, residuals, map_rows, row_select, row_w, col_placed, coil_index):
-    rows = map_rows.shape[2]
+    coil_count, _, rows, extent = map_rows.shape
     spread = (row_w.astype(jnp.float32)[None, None] * residuals[:, :, :, None, :]).astype(jnp.bfloat16)
     placed = jnp.einsum(
-        "cpgrj,gjk->cpgrk", spread, col_placed, preferred_element_type=jnp.float32
+        "cpgrj,gjk->pgrck", spread, col_placed, preferred_element_type=jnp.float32
     ).astype(jnp.bfloat16)
     row_table = lax.dynamic_slice_in_dim(transform, coil_index * rows, rows, axis=1)
-    table_at = jnp.einsum(
-        "aij,gjr->aigr", row_table, row_select, preferred_element_type=jnp.float32
+    cos_rows, sin_rows = row_table[0], row_table[1]
+    block = jnp.stack(
+        [jnp.stack([cos_rows, -sin_rows], axis=1), jnp.stack([sin_rows, cos_rows], axis=1)]
+    )
+    block_at = jnp.einsum(
+        "oibj,gjr->oibgr", block, row_select, preferred_element_type=jnp.float32
     ).astype(jnp.bfloat16)
-    products = jnp.einsum("aigr,cbgrk->abcik", table_at, placed, preferred_element_type=jnp.float32)
-    half_back = combine_parts(products, -1.0).astype(jnp.bfloat16)
-    products = jnp.einsum("bcij,ajk->abcik", half_back, transform, preferred_element_type=jnp.float32)
+    tiles, patch_side = row_select.shape[0], row_select.shape[2]
+    half_back = jnp.dot(
+        block_at.reshape(2 * rows, 2 * tiles * patch_side),
+        placed.reshape(2 * tiles * patch_side, coil_count * extent),
+        preferred_element_type=jnp.float32,
+    ).astype(jnp.bfloat16).reshape(2, rows, coil_count, extent)
+    products = jnp.einsum("bicj,ajk->abick", half_back, transform, preferred_element_type=jnp.float32)
     coil_back = combine_parts(products, -1.0)
-    maps = map_rows.astype(jnp.float32)
-    real_part = jnp.sum(maps[:, 0] * coil_back[0] + maps[:, 1] * coil_back[1], axis=0)
-    imaginary = jnp.sum(maps[:, 0] * coil_back[1] - maps[:, 1] * coil_back[0], axis=0)
+    maps = jnp.transpose(map_rows, (1, 2, 0, 3)).astype(jnp.float32)
+    real_part = jnp.sum(maps[0] * coil_back[0] + maps[1] * coil_back[1], axis=1)
+    imaginary = jnp.sum(maps[0] * coil_back[1] - maps[1] * coil_back[0], axis=1)
     return jnp.stack([real_part, imaginary])
 
 

time: 59.8 us -> 73.9 us (1.24)
  the two profiles are of different devices: /device:TPU:0 before, /device:TPU:2 now
where the time goes in v1:
time: 73.9 us; the launch traced here: 73.2 us
  local copies, waits for them, and re-layouts  20.1 us (27%)
  blocking collectives  16.6 us (22%)
  matrix products  13.4 us (18%)
  starting transfers between devices  13.4 us (18%)
  other arithmetic  9.36 us (13%)
    all_gather x1, blocking collectives, body(): lax.all_gather(grad_rows, 'coil', axis=1, tiled=True).astype(jnp.float32)  16.6 us
    convert_element_type x1, local copies, waits for them, and re-layouts, backward_rows(): placed = jnp.einsum('cpgrj,gjk->pgrck', spread, col_placed, preferred_ele...  8.46 us
    ppermute x6, starting transfers between devices, rotated(): lax.ppermute(block, 'coil', [(i, (i + shift) % coil_count) for i in range...  7.88 us
    unnamed x33, local copies, waits for them, and re-layouts  4.35 us
    dot_general x1, matrix products, backward_rows(): jnp.einsum('cpgrj,gjk->pgrck', spread, col_placed, preferred_element_type...  4.32 us
    ppermute x1, starting transfers between devices, tv_single(): later = lax.ppermute(image, 'frame', [(i + 1, i) for i in range(count - 1)])  3.64 us
    dot_general x1, matrix products, backward_rows(): jnp.dot(block_at.reshape(2 * rows, 2 * tiles * patch_side), placed.reshap...  1.93 us
    ppermute x1, starting transfers between devices, tv_single(): lax.ppermute(image, 'frame', [(i, i + 1) for i in range(count - 1)])  1.91 us
  transfers between devices with their start and end apart: 8, of which 0 were waited for; matrix products, arithmetic and copies ran while one was open for 41% of the time, Pallas kernels for 0%

profile of v1, /device:TPU:2, one launch (start us, length us, event | category | flops | bytes accessed | tf_op | source)
XLA Modules:
  0.0 73.2 jit_solution(17821345270183482129)
XLA Ops:
  0.0 1.2 %bitcast_convert_fusion.1 = f32[2,384,384]{2,1,0:T(8,128)S(1)} fusion(bf16[1,2,384,384]{3,2,1,0:T(8,128)(2,1)} %param.9), kind=kLoop, calls=%fused_computation.122 | loop fusion | flops 294912 | bytes 1769472 | tf_op jit(solution)/shard_map/convert_element_type | solution.py:135
  1.5 0.9 %copy-done.1 = bf16[2,384,384,1]{2,1,0,3:T(8,128)(2,1)S(1)} copy-done((bf16[2,384,384,1]{2,1,0,3:T(8,128)(2,1)S(1)}, bf16[2,384,384,1]{2,1,0,3:T(8,128)(2,1)}, u32[]{:S(2)}) %copy-start.1) | copy-done | bytes 589848
  2.4 0.8 %convolution_bitcast_fusion.2 = f32[2,2,384,384]{3,2,0,1:T(8,128)S(1)} fusion(bf16[2,384,384,1]{2,1,0,3:T(8,128)(2,1)S(1)} %copy-done.1, bf16[1,384,384]{2,1,0:T(8,128)(2,1)S(1)} %get-tuple-element.12, bf16[1,384,384]{2,1,0:T(8,128)(2,1)S(1)} %get-tuple-element.11), kind=kOutput, calls=%fused_computation.9 | convolution fusion | flops 454164480 | bytes 3538944 | tf_op jit(solution)/shard_map/bij,ajk->abik/dot_general | solution.py:84
  3.3 0.8 %convolution_bitcast_fusion.1 = f32[2,2,384,384]{2,3,0,1:T(8,128)S(1)} fusion(bf16[2,384,384,1]{2,1,0,3:T(8,128)(2,1)S(1)} %copy-done.1, bf16[1,384,384]{2,1,0:T(8,128)(2,1)S(1)} %fusion.45, bf16[1,384,384]{2,1,0:T(8,128)(2,1)S(1)} %fusion.44), kind=kOutput, calls=%fused_computation.8 | convolution fusion | flops 454164480 | bytes 3538944 | tf_op jit(solution)/shard_map/aij,bjk->abik/dot_general | solution.py:88
  4.2 0.8 %fusion.46 = bf16[1,384,384]{1,2,0:T(8,128)(2,1)} fusion(f32[2,2,384,384]{2,3,0,1:T(8,128)S(1)} %convolution_bitcast_fusion.1), kind=kLoop, calls=%fused_computation.88 | loop fusion | flops 294912 | bytes 1474560 | tf_op jit(solution)/shard_map/add | solution.py:43
  4.9 0.8 %fusion.47 = bf16[1,384,384]{1,2,0:T(8,128)(2,1)} fusion(f32[2,2,384,384]{2,3,0,1:T(8,128)S(1)} %convolution_bitcast_fusion.1), kind=kLoop, calls=%fused_computation.89 | loop fusion | flops 294912 | bytes 1474560 | tf_op jit(solution)/shard_map/sub | solution.py:44
  6.9 1.5 %fusion.7 = bf16[1,6,128,128]{3,1,2,0:T(8,128)(2,1)S(1)} fusion(bf16[2,8,128,128]{3,2,1,0:T(8,128)(2,1)} %bitcast.239, s32[6]{0:T(128)S(1)} %bitcast.244), kind=kOutput, calls=%fused_computation.25 | convolution fusion | flops 3244128 | bytes 720920 | tf_op jit(solution)/shard_map/dot_general | solution.py:71
  9.0 0.9 %fusion = f32[2,6,128]{2,0,1:T(2,128)S(1)} fusion(f32[6,384,128]{1,2,0:T(8,128)S(1)} %copy.32, bf16[1,384,384]{1,2,0:T(8,128)(2,1)S(1)} %copy-done.11, bf16[1,384,384]{1,2,0:T(8,128)(2,1)S(1)} %copy-done.10, bf16[6,128,384]{2,1,0:T(8,128)(2,1)S(1)} %convolution_convert_fusion.4), kind=kOutput, calls=%fused_computation.6 | convolution fusion | flops 455342592 | bytes 2365440 | tf_op jit(solution)/shard_map/pik,gjk->pgij/dot_general | solution.py:90
  9.9 0.6 bitcast_subtract_fusion
  10.5 1.6 %collective-permute-start.5 = (f32[2,6,128]{2,0,1:T(2,128)}, f32[2,6,128]{2,0,1:T(2,128)S(1)}, u32[]{:S(2)}, u32[]{:S(2)}) collective-permute-start(f32[2,6,128]{2,0,1:T(2,128)} %bitcast_subtract_fusion), channel_id=1, source_target_pairs={{0,1},{1,2},{2,3},{3,0},{4,5},{5,6},{6,7},{7,4},{8,9},{9,10},{10,1... | collective-permute-start | bytes 18440 | tf_op jit(solution)/shard_map/ppermute | solution.py:49
  12.0 2.6 %collective-permute-start.6 = (f32[2,6,128]{2,0,1:T(2,128)}, f32[2,6,128]{2,0,1:T(2,128)}, u32[]{:S(2)}, u32[]{:S(2)}) collective-permute-start(f32[2,6,128]{2,0,1:T(2,128)} %bitcast_subtract_fusion), channel_id=1, source_target_pairs={{0,2},{1,3},{2,0},{3,1},{4,6},{5,7},{6,4},{7,5},{8,10},{9,11},{10,... | collective-permute-start | bytes 18440 | tf_op jit(solution)/shard_map/ppermute | solution.py:49
  14.6 1.3 %collective-permute-start.7 = (f32[2,6,128]{2,0,1:T(2,128)}, f32[2,6,128]{2,0,1:T(2,128)}, u32[]{:S(2)}, u32[]{:S(2)}) collective-permute-start(f32[2,6,128]{2,0,1:T(2,128)} %bitcast_subtract_fusion), channel_id=1, source_target_pairs={{0,3},{1,0},{2,1},{3,2},{4,7},{5,4},{6,5},{7,6},{8,11},{9,8},{10,9... | collective-permute-start | bytes 18440 | tf_op jit(solution)/shard_map/ppermute | solution.py:49
  16.0 1.9 %collective-permute-start = (bf16[2,384,384]{2,1,0:T(8,128)(2,1)S(1)}, bf16[2,384,384]{2,1,0:T(8,128)(2,1)S(1)}, u32[]{:S(2)}, u32[]{:S(2)}) collective-permute-start(bf16[2,384,384]{2,1,0:T(8,128)(2,1)S(1)} %bitcast.233), channel_id=1, source_target_pairs={{0,4},{4,8},{8,12},{1,5},{5,9},{9,13},{2,6},{6,10},{10,14},{3,7},{... | collective-permute-start | bytes 1769480 | tf_op jit(solution)/shard_map/ppermute | solution.py:143
  17.9 3.6 %collective-permute-start.1 = (bf16[2,384,384]{2,1,0:T(8,128)(2,1)S(1)}, bf16[2,384,384]{2,1,0:T(8,128)(2,1)S(1)}, u32[]{:S(2)}, u32[]{:S(2)}) collective-permute-start(bf16[2,384,384]{2,1,0:T(8,128)(2,1)S(1)} %bitcast.234), channel_id=1, source_target_pairs={{4,0},{8,4},{12,8},{5,1},{9,5},{13,9},{6,2},{10,6},{14,10},{7,3},{... | collective-permute-start | bytes 1769480 | tf_op jit(solution)/shard_map/ppermute | solution.py:144
  21.5 0.9 %dynamic-slice_bitcast_fusion.3 = (bf16[96,1,384]{2,0,1:T(8,128)(2,1)S(1)}, bf16[96,1,384]{2,0,1:T(8,128)(2,1)S(1)}) fusion(bf16[2,384,384]{2,1,0:T(8,128)(2,1)} %constant.52.clone, s32[]{:T(128)S(6)} %add.161, s32[]{:T(128)S(6)} %select_n.28), kind=kLoop, calls=%fused_computation.104 | loop fusion | bytes 294920 | tf_op jit(solution)/shard_map/squeeze | solution.py:102
  22.5 0.9 %fusion.54 = bf16[96,1,384]{2,0,1:T(8,128)(2,1)S(1)} fusion(bf16[2,384,384]{2,1,0:T(8,128)(2,1)} %constant.52.clone, s32[]{:T(128)S(6)} %add.161, s32[]{:T(128)S(6)} %select_n.28), kind=kLoop, calls=%fused_computation.108 | loop fusion | flops 110592 | bytes 147464 | tf_op jit(solution)/shard_map/neg | solution.py:104
  23.4 0.8 %bitcast_convert_fusion = f32[6,128,128]{2,1,0:T(8,128)} fusion(bf16[1,6,128,128]{3,1,2,0:T(8,128)(2,1)S(1)} %fusion.8), kind=kLoop, calls=%fused_computation.94 | loop fusion | flops 98304 | bytes 589824 | tf_op jit(solution)/shard_map/convert_element_type | solution.py:97
  24.2 1.3 %convolution_convert_fusion.5 = bf16[2,96,2,6,128]{4,1,3,2,0:T(8,128)(2,1)} fusion(s32[6,128]{1,0:T(8,128)S(1)} %iota_add_fusion.1, bf16[1,96,2,384]{3,1,2,0:T(8,128)(2,1)S(1)} %get-tuple-element.21, bf16[1,96,2,384]{3,1,2,0:T(8,128)(2,1)S(1)} %get-tuple-element.20), kind=kOutput, calls=%fused_computation.15 | convolution fusion | flops 227672064 | bytes 887808 | tf_op jit(solution)/shard_map/oibj,gjr->oibgr/dot_general | solution.py:106
  25.6 0.8 %dynamic-slice_bitcast_fusion.2 = (bf16[2,96,384]{2,1,0:T(8,128)(2,1)}, bf16[2,96,384]{2,1,0:T(8,128)(2,1)}, bf16[2,96,384]{2,1,0:T(8,128)(2,1)}) fusion(bf16[1,2,384,384]{3,2,1,0:T(8,128)(2,1)S(1)} %copy-done.2, s32[]{:T(128)S(6)} %select_n.30, s32[]{:T(128)S(6)} %select_n.32, s32[]{:T(128)S(6)} %select_n.34), kind=kLoop, calls=%fused_computation.102 | loop fusion | bytes 884748 | tf_op jit(solution)/shard_map/dynamic_slice | solution.py:56
  26.4 0.7 constant_dynamic-slice_fusion
  27.1 1.4 %copy.25 = bf16[2,96,2,6,128]{4,3,2,1,0:T(8,128)(2,1)S(1)} copy(bf16[2,96,2,6,128]{4,1,3,2,0:T(8,128)(2,1)} %convolution_convert_fusion.5) | data formatting | bytes 1179648 | tf_op jit(solution)/shard_map/convert_element_type | solution.py:108
  28.5 1.5 %reshape.191 = bf16[192,1536]{1,0:T(8,128)(2,1)} reshape(bf16[2,96,2,6,128]{4,3,2,1,0:T(8,128)(2,1)S(1)} %copy.25) | data formatting | bytes 1179648 | tf_op jit(solution)/shard_map/reshape | solution.py:111
  30.4 1.6 %collective-permute-start.2 = (bf16[2,96,384]{2,1,0:T(8,128)(2,1)}, bf16[2,96,384]{2,1,0:T(8,128)(2,1)}, u32[]{:S(2)}, u32[]{:S(2)}) collective-permute-start(bf16[2,96,384]{2,1,0:T(8,128)(2,1)} %get-tuple-element.15), channel_id=1, source_target_pairs={{0,1},{1,2},{2,3},{3,0},{4,5},{5,6},{6,7},{7,4},{8,9},{9,10},{10,1... | collective-permute-start | bytes 442376 | tf_op jit(solution)/shard_map/ppermute | solution.py:49
  32.3 4.3 %convert_bitcast_fusion = bf16[2,6,128,4,384]{2,4,0,3,1:T(8,128)(2,1)} fusion(f32[6,128,128]{2,1,0:T(8,128)S(1)} %copy-done.5, bf16[6,128,384]{2,1,0:T(8,128)(2,1)S(1)} %copy-done.4, f32[1,2,6,128]{3,1,2,0:T(2,128)} %bitcast.46, f32[1,2,6,128]{3,1,2,0:T(2,128)} %bitcast.45, f32[1,2,6,128]{3,1,2,0:T(2,128)S(1)} %bitcast.242, ...), kind=kOutput, calls=%fused_computation.2 | convolution fusion | flops 607930368 | bytes 5726208 | tf_op jit(solution)/shard_map/cpgrj,gjk->pgrck/dot_general | solution.py:98
  36.6 8.5 %copy.35 = bf16[2,6,128,4,384]{4,3,2,1,0:T(4,128)(2,1)} copy(bf16[2,6,128,4,384]{2,4,0,3,1:T(8,128)(2,1)} %convert_bitcast_fusion) | data formatting | bytes 9437184 | tf_op jit(solution)/shard_map/convert_element_type | solution.py:100
  45.1 3.3 %copy.66 = bf16[192,8,4,384]{3,1,2,0:T(8,128)(2,1)S(1)} copy(bf16[192,8,4,384]{3,2,1,0:T(4,128)(2,1)} %bitcast.232) | data formatting | bytes 9437184
  48.3 1.9 %convolution_convert_fusion.2 = bf16[192,1536]{1,0:T(8,128)(2,1)} fusion(bf16[192,1536]{1,0:T(8,128)(2,1)S(1)} %copy-done.8, bf16[1536,1536]{1,0:T(8,128)(2,1)S(1)} %bitcast.235), kind=kOutput, calls=%fused_computation.4 | convolution fusion | flops 906264576 | bytes 5898240 | tf_op jit(solution)/shard_map/dot_general | solution.py:110
  50.3 1.7 %reshape.197 = bf16[2,96,4,384]{3,2,1,0:T(4,128)(2,1)S(1)} reshape(bf16[192,1536]{1,0:T(8,128)(2,1)} %convolution_convert_fusion.2) | data formatting | bytes 1179648 | tf_op jit(solution)/shard_map/reshape | solution.py:114
  52.0 0.8 %convolution_bitcast_fusion = f32[2,2,96,4,384]{4,2,0,3,1:T(8,128)S(1)} fusion(bf16[2,384,384,1,1]{2,1,0,4,3:T(8,128)(2,1)S(1)} %copy-done.7, bf16[2,96,4,384,1]{3,2,1,0,4:T(4,128)(2,1)S(1)} %bitcast.237), kind=kOutput, calls=%fused_computation.7 | convolution fusion | flops 452984832 | bytes 3538944 | tf_op jit(solution)/shard_map/bicj,ajk->abick/dot_general | solution.py:115
  52.9 1.2 %convert_bitcast_fusion.1 = f32[2,96,4,384]{3,1,2,0:T(8,128)S(1)} fusion(bf16[1,2,96,384]{3,2,0,1:T(8,128)(2,1)} %bitcast.10, bf16[1,2,96,384]{3,2,0,1:T(8,128)(2,1)} %bitcast.8, bf16[1,2,96,384]{3,2,0,1:T(8,128)(2,1)} %bitcast.6, bf16[1,2,96,384]{3,2,0,1:T(8,128)(2,1)S(1)} %copy-done.6), kind=kLoop, calls=%fused_computation.18 | loop fusion | flops 1179648 | bytes 1769472 | tf_op jit(solution)/shard_map/convert_element_type | solution.py:117
  55.5 16.6 %all_gather.3 = bf16[2,384,384]{2,1,0:T(8,128)(2,1)S(1)} all-gather(bf16[2,96,384]{2,1,0:T(8,128)(2,1)S(1)} %pad_maximum_fusion), channel_id=1, replica_groups=mesh['grp'=2,'frame'=4,'coil'=4] {'coil'}, dimensions={1}, use_global_device_ids=true | all-gather | bytes 737280 | tf_op jit(solution)/shard_map/all_gather | solution.py:184
  72.0 1.2 %fusion.4 = f32[1,2,384,384]{3,2,1,0:T(8,128)} fusion(f32[1,2,384,384]{3,2,1,0:T(8,128)S(1)} %subtract_bitcast_fusion, bf16[1,2,384,384]{3,2,1,0:T(8,128)(2,1)S(1)} %copy-done, bf16[2,384,384]{2,1,0:T(8,128)(2,1)S(1)} %all_gather.3), kind=kLoop, calls=%fused_computation.17 | loop fusion | flops 1474560 | bytes 3538944 | tf_op jit(solution)/shard_map/sub | solution.py:185
  (58 shorter events, 4.4 us)
Async XLA Ops:
  0.0 1.2 %copy-start.2 = (bf16[1,2,384,384]{3,2,1,0:T(8,128)(2,1)S(1)}, bf16[1,2,384,384]{3,2,1,0:T(8,128)(2,1)}, u32[]{:S(2)}) copy-start(bf16[1,2,384,384]{3,2,1,0:T(8,128)(2,1)} %param.10) | copy-start | bytes 1769476
  1.3 1.1 %copy-start.1 = (bf16[2,384,384,1]{2,1,0,3:T(8,128)(2,1)S(1)}, bf16[2,384,384,1]{2,1,0,3:T(8,128)(2,1)}, u32[]{:S(2)}) copy-start(bf16[2,384,384,1]{2,1,0,3:T(8,128)(2,1)} %constant.59) | copy-start | bytes 1769476
  4.1 1.6 %copy-start.14 = (s32[1,6]{1,0:T(1,128)S(1)}, s32[1,6]{1,0:T(1,128)}, u32[]{:S(2)}) copy-start(s32[1,6]{1,0:T(1,128)} %param.13) | copy-start | bytes 76
  4.1 1.6 %copy-start.9 = (bf16[16,128,128]{2,1,0:T(8,128)(2,1)S(1)}, bf16[16,128,128]{2,1,0:T(8,128)(2,1)}, u32[]{:S(2)}) copy-start(bf16[16,128,128]{2,1,0:T(8,128)(2,1)} %param.15) | copy-start | bytes 1572868
  4.1 1.6 %copy-start.13 = (s32[1,6]{1,0:T(1,128)S(1)}, s32[1,6]{1,0:T(1,128)}, u32[]{:S(2)}) copy-start(s32[1,6]{1,0:T(1,128)} %param.12) | copy-start | bytes 76
  6.5 1.9 %copy-start.15 = (s32[1,6]{1,0:T(1,128)S(1)}, s32[1,6]{1,0:T(1,128)}, u32[]{:S(2)}) copy-start(s32[1,6]{1,0:T(1,128)} %param.14) | copy-start | bytes 76
  6.9 2.0 %copy-start.10 = (bf16[1,384,384]{1,2,0:T(8,128)(2,1)S(1)}, bf16[1,384,384]{1,2,0:T(8,128)(2,1)}, u32[]{:S(2)}) copy-start(bf16[1,384,384]{1,2,0:T(8,128)(2,1)} %fusion.46) | copy-start | bytes 884740
  6.9 2.0 %copy-start.11 = (bf16[1,384,384]{1,2,0:T(8,128)(2,1)S(1)}, bf16[1,384,384]{1,2,0:T(8,128)(2,1)}, u32[]{:S(2)}) copy-start(bf16[1,384,384]{1,2,0:T(8,128)(2,1)} %fusion.47) | copy-start | bytes 884740
  8.9 0.9 %copy-start.3 = (bf16[6,128,384]{2,1,0:T(8,128)(2,1)}, bf16[6,128,384]{2,1,0:T(8,128)(2,1)S(1)}, u32[]{:S(2)}) copy-start(bf16[6,128,384]{2,1,0:T(8,128)(2,1)S(1)} %convolution_convert_fusion.4) | copy-start | bytes 1769476
  8.9 0.9 %copy-start.12 = (f32[1,1,2,6,128]{4,2,3,1,0:T(2,128)S(1)}, f32[1,1,2,6,128]{4,2,3,1,0:T(2,128)}, u32[]{:S(2)}) copy-start(f32[1,1,2,6,128]{4,2,3,1,0:T(2,128)} %param.11) | copy-start | bytes 18436
  9.0 7.0 %copy-start = (bf16[1,2,384,384]{3,2,1,0:T(8,128)(2,1)S(1)}, bf16[1,2,384,384]{3,2,1,0:T(8,128)(2,1)}, u32[]{:S(2)}) copy-start(bf16[1,2,384,384]{3,2,1,0:T(8,128)(2,1)} %param.9) | copy-start | bytes 1769476
  10.5 19.5 %collective-permute-start.5 = (f32[2,6,128]{2,0,1:T(2,128)}, f32[2,6,128]{2,0,1:T(2,128)S(1)}, u32[]{:S(2)}, u32[]{:S(2)}) collective-permute-start(f32[2,6,128]{2,0,1:T(2,128)} %bitcast_subtract_fusion), channel_id=1, source_target_pairs={{0,1},{1,2},{2,3},{3,0},{4,5},{5,6},{6,7},{7,4},{8,9},{9,10},{10,1... | collective-permute-start | bytes 18440 | tf_op jit(solution)/shard_map/ppermute | solution.py:49
  12.0 18.3 %collective-permute-start.6 = (f32[2,6,128]{2,0,1:T(2,128)}, f32[2,6,128]{2,0,1:T(2,128)}, u32[]{:S(2)}, u32[]{:S(2)}) collective-permute-start(f32[2,6,128]{2,0,1:T(2,128)} %bitcast_subtract_fusion), channel_id=1, source_target_pairs={{0,2},{1,3},{2,0},{3,1},{4,6},{5,7},{6,4},{7,5},{8,10},{9,11},{10,... | collective-permute-start | bytes 18440 | tf_op jit(solution)/shard_map/ppermute | solution.py:49
  14.6 17.3 %collective-permute-start.7 = (f32[2,6,128]{2,0,1:T(2,128)}, f32[2,6,128]{2,0,1:T(2,128)}, u32[]{:S(2)}, u32[]{:S(2)}) collective-permute-start(f32[2,6,128]{2,0,1:T(2,128)} %bitcast_subtract_fusion), channel_id=1, source_target_pairs={{0,3},{1,0},{2,1},{3,2},{4,7},{5,4},{6,5},{7,6},{8,11},{9,8},{10,9... | collective-permute-start | bytes 18440 | tf_op jit(solution)/shard_map/ppermute | solution.py:49
  16.0 38.4 %collective-permute-start = (bf16[2,384,384]{2,1,0:T(8,128)(2,1)S(1)}, bf16[2,384,384]{2,1,0:T(8,128)(2,1)S(1)}, u32[]{:S(2)}, u32[]{:S(2)}) collective-permute-start(bf16[2,384,384]{2,1,0:T(8,128)(2,1)S(1)} %bitcast.233), channel_id=1, source_target_pairs={{0,4},{4,8},{8,12},{1,5},{5,9},{9,13},{2,6},{6,10},{10,14},{3,7},{... | collective-permute-start | bytes 1769480 | tf_op jit(solution)/shard_map/ppermute | solution.py:143
  17.9 36.5 %collective-permute-start.1 = (bf16[2,384,384]{2,1,0:T(8,128)(2,1)S(1)}, bf16[2,384,384]{2,1,0:T(8,128)(2,1)S(1)}, u32[]{:S(2)}, u32[]{:S(2)}) collective-permute-start(bf16[2,384,384]{2,1,0:T(8,128)(2,1)S(1)} %bitcast.234), channel_id=1, source_target_pairs={{4,0},{8,4},{12,8},{5,1},{9,5},{13,9},{6,2},{10,6},{14,10},{7,3},{... | collective-permute-start | bytes 1769480 | tf_op jit(solution)/shard_map/ppermute | solution.py:144
  27.1 5.2 %copy-start.4 = (bf16[6,128,384]{2,1,0:T(8,128)(2,1)S(1)}, bf16[6,128,384]{2,1,0:T(8,128)(2,1)}, u32[]{:S(2)}) copy-start(bf16[6,128,384]{2,1,0:T(8,128)(2,1)} %copy-done.3) | copy-start | bytes 1769476
  27.1 5.2 %copy-start.5 = (f32[6,128,128]{2,1,0:T(8,128)S(1)}, f32[6,128,128]{2,1,0:T(8,128)}, u32[]{:S(2)}) copy-start(f32[6,128,128]{2,1,0:T(8,128)} %bitcast_convert_fusion) | copy-start | bytes 1179652
  29.9 22.8 %collective-permute-start.4 = (bf16[2,96,384]{2,1,0:T(8,128)(2,1)}, bf16[2,96,384]{2,1,0:T(8,128)(2,1)}, u32[]{:S(2)}, u32[]{:S(2)}) collective-permute-start(bf16[2,96,384]{2,1,0:T(8,128)(2,1)} %get-tuple-element.17), channel_id=1, source_target_pairs={{0,3},{1,0},{2,1},{3,2},{4,7},{5,4},{6,5},{7,6},{8,11},{9,8},{10,9... | collective-permute-start | bytes 442376 | tf_op jit(solution)/shard_map/ppermute | solution.py:49
  30.4 22.4 %collective-permute-start.2 = (bf16[2,96,384]{2,1,0:T(8,128)(2,1)}, bf16[2,96,384]{2,1,0:T(8,128)(2,1)}, u32[]{:S(2)}, u32[]{:S(2)}) collective-permute-start(bf16[2,96,384]{2,1,0:T(8,128)(2,1)} %get-tuple-element.15), channel_id=1, source_target_pairs={{0,1},{1,2},{2,3},{3,0},{4,5},{5,6},{6,7},{7,4},{8,9},{9,10},{10,1... | collective-permute-start | bytes 442376 | tf_op jit(solution)/shard_map/ppermute | solution.py:49
  32.0 20.8 %collective-permute-start.3 = (bf16[2,96,384]{2,1,0:T(8,128)(2,1)}, bf16[2,96,384]{2,1,0:T(8,128)(2,1)}, u32[]{:S(2)}, u32[]{:S(2)}) collective-permute-start(bf16[2,96,384]{2,1,0:T(8,128)(2,1)} %get-tuple-element.16), channel_id=1, source_target_pairs={{0,2},{1,3},{2,0},{3,1},{4,6},{5,7},{6,4},{7,5},{8,10},{9,11},{10,... | collective-permute-start | bytes 442376 | tf_op jit(solution)/shard_map/ppermute | solution.py:49
  45.1 3.3 %copy-start.8 = (bf16[192,1536]{1,0:T(8,128)(2,1)S(1)}, bf16[192,1536]{1,0:T(8,128)(2,1)}, u32[]{:S(2)}) copy-start(bf16[192,1536]{1,0:T(8,128)(2,1)} %reshape.191) | copy-start | bytes 1769476
  50.3 1.7 %copy-start.7 = (bf16[2,384,384,1,1]{2,1,0,4,3:T(8,128)(2,1)S(1)}, bf16[2,384,384,1,1]{2,1,0,4,3:T(8,128)(2,1)}, u32[]{:S(2)}) copy-start(bf16[2,384,384,1,1]{2,1,0,4,3:T(8,128)(2,1)} %constant.60) | copy-start | bytes 1769476
  51.9 0.9 %copy-start.6 = (bf16[1,2,96,384]{3,2,0,1:T(8,128)(2,1)S(1)}, bf16[1,2,96,384]{3,2,0,1:T(8,128)(2,1)}, u32[]{:S(2)}) copy-start(bf16[1,2,96,384]{3,2,0,1:T(8,128)(2,1)} %constant_dynamic-slice_fusion) | copy-start | bytes 442372

commit v2 on v0

--- a/solution.py
+++ b/solution.py
@@ -72,7 +72,7 @@
     return picked.astype(kernels.dtype).reshape((angle_ids.shape[0],) + kernels.shape[1:])
 
 
-def forward_residual(transform, frame_image, coil_map, measured, row_placed, col_placed):
+def forward_residual(transform, block, frame_image, coil_map, measured, row_placed, col_placed):
     map_planes = coil_map.astype(jnp.float32)
     image_planes = frame_image.astype(jnp.float32)
     coil_image = jnp.stack(
@@ -85,14 +85,16 @@
         "bij,ajk->abik", coil_image, transform, preferred_element_type=jnp.float32
     )
     half_done = combine_parts(products, 1.0).astype(jnp.bfloat16)
-    products = jnp.einsum("aij,bjk->abik", transform, half_done, preferred_element_type=jnp.float32)
-    kspace = combine_parts(products, 1.0).astype(jnp.bfloat16)
+    extent = transform.shape[-1]
+    kspace = jnp.dot(
+        block, half_done.reshape(2 * extent, extent), preferred_element_type=jnp.float32
+    ).astype(jnp.bfloat16).reshape(2, extent, extent)
     contracted = jnp.einsum("pik,gjk->pgij", kspace, col_placed, preferred_element_type=jnp.float32)
-    predicted = jnp.sum(contracted * row_placed.astype(jnp.float32)[None], axis=2)
+    predicted = jnp.sum(contracted * row_placed[None], axis=2)
     return predicted - measured
 
 
-def backward_rows(transform, residuals, map_rows, row_select, row_w, col_placed, coil_index):
+def backward_rows(transform, block_t, residuals, map_rows, row_select, row_w, col_placed, coil_index):
     rows = map_rows.shape[2]
     spread = (row_w.astype(jnp.float32)[None, None] * residuals[:, :, :, None, :]).astype(jnp.bfloat16)
     placed = jnp.einsum(
@@ -104,11 +106,13 @@
     ).astype(jnp.bfloat16)
     products = jnp.einsum("aigr,cbgrk->abcik", table_at, placed, preferred_element_type=jnp.float32)
     half_back = combine_parts(products, -1.0).astype(jnp.bfloat16)
-    products = jnp.einsum("bcij,ajk->abcik", half_back, transform, preferred_element_type=jnp.float32)
-    coil_back = combine_parts(products, -1.0)
+    coil_count, extent = half_back.shape[1], half_back.shape[-1]
+    side_by_side = jnp.transpose(half_back, (1, 2, 0, 3)).reshape(coil_count * rows, 2 * extent)
+    coil_back = jnp.dot(side_by_side, block_t.T, preferred_element_type=jnp.float32)
+    coil_back = coil_back.reshape(coil_count, rows, 2, extent)
     maps = map_rows.astype(jnp.float32)
-    real_part = jnp.sum(maps[:, 0] * coil_back[0] + maps[:, 1] * coil_back[1], axis=0)
-    imaginary = jnp.sum(maps[:, 0] * coil_back[1] - maps[:, 1] * coil_back[0], axis=0)
+    real_part = jnp.sum(maps[:, 0] * coil_back[:, :, 0] + maps[:, 1] * coil_back[:, :, 1], axis=0)
+    imaginary = jnp.sum(maps[:, 0] * coil_back[:, :, 1] - maps[:, 1] * coil_back[:, :, 0], axis=0)
     return jnp.stack([real_part, imaginary])
 
 
@@ -162,15 +166,22 @@
     col_select = selector(band_col[0], extent, patch_side)
     exact = dict(preferred_element_type=jnp.float32)
     col_placed = jnp.einsum("gjq,gkq->gjk", col_w, col_select, **exact).astype(jnp.bfloat16)
-    row_placed = jnp.einsum("grj,gir->gij", row_w, row_select, **exact).astype(jnp.bfloat16)
+    row_placed = jnp.einsum("grj,gir->gij", row_w, row_select, **exact)
+    cos_t, sin_t = lax.optimization_barrier(transform)
+    block = jnp.concatenate(
+        [jnp.concatenate([cos_t, sin_t], axis=1), jnp.concatenate([-sin_t, cos_t], axis=1)]
+    )
+    block_t = jnp.concatenate(
+        [jnp.concatenate([cos_t, -sin_t], axis=1), jnp.concatenate([sin_t, cos_t], axis=1)]
+    )
     residual = forward_residual(
-        transform, images[0], coil_maps[0], kspace_data[0, 0], row_placed, col_placed
+        transform, block, images[0], coil_maps[0], kspace_data[0, 0], row_placed, col_placed
     )
     residuals = jnp.stack(
         [residual] + [rotated(residual, coil_count, shift) for shift in range(1, coil_count)]
     )
     grad_rows = backward_rows(
-        transform, residuals, map_rows, row_select, row_w, col_placed, coil_index
+        transform, block_t, residuals, map_rows, row_select, row_w, col_placed, coil_index
     )
     tv_grad, grad_rows = lax.optimization_barrier((tv_grad, grad_rows.astype(jnp.bfloat16)))
     data_grad = lax.all_gather(grad_rows, "coil", axis=1, tiled=True).astype(jnp.float32)[None]

time: 59.8 us -> 59.9 us (level)
  waiting for transfers between devices: 5.49 us -> 2.61 us
  other arithmetic: 9.84 us -> 11.4 us
  local copies, waits for them, and re-layouts: 3.69 us -> 4.6 us
    ppermute x6, waiting for transfers between devices: 5.48 us -> 2.6 us  [rotated(): lax.ppermute(block, 'coil', [(i, (i + shift) % coil_count) for i in range...]
    convert_element_type x1 -> x0, local copies, waits for them, and re-layouts: 1.38 us -> none  [forward_residual(): row_placed.astype(jnp.float32)[None]]
    unnamed x26 -> x22, local copies, waits for them, and re-layouts: 1.51 us -> 2.74 us
    dot_general x3, matrix products: 1.91 us -> 3.12 us  [the longest x1 1.92 us: backward_rows(): jnp.dot(side_by_side, block_t.T, preferred_element_type=jnp.float32)]
    concatenate x0 -> x1, other arithmetic: none -> 1.11 us  [body(): jnp.concatenate([jnp.concatenate([cos_t, -sin_t], axis=1), jnp.concatenat...]
    dot_general x1, matrix products: 2.06 us -> 1.1 us  [backward_rows(): jnp.einsum('aij,gjr->aigr', row_table, row_select, preferred_element_type...]
    sub x3 -> x2, other arithmetic: 2.14 us -> 1.37 us  [combine_parts(): imaginary = products[0, 1] - direction * products[1, 0]]
    another operation x1, other arithmetic: 0.01 us -> 0.74 us  [body(): jnp.stack([residual] + [rotated(residual, coil_count, shift) for shift in...]
  transfers between devices with their start and end apart: 8 -> 8, of which waited for: 1 -> 1; matrix products, arithmetic and copies ran while one was open for 22% -> 27% of each run, Pallas kernels for 0% -> 0%
where the time goes in v2:
time: 59.9 us; the launch traced here: 59.2 us
  blocking collectives  16.7 us (28%)
  starting transfers between devices  11.9 us (20%)
  matrix products  11.8 us (20%)
  other arithmetic  11.4 us (19%)
  local copies, waits for them, and re-layouts  4.6 us (8%)
  waiting for transfers between devices  2.61 us (4%)
    all_gather x1, blocking collectives, body(): lax.all_gather(grad_rows, 'coil', axis=1, tiled=True).astype(jnp.float32)  16.7 us
    ppermute x6, starting transfers between devices, rotated(): lax.ppermute(block, 'coil', [(i, (i + shift) % coil_count) for i in range...  9.25 us
    dot_general x1, matrix products, backward_rows(): jnp.einsum('aigr,cbgrk->abcik', table_at, placed, preferred_element_type=...  4.72 us
    unnamed x22, local copies, waits for them, and re-layouts  2.74 us
    ppermute x6, waiting for transfers between devices, rotated(): lax.ppermute(block, 'coil', [(i, (i + shift) % coil_count) for i in range...  2.6 us
    dot_general x1, matrix products, backward_rows(): jnp.dot(side_by_side, block_t.T, preferred_element_type=jnp.float32)  1.92 us
    sub x2, other arithmetic, combine_parts(): imaginary = products[0, 1] - direction * products[1, 0]  1.37 us
    add x2, other arithmetic, combine_parts(): real_part = products[0, 0] + direction * products[1, 1]  1.37 us
  transfers between devices with their start and end apart: 8, of which 1 were waited for; matrix products, arithmetic and copies ran while one was open for 27% of the time, Pallas kernels for 0%

profile of v2, /device:TPU:0, one launch (start us, length us, event | category | flops | bytes accessed | tf_op | source)
XLA Modules:
  0.0 59.2 jit_solution(3255010522795613015)
XLA Ops:
  0.0 1.2 %bitcast_convert_fusion.1 = f32[2,384,384]{2,1,0:T(8,128)S(1)} fusion(bf16[1,2,384,384]{3,2,1,0:T(8,128)(2,1)} %param.9), kind=kLoop, calls=%fused_computation.120 | loop fusion | flops 294912 | bytes 1769472 | tf_op jit(solution)/shard_map/convert_element_type | solution.py:131
  1.5 0.9 %copy-done.3 = bf16[2,384,384,1]{2,1,0,3:T(8,128)(2,1)S(1)} copy-done((bf16[2,384,384,1]{2,1,0,3:T(8,128)(2,1)S(1)}, bf16[2,384,384,1]{2,1,0,3:T(8,128)(2,1)}, u32[]{:S(2)}) %copy-start.3) | copy-done | bytes 589848
  2.4 0.8 %convolution_bitcast_fusion = f32[2,2,384,384]{3,2,0,1:T(8,128)S(1)} fusion(bf16[2,384,384,1]{2,1,0,3:T(8,128)(2,1)S(1)} %copy-done.3, bf16[1,384,384]{2,1,0:T(8,128)(2,1)S(1)} %get-tuple-element.12, bf16[1,384,384]{2,1,0:T(8,128)(2,1)S(1)} %get-tuple-element.11), kind=kOutput, calls=%fused_computation.10 | convolution fusion | flops 454164480 | bytes 3538944 | tf_op jit(solution)/shard_map/bij,ajk->abik/dot_general | solution.py:84
  3.3 0.9 %copy-done.2 = bf16[2,384,384]{2,1,0:T(8,128)(2,1)S(1)} copy-done((bf16[2,384,384]{2,1,0:T(8,128)(2,1)S(1)}, bf16[2,384,384]{2,1,0:T(8,128)(2,1)}, u32[]{:S(2)}) %copy-start.2) | copy-done | bytes 589848
  4.4 0.5 copy-done.9
  6.3 0.4 fusion.20
  7.1 0.8 %convolution_convert_fusion.2 = bf16[768,384]{1,0:T(8,128)(2,1)S(1)} fusion(bf16[768,384]{1,0:T(8,128)(2,1)S(1)} %bitcast.222, bf16[384,384]{1,0:T(8,128)(2,1)S(1)} %get-tuple-element.14, bf16[384,384]{1,0:T(8,128)(2,1)S(1)} %fusion.72, bf16[384,384]{1,0:T(8,128)(2,1)S(1)} %get-tuple-element.13), kind=kOutput, calls=%fused_computation.17 | convolution fusion | flops 457998336 | bytes 2064384 | tf_op jit(solution)/shard_map/dot_general | solution.py:89
  7.9 0.9 %fusion.5 = f32[2,6,128]{2,0,1:T(2,128)S(1)} fusion(bf16[2,384,384,1]{2,1,0,3:T(8,128)(2,1)S(1)} %bitcast.231, f32[6,384,128]{1,2,0:T(8,128)S(1)} %fusion.20, bf16[6,128,384]{2,1,0:T(8,128)(2,1)S(1)} %convolution_convert_fusion.3), kind=kOutput, calls=%fused_computation.8 | convolution fusion | flops 454162944 | bytes 2365440 | tf_op jit(solution)/shard_map/pik,gjk->pgij/dot_general | solution.py:92
  8.8 0.6 %bitcast_subtract_fusion = f32[2,6,128]{2,0,1:T(2,128)} fusion(f32[2,6,128]{2,0,1:T(2,128)S(1)} %fusion.5, f32[1,1,2,6,128]{4,2,3,1,0:T(2,128)S(1)} %copy-done.7), kind=kLoop, calls=%fused_computation.109 | loop fusion | flops 1536 | bytes 18432 | tf_op jit(solution)/shard_map/sub | solution.py:94
  9.4 3.1 %collective-permute-start.5 = (f32[2,6,128]{2,0,1:T(2,128)}, f32[2,6,128]{2,0,1:T(2,128)}, u32[]{:S(2)}, u32[]{:S(2)}) collective-permute-start(f32[2,6,128]{2,0,1:T(2,128)} %bitcast_subtract_fusion), channel_id=1, source_target_pairs={{0,1},{1,2},{2,3},{3,0},{4,5},{5,6},{6,7},{7,4},{8,9},{9,10},{10,1... | collective-permute-start | bytes 18440 | tf_op jit(solution)/shard_map/ppermute | solution.py:49
  12.4 2.6 %collective-permute-start.6 = (f32[2,6,128]{2,0,1:T(2,128)}, f32[2,6,128]{2,0,1:T(2,128)}, u32[]{:S(2)}, u32[]{:S(2)}) collective-permute-start(f32[2,6,128]{2,0,1:T(2,128)} %bitcast_subtract_fusion), channel_id=1, source_target_pairs={{0,2},{1,3},{2,0},{3,1},{4,6},{5,7},{6,4},{7,5},{8,10},{9,11},{10,... | collective-permute-start | bytes 18440 | tf_op jit(solution)/shard_map/ppermute | solution.py:49
  15.0 1.3 %collective-permute-start.7 = (f32[2,6,128]{2,0,1:T(2,128)}, f32[2,6,128]{2,0,1:T(2,128)}, u32[]{:S(2)}, u32[]{:S(2)}) collective-permute-start(f32[2,6,128]{2,0,1:T(2,128)} %bitcast_subtract_fusion), channel_id=1, source_target_pairs={{0,3},{1,0},{2,1},{3,2},{4,7},{5,4},{6,5},{7,6},{8,11},{9,8},{10,9... | collective-permute-start | bytes 18440 | tf_op jit(solution)/shard_map/ppermute | solution.py:49
  16.4 1.3 %collective-permute-start = (bf16[2,384,384]{2,1,0:T(8,128)(2,1)S(1)}, bf16[2,384,384]{2,1,0:T(8,128)(2,1)S(1)}, u32[]{:S(2)}, u32[]{:S(2)}) collective-permute-start(bf16[2,384,384]{2,1,0:T(8,128)(2,1)S(1)} %bitcast.218), channel_id=1, source_target_pairs={{0,4},{4,8},{8,12},{1,5},{5,9},{9,13},{2,6},{6,10},{10,14},{3,7},{... | collective-permute-start | bytes 1769480 | tf_op jit(solution)/shard_map/ppermute | solution.py:139
  17.7 1.3 %collective-permute-start.1 = (bf16[2,384,384]{2,1,0:T(8,128)(2,1)S(1)}, bf16[2,384,384]{2,1,0:T(8,128)(2,1)S(1)}, u32[]{:S(2)}, u32[]{:S(2)}) collective-permute-start(bf16[2,384,384]{2,1,0:T(8,128)(2,1)S(1)} %bitcast.219), channel_id=1, source_target_pairs={{4,0},{8,4},{12,8},{5,1},{9,5},{13,9},{6,2},{10,6},{14,10},{7,3},{... | collective-permute-start | bytes 1769480 | tf_op jit(solution)/shard_map/ppermute | solution.py:140
  19.0 0.8 %bitcast_convert_fusion = f32[6,128,128]{2,1,0:T(8,128)} fusion(bf16[1,6,128,128]{3,1,2,0:T(8,128)(2,1)S(1)} %fusion.26), kind=kLoop, calls=%fused_computation.96 | loop fusion | flops 98304 | bytes 589824 | tf_op jit(solution)/shard_map/convert_element_type | solution.py:99
  19.8 1.1 %fusion.15 = bf16[768,768]{1,0:T(8,128)(2,1)} fusion(bf16[384,384]{1,0:T(8,128)(2,1)S(1)} %get-tuple-element.14, bf16[384,384]{1,0:T(8,128)(2,1)S(1)} %get-tuple-element.13, bf16[384,384]{1,0:T(8,128)(2,1)S(1)} %fusion.72), kind=kLoop, calls=%fused_computation.21 | loop fusion | flops 4718592 | bytes 2064384 | tf_op jit(solution)/shard_map/concatenate | solution.py:174
  20.9 1.1 %fusion.22 = bf16[2,96,6,128,1,1]{3,1,2,0,5,4:T(8,128)(2,1)} fusion(s32[6,128]{1,0:T(8,128)S(1)} %iota_add_fusion, bf16[2,384,384]{2,1,0:T(8,128)(2,1)S(1)} %copy-done.2, s32[]{:T(128)S(6)} %select_n.28), kind=kOutput, calls=%fused_computation.33 | convolution fusion | flops 113688576 | bytes 446468 | tf_op jit(solution)/shard_map/aij,gjr->aigr/dot_general | solution.py:104
  22.0 0.8 %dynamic-slice_bitcast_fusion.2 = (bf16[2,96,384]{2,1,0:T(8,128)(2,1)}, bf16[2,96,384]{2,1,0:T(8,128)(2,1)}, bf16[2,96,384]{2,1,0:T(8,128)(2,1)}) fusion(bf16[1,2,384,384]{3,2,1,0:T(8,128)(2,1)S(1)} %copy-done.1, s32[]{:T(128)S(6)} %select_n.30, s32[]{:T(128)S(6)} %select_n.32, s32[]{:T(128)S(6)} %select_n.34), kind=kLoop, calls=%fused_computation.104 | loop fusion | bytes 884748 | tf_op jit(solution)/shard_map/dynamic_slice | solution.py:56
  22.9 0.5 collective-permute-start.4
  23.4 1.6 %collective-permute-start.2 = (bf16[2,96,384]{2,1,0:T(8,128)(2,1)}, bf16[2,96,384]{2,1,0:T(8,128)(2,1)}, u32[]{:S(2)}, u32[]{:S(2)}) collective-permute-start(bf16[2,96,384]{2,1,0:T(8,128)(2,1)} %get-tuple-element.15), channel_id=1, source_target_pairs={{0,1},{1,2},{2,3},{3,0},{4,5},{5,6},{6,7},{7,4},{8,9},{9,10},{10,1... | collective-permute-start | bytes 442376 | tf_op jit(solution)/shard_map/ppermute | solution.py:49
  25.1 0.7 %pad_maximum_fusion.7 = f32[4,2,6,128]{3,1,2,0:T(2,128)S(1)} fusion(f32[1,2,6,128]{3,1,2,0:T(2,128)} %bitcast.38, f32[1,2,6,128]{3,1,2,0:T(2,128)} %bitcast.37, f32[1,2,6,128]{3,1,2,0:T(2,128)} %bitcast.36, f32[1,2,6,128]{3,1,2,0:T(2,128)S(1)} %bitcast_subtract_fusion.1), kind=kLoop, calls=%fused_computation.108 | loop fusion | flops 18432 | bytes 49152 | tf_op jit(solution)/shard_map/stack | solution.py:180
  25.9 4.7 %fusion.6 = f32[2,2,4,96,384]{4,3,0,1,2:T(8,128)} fusion(bf16[2,96,6,128,1,1]{3,1,2,0,5,4:T(8,128)(2,1)} %fusion.22, f32[4,2,6,128]{3,2,1,0:T(8,128)S(1)} %copy.23, f32[6,128,128]{2,1,0:T(8,128)S(1)} %copy-done.6, bf16[6,128,384]{2,1,0:T(8,128)(2,1)S(1)} %convolution_convert_fusion.3), kind=kOutput, calls=%fused_computation.9 | convolution fusion | flops 1513881600 | bytes 3661824 | tf_op jit(solution)/shard_map/aigr,cbgrk->abcik/dot_general | solution.py:107
  30.6 1.3 %fusion.59 = bf16[1,4,96,384]{3,2,1,0:T(8,128)(2,1)S(1)} fusion(f32[2,2,4,96,384]{4,3,0,1,2:T(8,128)} %fusion.6), kind=kLoop, calls=%fused_computation.91 | loop fusion | flops 442368 | bytes 1474560 | tf_op jit(solution)/shard_map/add | solution.py:43
  31.9 1.3 %fusion.60 = bf16[1,4,96,384]{3,2,1,0:T(8,128)(2,1)S(1)} fusion(f32[2,2,4,96,384]{4,3,0,1,2:T(8,128)} %fusion.6), kind=kLoop, calls=%fused_computation.92 | loop fusion | flops 442368 | bytes 1474560 | tf_op jit(solution)/shard_map/sub | solution.py:44
  33.3 0.6 %copy.27 = bf16[4,96,2,384]{3,2,1,0:T(2,128)(2,1)S(1)} copy(bf16[4,96,2,384]{3,1,0,2:T(8,128)(2,1)S(1)} %maximum_bitcast_fusion.2) | data formatting | bytes 1179648 | tf_op jit(solution)/shard_map/transpose | solution.py:110
  34.3 1.9 %fusion.48 = f32[4,96,2,384]{3,1,2,0:T(8,128)S(1)} fusion(bf16[2,384,768,1]{2,1,0,3:T(8,128)(2,1)} %bitcast.221, bf16[4,96,768,1]{2,1,0,3:T(8,128)(2,1)S(1)} %reshape.203), kind=kOutput, calls=%fused_computation.76 | convolution fusion | flops 452984832 | bytes 2949120 | tf_op jit(solution)/shard_map/dot_general | solution.py:111
  36.3 2.6 %collective-permute-done.3 = bf16[2,96,384]{2,1,0:T(8,128)(2,1)} collective-permute-done((bf16[2,96,384]{2,1,0:T(8,128)(2,1)}, bf16[2,96,384]{2,1,0:T(8,128)(2,1)}, u32[]{:S(2)}, u32[]{:S(2)}) %collective-permute-start.3) | collective-permute-done | bytes 147488 | tf_op jit(solution)/shard_map/ppermute | solution.py:49
  38.9 1.2 %maximum_convert_fusion = f32[4,2,96,384]{3,2,0,1:T(8,128)S(1)} fusion(bf16[1,2,96,384]{3,2,0,1:T(8,128)(2,1)} %bitcast.10, bf16[1,2,96,384]{3,2,0,1:T(8,128)(2,1)} %bitcast.8, bf16[1,2,96,384]{3,2,0,1:T(8,128)(2,1)} %bitcast.6, bf16[1,2,96,384]{3,2,0,1:T(8,128)(2,1)S(1)} %constant_dynamic-slice_fusion), kind=kLoop, calls=%fused_computation.68 | loop fusion | flops 1179648 | bytes 1769472 | tf_op jit(solution)/shard_map/convert_element_type | solution.py:113
  40.5 0.4 fusion.38
  40.9 0.5 subtract_bitcast_fusion
  41.3 16.7 %all_gather.3 = bf16[2,384,384]{2,1,0:T(8,128)(2,1)S(1)} all-gather(bf16[2,96,384]{2,1,0:T(8,128)(2,1)S(1)} %pad_maximum_fusion.6), channel_id=1, replica_groups=mesh['grp'=2,'frame'=4,'coil'=4] {'coil'}, dimensions={1}, use_global_device_ids=true | all-gather | bytes 737280 | tf_op jit(solution)/shard_map/all_gather | solution.py:187
  58.0 1.2 %fusion.18 = f32[1,2,384,384]{3,2,1,0:T(8,128)} fusion(f32[1,2,384,384]{3,2,1,0:T(8,128)S(1)} %subtract_bitcast_fusion, bf16[1,2,384,384]{3,2,1,0:T(8,128)(2,1)S(1)} %copy-done, bf16[2,384,384]{2,1,0:T(8,128)(2,1)S(1)} %all_gather.3), kind=kLoop, calls=%fused_computation.25 | loop fusion | flops 1474560 | bytes 3538944 | tf_op jit(solution)/shard_map/sub | solution.py:188
  (47 shorter events, 3.3 us)
Async XLA Ops:
  0.0 1.2 %copy-start.1 = (bf16[1,2,384,384]{3,2,1,0:T(8,128)(2,1)S(1)}, bf16[1,2,384,384]{3,2,1,0:T(8,128)(2,1)}, u32[]{:S(2)}) copy-start(bf16[1,2,384,384]{3,2,1,0:T(8,128)(2,1)} %param.10) | copy-start | bytes 1769476
  1.3 1.1 %copy-start.3 = (bf16[2,384,384,1]{2,1,0,3:T(8,128)(2,1)S(1)}, bf16[2,384,384,1]{2,1,0,3:T(8,128)(2,1)}, u32[]{:S(2)}) copy-start(bf16[2,384,384,1]{2,1,0,3:T(8,128)(2,1)} %constant.59) | copy-start | bytes 1769476
  3.2 1.1 %copy-start.2 = (bf16[2,384,384]{2,1,0:T(8,128)(2,1)S(1)}, bf16[2,384,384]{2,1,0:T(8,128)(2,1)}, u32[]{:S(2)}) copy-start(bf16[2,384,384]{2,1,0:T(8,128)(2,1)} %constant.52.clone) | copy-start | bytes 1769476
  4.2 0.7 %copy-start.9 = (s32[1,6]{1,0:T(1,128)S(1)}, s32[1,6]{1,0:T(1,128)}, u32[]{:S(2)}) copy-start(s32[1,6]{1,0:T(1,128)} %param.13) | copy-start | bytes 76
  4.2 1.1 %copy-start.4 = (bf16[16,128,128]{2,1,0:T(8,128)(2,1)S(1)}, bf16[16,128,128]{2,1,0:T(8,128)(2,1)}, u32[]{:S(2)}) copy-start(bf16[16,128,128]{2,1,0:T(8,128)(2,1)} %param.15) | copy-start | bytes 1572868
  4.2 1.1 %copy-start.8 = (s32[1,6]{1,0:T(1,128)S(1)}, s32[1,6]{1,0:T(1,128)}, u32[]{:S(2)}) copy-start(s32[1,6]{1,0:T(1,128)} %param.12) | copy-start | bytes 76
  4.2 1.5 %copy-start.5 = (bf16[16,128,128]{2,1,0:T(8,128)(2,1)S(1)}, bf16[16,128,128]{2,1,0:T(8,128)(2,1)}, u32[]{:S(2)}) copy-start(bf16[16,128,128]{2,1,0:T(8,128)(2,1)} %param.16) | copy-start | bytes 1572868
  4.3 1.8 %copy-start.10 = (s32[1,6]{1,0:T(1,128)S(1)}, s32[1,6]{1,0:T(1,128)}, u32[]{:S(2)}) copy-start(s32[1,6]{1,0:T(1,128)} %param.14) | copy-start | bytes 76
  7.9 0.9 %copy-start.7 = (f32[1,1,2,6,128]{4,2,3,1,0:T(2,128)S(1)}, f32[1,1,2,6,128]{4,2,3,1,0:T(2,128)}, u32[]{:S(2)}) copy-start(f32[1,1,2,6,128]{4,2,3,1,0:T(2,128)} %param.11) | copy-start | bytes 18436
  7.9 8.5 %copy-start = (bf16[1,2,384,384]{3,2,1,0:T(8,128)(2,1)S(1)}, bf16[1,2,384,384]{3,2,1,0:T(8,128)(2,1)}, u32[]{:S(2)}) copy-start(bf16[1,2,384,384]{3,2,1,0:T(8,128)(2,1)} %param.9) | copy-start | bytes 1769476
  9.4 13.5 %collective-permute-start.5 = (f32[2,6,128]{2,0,1:T(2,128)}, f32[2,6,128]{2,0,1:T(2,128)}, u32[]{:S(2)}, u32[]{:S(2)}) collective-permute-start(f32[2,6,128]{2,0,1:T(2,128)} %bitcast_subtract_fusion), channel_id=1, source_target_pairs={{0,1},{1,2},{2,3},{3,0},{4,5},{5,6},{6,7},{7,4},{8,9},{9,10},{10,1... | collective-permute-start | bytes 18440 | tf_op jit(solution)/shard_map/ppermute | solution.py:49
  12.4 10.9 %collective-permute-start.6 = (f32[2,6,128]{2,0,1:T(2,128)}, f32[2,6,128]{2,0,1:T(2,128)}, u32[]{:S(2)}, u32[]{:S(2)}) collective-permute-start(f32[2,6,128]{2,0,1:T(2,128)} %bitcast_subtract_fusion), channel_id=1, source_target_pairs={{0,2},{1,3},{2,0},{3,1},{4,6},{5,7},{6,4},{7,5},{8,10},{9,11},{10,... | collective-permute-start | bytes 18440 | tf_op jit(solution)/shard_map/ppermute | solution.py:49
  15.0 9.9 %collective-permute-start.7 = (f32[2,6,128]{2,0,1:T(2,128)}, f32[2,6,128]{2,0,1:T(2,128)}, u32[]{:S(2)}, u32[]{:S(2)}) collective-permute-start(f32[2,6,128]{2,0,1:T(2,128)} %bitcast_subtract_fusion), channel_id=1, source_target_pairs={{0,3},{1,0},{2,1},{3,2},{4,7},{5,4},{6,5},{7,6},{8,11},{9,8},{10,9... | collective-permute-start | bytes 18440 | tf_op jit(solution)/shard_map/ppermute | solution.py:49
  16.4 23.9 %collective-permute-start = (bf16[2,384,384]{2,1,0:T(8,128)(2,1)S(1)}, bf16[2,384,384]{2,1,0:T(8,128)(2,1)S(1)}, u32[]{:S(2)}, u32[]{:S(2)}) collective-permute-start(bf16[2,384,384]{2,1,0:T(8,128)(2,1)S(1)} %bitcast.218), channel_id=1, source_target_pairs={{0,4},{4,8},{8,12},{1,5},{5,9},{9,13},{2,6},{6,10},{10,14},{3,7},{... | collective-permute-start | bytes 1769480 | tf_op jit(solution)/shard_map/ppermute | solution.py:139
  17.7 22.5 %collective-permute-start.1 = (bf16[2,384,384]{2,1,0:T(8,128)(2,1)S(1)}, bf16[2,384,384]{2,1,0:T(8,128)(2,1)S(1)}, u32[]{:S(2)}, u32[]{:S(2)}) collective-permute-start(bf16[2,384,384]{2,1,0:T(8,128)(2,1)S(1)} %bitcast.219), channel_id=1, source_target_pairs={{4,0},{8,4},{12,8},{5,1},{9,5},{13,9},{6,2},{10,6},{14,10},{7,3},{... | collective-permute-start | bytes 1769480 | tf_op jit(solution)/shard_map/ppermute | solution.py:140
  22.0 3.9 %copy-start.6 = (f32[6,128,128]{2,1,0:T(8,128)S(1)}, f32[6,128,128]{2,1,0:T(8,128)}, u32[]{:S(2)}) copy-start(f32[6,128,128]{2,1,0:T(8,128)} %bitcast_convert_fusion) | copy-start | bytes 1179652
  22.9 13.4 %collective-permute-start.4 = (bf16[2,96,384]{2,1,0:T(8,128)(2,1)}, bf16[2,96,384]{2,1,0:T(8,128)(2,1)}, u32[]{:S(2)}, u32[]{:S(2)}) collective-permute-start(bf16[2,96,384]{2,1,0:T(8,128)(2,1)} %get-tuple-element.17), channel_id=1, source_target_pairs={{0,3},{1,0},{2,1},{3,2},{4,7},{5,4},{6,5},{7,6},{8,11},{9,8},{10,9... | collective-permute-start | bytes 442376 | tf_op jit(solution)/shard_map/ppermute | solution.py:49
  23.4 12.9 %collective-permute-start.2 = (bf16[2,96,384]{2,1,0:T(8,128)(2,1)}, bf16[2,96,384]{2,1,0:T(8,128)(2,1)}, u32[]{:S(2)}, u32[]{:S(2)}) collective-permute-start(bf16[2,96,384]{2,1,0:T(8,128)(2,1)} %get-tuple-element.15), channel_id=1, source_target_pairs={{0,1},{1,2},{2,3},{3,0},{4,5},{5,6},{6,7},{7,4},{8,9},{9,10},{10,1... | collective-permute-start | bytes 442376 | tf_op jit(solution)/shard_map/ppermute | solution.py:49
  24.9 13.9 %collective-permute-start.3 = (bf16[2,96,384]{2,1,0:T(8,128)(2,1)}, bf16[2,96,384]{2,1,0:T(8,128)(2,1)}, u32[]{:S(2)}, u32[]{:S(2)}) collective-permute-start(bf16[2,96,384]{2,1,0:T(8,128)(2,1)} %get-tuple-element.16), channel_id=1, source_target_pairs={{0,2},{1,3},{2,0},{3,1},{4,6},{5,7},{6,4},{7,5},{8,10},{9,11},{10,... | collective-permute-start | bytes 442376 | tf_op jit(solution)/shard_map/ppermute | solution.py:49

commit v3 on v0

--- a/solution.py
+++ b/solution.py
@@ -5,6 +5,7 @@
 import numpy as np
 import jax.numpy as jnp
 from jax import lax
+from jax.experimental import pallas as pl
 from jax.sharding import PartitionSpec as P
 
 
@@ -85,26 +86,64 @@
         "bij,ajk->abik", coil_image, transform, preferred_element_type=jnp.float32
     )
     half_done = combine_parts(products, 1.0).astype(jnp.bfloat16)
-    products = jnp.einsum("aij,bjk->abik", transform, half_done, preferred_element_type=jnp.float32)
-    kspace = combine_parts(products, 1.0).astype(jnp.bfloat16)
+    cos_t, sin_t = lax.optimization_barrier(transform)
+    block = jnp.concatenate(
+        [jnp.concatenate([cos_t, sin_t], axis=1), jnp.concatenate([-sin_t, cos_t], axis=1)]
+    )
+    extent = transform.shape[-1]
+    kspace = jnp.dot(
+        block, half_done.reshape(2 * extent, extent), preferred_element_type=jnp.float32
+    ).astype(jnp.bfloat16).reshape(2, extent, extent)
     contracted = jnp.einsum("pik,gjk->pgij", kspace, col_placed, preferred_element_type=jnp.float32)
-    predicted = jnp.sum(contracted * row_placed.astype(jnp.float32)[None], axis=2)
+    predicted = jnp.sum(contracted * row_placed[None], axis=2)
     return predicted - measured
+
+
+def _product_kernel(lhs_ref, rhs_ref, out_ref):
+    tiles, _, planes, patch_side, width = rhs_ref.shape
+    rhs = rhs_ref[...].reshape(tiles * planes * patch_side, width)
+    out_ref[0] = jnp.dot(lhs_ref[...], rhs, preferred_element_type=jnp.float32).astype(out_ref.dtype)
+
+
+def per_coil_product(lhs, rhs):
+    tiles, count, planes, patch_side, width = rhs.shape
+    height, depth = lhs.shape
+    return pl.pallas_call(
+        _product_kernel,
+        out_shape=jax.ShapeDtypeStruct((count, height, width), jnp.bfloat16),
+        grid=(count,),
+        in_specs=[
+            pl.BlockSpec((height, depth), lambda c: (0, 0)),
+            pl.BlockSpec((tiles, 1, planes, patch_side, width), lambda c: (0, c, 0, 0, 0)),
+        ],
+        out_specs=pl.BlockSpec((1, height, width), lambda c: (c, 0, 0)),
+        cost_estimate=pl.CostEstimate(
+            flops=2 * count * height * depth * width,
+            transcendentals=0,
+            bytes_accessed=2 * (height * depth + count * depth * width + count * height * width),
+        ),
+    )(lhs, rhs)
 
 
 def backward_rows(transform, residuals, map_rows, row_select, row_w, col_placed, coil_index):
     rows = map_rows.shape[2]
     spread = (row_w.astype(jnp.float32)[None, None] * residuals[:, :, :, None, :]).astype(jnp.bfloat16)
     placed = jnp.einsum(
-        "cpgrj,gjk->cpgrk", spread, col_placed, preferred_element_type=jnp.float32
+        "cpgrj,gjk->gcprk", spread, col_placed, preferred_element_type=jnp.float32
     ).astype(jnp.bfloat16)
     row_table = lax.dynamic_slice_in_dim(transform, coil_index * rows, rows, axis=1)
-    table_at = jnp.einsum(
-        "aij,gjr->aigr", row_table, row_select, preferred_element_type=jnp.float32
+    cos_rows, sin_rows = row_table[0], row_table[1]
+    block = jnp.stack(
+        [jnp.stack([cos_rows, -sin_rows], axis=1), jnp.stack([sin_rows, cos_rows], axis=1)]
+    )
+    block_at = jnp.einsum(
+        "oibj,gjr->oigbr", block, row_select, preferred_element_type=jnp.float32
     ).astype(jnp.bfloat16)
-    products = jnp.einsum("aigr,cbgrk->abcik", table_at, placed, preferred_element_type=jnp.float32)
-    half_back = combine_parts(products, -1.0).astype(jnp.bfloat16)
-    products = jnp.einsum("bcij,ajk->abcik", half_back, transform, preferred_element_type=jnp.float32)
+    tiles, coil_count, planes, patch_side, extent = placed.shape
+    half_back = per_coil_product(
+        block_at.reshape(2 * rows, tiles * planes * patch_side), placed
+    ).reshape(coil_count, 2, rows, extent)
+    products = jnp.einsum("cbij,ajk->abcik", half_back, transform, preferred_element_type=jnp.float32)
     coil_back = combine_parts(products, -1.0)
     maps = map_rows.astype(jnp.float32)
     real_part = jnp.sum(maps[:, 0] * coil_back[0] + maps[:, 1] * coil_back[1], axis=0)
@@ -162,7 +201,7 @@
     col_select = selector(band_col[0], extent, patch_side)
     exact = dict(preferred_element_type=jnp.float32)
     col_placed = jnp.einsum("gjq,gkq->gjk", col_w, col_select, **exact).astype(jnp.bfloat16)
-    row_placed = jnp.einsum("grj,gir->gij", row_w, row_select, **exact).astype(jnp.bfloat16)
+    row_placed = jnp.einsum("grj,gir->gij", row_w, row_select, **exact)
     residual = forward_residual(
         transform, images[0], coil_maps[0], kspace_data[0, 0], row_placed, col_placed
     )

time: 59.8 us -> 65.4 us (1.094)
  Pallas kernels: 0 us -> 5.14 us
  local copies, waits for them, and re-layouts: 3.69 us -> 6.99 us
  waiting for transfers between devices: 5.49 us -> 2.51 us
  other arithmetic: 9.84 us -> 8.86 us
    pallas_call x0 -> x1, Pallas kernels: none -> 5.14 us  [per_coil_product(): pl.pallas_call(_product_kernel, out_shape=jax.ShapeDtypeStruct((count, he...]
    ppermute x6, waiting for transfers between devices: 5.48 us -> 2.5 us  [rotated(): lax.ppermute(block, 'coil', [(i, (i + shift) % coil_count) for i in range...]
    sub x3 -> x1, other arithmetic: 2.14 us -> 0.06 us  [combine_parts(): imaginary = products[0, 1] - direction * products[1, 0]]
    add x3 -> x1, other arithmetic: 1.49 us -> 0.06 us  [combine_parts(): real_part = products[0, 0] + direction * products[1, 1]]
    unnamed x26, local copies, waits for them, and re-layouts: 1.51 us -> 2.86 us
    another operation x2 -> x3, other arithmetic: 0.19 us -> 1.28 us  [the longest x1 1.03 us: backward_rows(): jnp.stack([jnp.stack([cos_rows, -sin_rows], axis=1), jnp.stack([sin_rows,...]
    reshape x0 -> x1, local copies, waits for them, and re-layouts: none -> 1.04 us  [backward_rows(): block_at.reshape(2 * rows, tiles * planes * patch_side)]
    squeeze x0 -> x1, local copies, waits for them, and re-layouts: none -> 0.68 us  [backward_rows(): cos_rows, sin_rows = (row_table[0], row_table[1])]
  transfers between devices with their start and end apart: 8 -> 8, of which waited for: 1 -> 1; matrix products, arithmetic and copies ran while one was open for 22% -> 25% of each run, Pallas kernels for 0% -> 8%
where the time goes in v3:
time: 65.4 us; the launch traced here: 64.4 us
  blocking collectives  16.7 us (26%)
  matrix products  12.1 us (19%)
  starting transfers between devices  11.8 us (18%)
  other arithmetic  8.86 us (14%)
  local copies, waits for them, and re-layouts  6.99 us (11%)
  Pallas kernels  5.14 us (8%)
  waiting for transfers between devices  2.51 us (4%)
    all_gather x1, blocking collectives, body(): lax.all_gather(grad_rows, 'coil', axis=1, tiled=True).astype(jnp.float32)  16.7 us
    ppermute x6, starting transfers between devices, rotated(): lax.ppermute(block, 'coil', [(i, (i + shift) % coil_count) for i in range...  9.21 us
    pallas_call x1, Pallas kernels, per_coil_product(): pl.pallas_call(_product_kernel, out_shape=jax.ShapeDtypeStruct((count, he...  5.14 us
    dot_general x1, matrix products, backward_rows(): jnp.einsum('cpgrj,gjk->gcprk', spread, col_placed, preferred_element_type...  4.24 us
    unnamed x26, local copies, waits for them, and re-layouts  2.86 us
    ppermute x6, waiting for transfers between devices, rotated(): lax.ppermute(block, 'coil', [(i, (i + shift) % coil_count) for i in range...  2.5 us
    dot_general x1, matrix products, backward_rows(): jnp.einsum('oibj,gjr->oigbr', block, row_select, preferred_element_type=j...  2.02 us
    dot_general x1, matrix products, backward_rows(): jnp.einsum('cbij,ajk->abcik', half_back, transform, preferred_element_typ...  1.83 us
  transfers between devices with their start and end apart: 8, of which 1 were waited for; matrix products, arithmetic and copies ran while one was open for 25% of the time, Pallas kernels for 8%

profile of v3, /device:TPU:0, one launch (start us, length us, event | category | flops | bytes accessed | tf_op | source)
XLA Modules:
  0.0 64.4 jit_solution(7037563012423144791)
XLA Ops:
  0.0 1.2 %bitcast_convert_fusion.1 = f32[2,384,384]{2,1,0:T(8,128)S(1)} fusion(bf16[1,2,384,384]{3,2,1,0:T(8,128)(2,1)} %param.9), kind=kLoop, calls=%fused_computation.115 | loop fusion | flops 294912 | bytes 1769472 | tf_op jit(solution)/shard_map/convert_element_type | solution.py:166
  1.5 0.9 %copy-done.5 = bf16[2,384,384,1]{2,1,0,3:T(8,128)(2,1)S(1)} copy-done((bf16[2,384,384,1]{2,1,0,3:T(8,128)(2,1)S(1)}, bf16[2,384,384,1]{2,1,0,3:T(8,128)(2,1)}, u32[]{:S(2)}) %copy-start.5) | copy-done | bytes 589848
  2.4 0.8 %convolution_bitcast_fusion.1 = f32[2,2,384,384]{3,2,0,1:T(8,128)S(1)} fusion(bf16[2,384,384,1]{2,1,0,3:T(8,128)(2,1)S(1)} %copy-done.5, bf16[1,384,384]{2,1,0:T(8,128)(2,1)S(1)} %get-tuple-element.12, bf16[1,384,384]{2,1,0:T(8,128)(2,1)S(1)} %get-tuple-element.11), kind=kOutput, calls=%fused_computation.7 | convolution fusion | flops 454164480 | bytes 3538944 | tf_op jit(solution)/shard_map/bij,ajk->abik/dot_general | solution.py:85
  3.3 0.9 %copy-done.2 = bf16[2,384,384]{2,1,0:T(8,128)(2,1)S(1)} copy-done((bf16[2,384,384]{2,1,0:T(8,128)(2,1)S(1)}, bf16[2,384,384]{2,1,0:T(8,128)(2,1)}, u32[]{:S(2)}) %copy-start.2) | copy-done | bytes 589848
  4.4 0.5 copy-done.11
  7.2 0.8 %convolution_convert_fusion.3 = bf16[768,384]{1,0:T(8,128)(2,1)S(1)} fusion(bf16[768,384]{1,0:T(8,128)(2,1)S(1)} %bitcast.215, bf16[384,384]{1,0:T(8,128)(2,1)S(1)} %get-tuple-element.14, bf16[384,384]{1,0:T(8,128)(2,1)S(1)} %fusion.58, bf16[384,384]{1,0:T(8,128)(2,1)S(1)} %get-tuple-element.13), kind=kOutput, calls=%fused_computation.10 | convolution fusion | flops 457998336 | bytes 2064384 | tf_op jit(solution)/shard_map/dot_general | solution.py:94
  8.0 0.9 %fusion = f32[2,6,128]{2,0,1:T(2,128)S(1)} fusion(bf16[2,384,384,1]{2,1,0,3:T(8,128)(2,1)S(1)} %bitcast.224, f32[6,384,128]{1,2,0:T(8,128)S(1)} %fusion.12, bf16[6,128,384]{2,1,0:T(8,128)(2,1)S(1)} %convolution_convert_fusion.4), kind=kOutput, calls=%fused_computation.5 | convolution fusion | flops 454162944 | bytes 2365440 | tf_op jit(solution)/shard_map/pik,gjk->pgij/dot_general | solution.py:97
  8.9 0.6 bitcast_subtract_fusion
  9.5 3.1 %collective-permute-start.5 = (f32[2,6,128]{2,0,1:T(2,128)}, f32[2,6,128]{2,0,1:T(2,128)}, u32[]{:S(2)}, u32[]{:S(2)}) collective-permute-start(f32[2,6,128]{2,0,1:T(2,128)} %bitcast_subtract_fusion), channel_id=1, source_target_pairs={{0,1},{1,2},{2,3},{3,0},{4,5},{5,6},{6,7},{7,4},{8,9},{9,10},{10,1... | collective-permute-start | bytes 18440 | tf_op jit(solution)/shard_map/ppermute | solution.py:50
  12.6 2.6 %collective-permute-start.6 = (f32[2,6,128]{2,0,1:T(2,128)}, f32[2,6,128]{2,0,1:T(2,128)}, u32[]{:S(2)}, u32[]{:S(2)}) collective-permute-start(f32[2,6,128]{2,0,1:T(2,128)} %bitcast_subtract_fusion), channel_id=1, source_target_pairs={{0,2},{1,3},{2,0},{3,1},{4,6},{5,7},{6,4},{7,5},{8,10},{9,11},{10,... | collective-permute-start | bytes 18440 | tf_op jit(solution)/shard_map/ppermute | solution.py:50
  15.2 1.3 %collective-permute-start.7 = (f32[2,6,128]{2,0,1:T(2,128)}, f32[2,6,128]{2,0,1:T(2,128)}, u32[]{:S(2)}, u32[]{:S(2)}) collective-permute-start(f32[2,6,128]{2,0,1:T(2,128)} %bitcast_subtract_fusion), channel_id=1, source_target_pairs={{0,3},{1,0},{2,1},{3,2},{4,7},{5,4},{6,5},{7,6},{8,11},{9,8},{10,9... | collective-permute-start | bytes 18440 | tf_op jit(solution)/shard_map/ppermute | solution.py:50
  16.5 1.3 %collective-permute-start = (bf16[2,384,384]{2,1,0:T(8,128)(2,1)S(1)}, bf16[2,384,384]{2,1,0:T(8,128)(2,1)S(1)}, u32[]{:S(2)}, u32[]{:S(2)}) collective-permute-start(bf16[2,384,384]{2,1,0:T(8,128)(2,1)S(1)} %bitcast.211), channel_id=1, source_target_pairs={{0,4},{4,8},{8,12},{1,5},{5,9},{9,13},{2,6},{6,10},{10,14},{3,7},{... | collective-permute-start | bytes 1769480 | tf_op jit(solution)/shard_map/ppermute | solution.py:174
  17.9 1.3 %collective-permute-start.1 = (bf16[2,384,384]{2,1,0:T(8,128)(2,1)S(1)}, bf16[2,384,384]{2,1,0:T(8,128)(2,1)S(1)}, u32[]{:S(2)}, u32[]{:S(2)}) collective-permute-start(bf16[2,384,384]{2,1,0:T(8,128)(2,1)S(1)} %bitcast.212), channel_id=1, source_target_pairs={{4,0},{8,4},{12,8},{5,1},{9,5},{13,9},{6,2},{10,6},{14,10},{7,3},{... | collective-permute-start | bytes 1769480 | tf_op jit(solution)/shard_map/ppermute | solution.py:175
  19.2 0.7 %dynamic-slice_bitcast_fusion.3 = (bf16[96,1,384]{2,0,1:T(8,128)(2,1)}, bf16[96,1,384]{2,0,1:T(8,128)(2,1)}) fusion(bf16[2,384,384]{2,1,0:T(8,128)(2,1)S(1)} %copy-done.2, s32[]{:T(128)S(6)} %add.146, s32[]{:T(128)S(6)} %select_n.28), kind=kLoop, calls=%fused_computation.98 | loop fusion | bytes 294920 | tf_op jit(solution)/shard_map/squeeze | solution.py:135
  19.8 0.6 fusion.52
  20.5 1.0 %bitcast_convert_fusion = f32[6,128,128]{2,1,0:T(8,128)S(1)} fusion(bf16[1,6,128,128]{3,1,2,0:T(8,128)(2,1)} %copy-done.3), kind=kLoop, calls=%fused_computation.90 | loop fusion | flops 98304 | bytes 589824 | tf_op jit(solution)/shard_map/convert_element_type | solution.py:130
  21.5 1.0 %maximum_bitcast_fusion.4 = (bf16[1,96,2,384]{3,1,2,0:T(8,128)(2,1)S(1)}, bf16[1,96,2,384]{3,1,2,0:T(8,128)(2,1)S(1)}) fusion(bf16[96,1,384]{2,0,1:T(8,128)(2,1)} %fusion.52, bf16[96,1,384]{2,0,1:T(8,128)(2,1)} %get-tuple-element.16, bf16[96,1,384]{2,0,1:T(8,128)(2,1)} %get-tuple-element.15), kind=kLoop, calls=%fused_computation.91 | loop fusion | flops 147456 | bytes 516096 | tf_op jit(solution)/shard_map/stack | solution.py:136
  22.5 2.0 %fusion.3 = bf16[2,96,6,2,128]{4,1,3,0,2:T(8,128)(2,1)} fusion(s32[6,128]{1,0:T(8,128)} %copy-done.9, bf16[1,96,2,384]{3,1,2,0:T(8,128)(2,1)S(1)} %get-tuple-element.23, bf16[1,96,2,384]{3,1,2,0:T(8,128)(2,1)S(1)} %get-tuple-element.22), kind=kOutput, calls=%fused_computation.13 | convolution fusion | flops 227672064 | bytes 887808 | tf_op jit(solution)/shard_map/oibj,gjr->oigbr/dot_general | solution.py:139
  24.6 0.8 %dynamic-slice_bitcast_fusion.2 = (bf16[2,96,384]{2,1,0:T(8,128)(2,1)}, bf16[2,96,384]{2,1,0:T(8,128)(2,1)}, bf16[2,96,384]{2,1,0:T(8,128)(2,1)}) fusion(bf16[1,2,384,384]{3,2,1,0:T(8,128)(2,1)S(1)} %copy-done.1, s32[]{:T(128)S(6)} %select_n.30, s32[]{:T(128)S(6)} %select_n.32, s32[]{:T(128)S(6)} %select_n.34), kind=kLoop, calls=%fused_computation.96 | loop fusion | bytes 884748 | tf_op jit(solution)/shard_map/dynamic_slice | solution.py:57
  25.4 1.5 %copy.11 = bf16[2,96,6,2,128]{4,3,2,1,0:T(2,128)(2,1)S(1)} copy(bf16[2,96,6,2,128]{4,1,3,0,2:T(8,128)(2,1)} %fusion.3) | data formatting | bytes 1179648 | tf_op jit(solution)/shard_map/convert_element_type | solution.py:141
  26.9 1.0 %reshape.156.lhs_ref = bf16[192,1536]{1,0:T(8,128)(2,1)} reshape(bf16[2,96,6,2,128]{4,3,2,1,0:T(2,128)(2,1)S(1)} %copy.11) | data formatting | bytes 1179648 | tf_op jit(solution)/shard_map/reshape | solution.py:144
  28.0 0.5 collective-permute-start.4
  28.4 1.6 %collective-permute-start.2 = (bf16[2,96,384]{2,1,0:T(8,128)(2,1)}, bf16[2,96,384]{2,1,0:T(8,128)(2,1)}, u32[]{:S(2)}, u32[]{:S(2)}) collective-permute-start(bf16[2,96,384]{2,1,0:T(8,128)(2,1)} %get-tuple-element.17), channel_id=1, source_target_pairs={{0,1},{1,2},{2,3},{3,0},{4,5},{5,6},{6,7},{7,4},{8,9},{9,10},{10,1... | collective-permute-start | bytes 442376 | tf_op jit(solution)/shard_map/ppermute | solution.py:50
  30.2 4.2 %convolution_convert_fusion.2.rhs_ref = bf16[6,4,2,128,384]{4,3,2,1,0:T(8,128)(2,1)} fusion(f32[6,128,128]{2,1,0:T(8,128)S(1)} %bitcast_convert_fusion, bf16[6,128,384]{2,1,0:T(8,128)(2,1)S(1)} %convolution_convert_fusion.4, f32[1,2,6,128]{3,1,2,0:T(2,128)} %bitcast.44, f32[1,2,6,128]{3,1,2,0:T(2,128)} %bitcast.43, f32[1,2,6,128]{3,1,2,0:T(2,128)} %bitcast.42, ...), kind=kOutput, calls=%fused_computation.3 | convolution fusion | flops 607930368 | bytes 5726208 | tf_op jit(solution)/shard_map/cpgrj,gjk->gcprk/dot_general | solution.py:131
  34.4 5.1 %shard_map.91 = bf16[4,192,384]{2,1,0:T(8,128)(2,1)} custom-call(bf16[192,1536]{1,0:T(8,128)(2,1)} %reshape.156.lhs_ref, bf16[6,4,2,128,384]{4,3,2,1,0:T(8,128)(2,1)} %convolution_convert_fusion.2.rhs_ref), custom_call_target="tpu_custom_call" | custom-call | flops 905969664 | bytes 5898240 | tf_op jit(solution)/shard_map/pallas_call | solution.py:111
  39.6 1.8 %convolution_bitcast_fusion = f32[2,2,4,96,384]{4,3,0,1,2:T(8,128)S(1)} fusion(bf16[4,2,96,384,1]{3,2,4,1,0:T(8,128)(2,1)} %bitcast.213, bf16[2,384,384,1,1]{2,1,0,4,3:T(8,128)(2,1)S(1)} %copy-done.4), kind=kOutput, calls=%fused_computation.6 | convolution fusion | flops 452984832 | bytes 3538944 | tf_op jit(solution)/shard_map/cbij,ajk->abcik/dot_general | solution.py:146
  41.4 2.5 %collective-permute-done.3 = bf16[2,96,384]{2,1,0:T(8,128)(2,1)} collective-permute-done((bf16[2,96,384]{2,1,0:T(8,128)(2,1)}, bf16[2,96,384]{2,1,0:T(8,128)(2,1)}, u32[]{:S(2)}, u32[]{:S(2)}) %collective-permute-start.3) | collective-permute-done | bytes 147488 | tf_op jit(solution)/shard_map/ppermute | solution.py:50
  43.9 1.2 %maximum_convert_fusion = f32[4,2,96,384]{3,2,0,1:T(8,128)S(1)} fusion(bf16[1,2,96,384]{3,2,0,1:T(8,128)(2,1)} %bitcast.10, bf16[1,2,96,384]{3,2,0,1:T(8,128)(2,1)} %bitcast.8, bf16[1,2,96,384]{3,2,0,1:T(8,128)(2,1)} %bitcast.6, bf16[1,2,96,384]{3,2,0,1:T(8,128)(2,1)S(1)} %constant_dynamic-slice_fusion), kind=kLoop, calls=%fused_computation.62 | loop fusion | flops 1179648 | bytes 1769472 | tf_op jit(solution)/shard_map/convert_element_type | solution.py:148
  45.6 0.4 fusion.28
  46.1 0.5 subtract_bitcast_fusion
  46.5 16.7 %all_gather.3 = bf16[2,384,384]{2,1,0:T(8,128)(2,1)S(1)} all-gather(bf16[2,96,384]{2,1,0:T(8,128)(2,1)S(1)} %pad_maximum_fusion.1), channel_id=1, replica_groups=mesh['grp'=2,'frame'=4,'coil'=4] {'coil'}, dimensions={1}, use_global_device_ids=true | all-gather | bytes 737280 | tf_op jit(solution)/shard_map/all_gather | solution.py:215
  63.2 1.3 %fusion.11 = f32[1,2,384,384]{3,2,1,0:T(8,128)} fusion(f32[1,2,384,384]{3,2,1,0:T(8,128)S(1)} %subtract_bitcast_fusion, bf16[1,2,384,384]{3,2,1,0:T(8,128)(2,1)S(1)} %copy-done, bf16[2,384,384]{2,1,0:T(8,128)(2,1)S(1)} %all_gather.3), kind=kLoop, calls=%fused_computation.22 | loop fusion | flops 1474560 | bytes 3538944 | tf_op jit(solution)/shard_map/sub | solution.py:216
  (49 shorter events, 3.6 us)
Async XLA Ops:
  0.0 1.2 %copy-start.1 = (bf16[1,2,384,384]{3,2,1,0:T(8,128)(2,1)S(1)}, bf16[1,2,384,384]{3,2,1,0:T(8,128)(2,1)}, u32[]{:S(2)}) copy-start(bf16[1,2,384,384]{3,2,1,0:T(8,128)(2,1)} %param.10) | copy-start | bytes 1769476
  1.3 1.1 %copy-start.5 = (bf16[2,384,384,1]{2,1,0,3:T(8,128)(2,1)S(1)}, bf16[2,384,384,1]{2,1,0,3:T(8,128)(2,1)}, u32[]{:S(2)}) copy-start(bf16[2,384,384,1]{2,1,0,3:T(8,128)(2,1)} %constant.59) | copy-start | bytes 1769476
  3.2 1.1 %copy-start.2 = (bf16[2,384,384]{2,1,0:T(8,128)(2,1)S(1)}, bf16[2,384,384]{2,1,0:T(8,128)(2,1)}, u32[]{:S(2)}) copy-start(bf16[2,384,384]{2,1,0:T(8,128)(2,1)} %constant.52.clone) | copy-start | bytes 1769476
  4.2 0.7 %copy-start.11 = (s32[1,6]{1,0:T(1,128)S(1)}, s32[1,6]{1,0:T(1,128)}, u32[]{:S(2)}) copy-start(s32[1,6]{1,0:T(1,128)} %param.13) | copy-start | bytes 76
  4.2 1.1 %copy-start.6 = (bf16[16,128,128]{2,1,0:T(8,128)(2,1)S(1)}, bf16[16,128,128]{2,1,0:T(8,128)(2,1)}, u32[]{:S(2)}) copy-start(bf16[16,128,128]{2,1,0:T(8,128)(2,1)} %param.15) | copy-start | bytes 1572868
  4.2 1.1 %copy-start.10 = (s32[1,6]{1,0:T(1,128)S(1)}, s32[1,6]{1,0:T(1,128)}, u32[]{:S(2)}) copy-start(s32[1,6]{1,0:T(1,128)} %param.12) | copy-start | bytes 76
  4.2 1.5 %copy-start.7 = (bf16[16,128,128]{2,1,0:T(8,128)(2,1)S(1)}, bf16[16,128,128]{2,1,0:T(8,128)(2,1)}, u32[]{:S(2)}) copy-start(bf16[16,128,128]{2,1,0:T(8,128)(2,1)} %param.16) | copy-start | bytes 1572868
  4.3 1.8 %copy-start.12 = (s32[1,6]{1,0:T(1,128)S(1)}, s32[1,6]{1,0:T(1,128)}, u32[]{:S(2)}) copy-start(s32[1,6]{1,0:T(1,128)} %param.14) | copy-start | bytes 76
  5.0 1.3 %copy-start.9 = (s32[6,128]{1,0:T(8,128)}, s32[6,128]{1,0:T(8,128)S(1)}, u32[]{:S(2)}) copy-start(s32[6,128]{1,0:T(8,128)S(1)} %iota_add_fusion.1) | copy-start | bytes 9220
  5.7 0.7 %copy-start.3 = (bf16[1,6,128,128]{3,1,2,0:T(8,128)(2,1)}, bf16[1,6,128,128]{3,1,2,0:T(8,128)(2,1)S(1)}, u32[]{:S(2)}) copy-start(bf16[1,6,128,128]{3,1,2,0:T(8,128)(2,1)S(1)} %fusion.15) | copy-start | bytes 589828
  8.0 0.9 %copy-start.8 = (f32[1,1,2,6,128]{4,2,3,1,0:T(2,128)S(1)}, f32[1,1,2,6,128]{4,2,3,1,0:T(2,128)}, u32[]{:S(2)}) copy-start(f32[1,1,2,6,128]{4,2,3,1,0:T(2,128)} %param.11) | copy-start | bytes 18436
  8.0 8.5 %copy-start = (bf16[1,2,384,384]{3,2,1,0:T(8,128)(2,1)S(1)}, bf16[1,2,384,384]{3,2,1,0:T(8,128)(2,1)}, u32[]{:S(2)}) copy-start(bf16[1,2,384,384]{3,2,1,0:T(8,128)(2,1)} %param.9) | copy-start | bytes 1769476
  9.5 18.4 %collective-permute-start.5 = (f32[2,6,128]{2,0,1:T(2,128)}, f32[2,6,128]{2,0,1:T(2,128)}, u32[]{:S(2)}, u32[]{:S(2)}) collective-permute-start(f32[2,6,128]{2,0,1:T(2,128)} %bitcast_subtract_fusion), channel_id=1, source_target_pairs={{0,1},{1,2},{2,3},{3,0},{4,5},{5,6},{6,7},{7,4},{8,9},{9,10},{10,1... | collective-permute-start | bytes 18440 | tf_op jit(solution)/shard_map/ppermute | solution.py:50
  12.6 15.8 %collective-permute-start.6 = (f32[2,6,128]{2,0,1:T(2,128)}, f32[2,6,128]{2,0,1:T(2,128)}, u32[]{:S(2)}, u32[]{:S(2)}) collective-permute-start(f32[2,6,128]{2,0,1:T(2,128)} %bitcast_subtract_fusion), channel_id=1, source_target_pairs={{0,2},{1,3},{2,0},{3,1},{4,6},{5,7},{6,4},{7,5},{8,10},{9,11},{10,... | collective-permute-start | bytes 18440 | tf_op jit(solution)/shard_map/ppermute | solution.py:50
  15.2 14.8 %collective-permute-start.7 = (f32[2,6,128]{2,0,1:T(2,128)}, f32[2,6,128]{2,0,1:T(2,128)}, u32[]{:S(2)}, u32[]{:S(2)}) collective-permute-start(f32[2,6,128]{2,0,1:T(2,128)} %bitcast_subtract_fusion), channel_id=1, source_target_pairs={{0,3},{1,0},{2,1},{3,2},{4,7},{5,4},{6,5},{7,6},{8,11},{9,8},{10,9... | collective-permute-start | bytes 18440 | tf_op jit(solution)/shard_map/ppermute | solution.py:50
  16.5 28.9 %collective-permute-start = (bf16[2,384,384]{2,1,0:T(8,128)(2,1)S(1)}, bf16[2,384,384]{2,1,0:T(8,128)(2,1)S(1)}, u32[]{:S(2)}, u32[]{:S(2)}) collective-permute-start(bf16[2,384,384]{2,1,0:T(8,128)(2,1)S(1)} %bitcast.211), channel_id=1, source_target_pairs={{0,4},{4,8},{8,12},{1,5},{5,9},{9,13},{2,6},{6,10},{10,14},{3,7},{... | collective-permute-start | bytes 1769480 | tf_op jit(solution)/shard_map/ppermute | solution.py:174
  17.9 27.6 %collective-permute-start.1 = (bf16[2,384,384]{2,1,0:T(8,128)(2,1)S(1)}, bf16[2,384,384]{2,1,0:T(8,128)(2,1)S(1)}, u32[]{:S(2)}, u32[]{:S(2)}) collective-permute-start(bf16[2,384,384]{2,1,0:T(8,128)(2,1)S(1)} %bitcast.212), channel_id=1, source_target_pairs={{4,0},{8,4},{12,8},{5,1},{9,5},{13,9},{6,2},{10,6},{14,10},{7,3},{... | collective-permute-start | bytes 1769480 | tf_op jit(solution)/shard_map/ppermute | solution.py:175
  28.0 13.4 %collective-permute-start.4 = (bf16[2,96,384]{2,1,0:T(8,128)(2,1)}, bf16[2,96,384]{2,1,0:T(8,128)(2,1)}, u32[]{:S(2)}, u32[]{:S(2)}) collective-permute-start(bf16[2,96,384]{2,1,0:T(8,128)(2,1)} %get-tuple-element.19), channel_id=1, source_target_pairs={{0,3},{1,0},{2,1},{3,2},{4,7},{5,4},{6,5},{7,6},{8,11},{9,8},{10,9... | collective-permute-start | bytes 442376 | tf_op jit(solution)/shard_map/ppermute | solution.py:50
  28.4 13.0 %collective-permute-start.2 = (bf16[2,96,384]{2,1,0:T(8,128)(2,1)}, bf16[2,96,384]{2,1,0:T(8,128)(2,1)}, u32[]{:S(2)}, u32[]{:S(2)}) collective-permute-start(bf16[2,96,384]{2,1,0:T(8,128)(2,1)} %get-tuple-element.17), channel_id=1, source_target_pairs={{0,1},{1,2},{2,3},{3,0},{4,5},{5,6},{6,7},{7,4},{8,9},{9,10},{10,1... | collective-permute-start | bytes 442376 | tf_op jit(solution)/shard_map/ppermute | solution.py:50
  30.0 13.9 %collective-permute-start.3 = (bf16[2,96,384]{2,1,0:T(8,128)(2,1)}, bf16[2,96,384]{2,1,0:T(8,128)(2,1)}, u32[]{:S(2)}, u32[]{:S(2)}) collective-permute-start(bf16[2,96,384]{2,1,0:T(8,128)(2,1)} %get-tuple-element.18), channel_id=1, source_target_pairs={{0,2},{1,3},{2,0},{3,1},{4,6},{5,7},{6,4},{7,5},{8,10},{9,11},{10,... | collective-permute-start | bytes 442376 | tf_op jit(solution)/shard_map/ppermute | solution.py:50
  34.4 5.1 %copy-start.4 = (bf16[2,384,384,1,1]{2,1,0,4,3:T(8,128)(2,1)S(1)}, bf16[2,384,384,1,1]{2,1,0,4,3:T(8,128)(2,1)}, u32[]{:S(2)}) copy-start(bf16[2,384,384,1,1]{2,1,0,4,3:T(8,128)(2,1)} %constant.60) | copy-start | bytes 1769476

commit v4 on v0

--- a/solution.py
+++ b/solution.py
@@ -45,14 +45,21 @@
     return jnp.stack([real_part, imaginary])
 
 
+def partner(index, coil_count, shift):
+    if coil_count & (coil_count - 1) == 0:
+        return index ^ shift
+    return (index + shift) % coil_count
+
+
 def rotated(block, coil_count, shift):
-    return lax.ppermute(block, "coil", [(i, (i + shift) % coil_count) for i in range(coil_count)])
+    pairs = [(i, partner(i, coil_count, shift)) for i in range(coil_count)]
+    return lax.ppermute(block, "coil", pairs)
 
 
 def exchange_rows(coil_map, rows, coil_count, coil_index):
     received = [lax.dynamic_slice_in_dim(coil_map, coil_index * rows, rows, axis=1)]
     for shift in range(1, coil_count):
-        target = (coil_index + shift) % coil_count
+        target = partner(coil_index, coil_count, shift)
         block = lax.dynamic_slice_in_dim(coil_map, target * rows, rows, axis=1)
         received.append(rotated(block, coil_count, shift))
     return jnp.stack(received)
@@ -85,10 +92,16 @@
         "bij,ajk->abik", coil_image, transform, preferred_element_type=jnp.float32
     )
     half_done = combine_parts(products, 1.0).astype(jnp.bfloat16)
-    products = jnp.einsum("aij,bjk->abik", transform, half_done, preferred_element_type=jnp.float32)
-    kspace = combine_parts(products, 1.0).astype(jnp.bfloat16)
+    cos_t, sin_t = lax.optimization_barrier(transform)
+    block = jnp.concatenate(
+        [jnp.concatenate([cos_t, sin_t], axis=1), jnp.concatenate([-sin_t, cos_t], axis=1)]
+    )
+    extent = transform.shape[-1]
+    kspace = jnp.dot(
+        block, half_done.reshape(2 * extent, extent), preferred_element_type=jnp.float32
+    ).astype(jnp.bfloat16).reshape(2, extent, extent)
     contracted = jnp.einsum("pik,gjk->pgij", kspace, col_placed, preferred_element_type=jnp.float32)
-    predicted = jnp.sum(contracted * row_placed.astype(jnp.float32)[None], axis=2)
+    predicted = jnp.sum(contracted * row_placed[None], axis=2)
     return predicted - measured
 
 
@@ -162,7 +175,7 @@
     col_select = selector(band_col[0], extent, patch_side)
     exact = dict(preferred_element_type=jnp.float32)
     col_placed = jnp.einsum("gjq,gkq->gjk", col_w, col_select, **exact).astype(jnp.bfloat16)
-    row_placed = jnp.einsum("grj,gir->gij", row_w, row_select, **exact).astype(jnp.bfloat16)
+    row_placed = jnp.einsum("grj,gir->gij", row_w, row_select, **exact)
     residual = forward_residual(
         transform, images[0], coil_maps[0], kspace_data[0, 0], row_placed, col_placed
     )

time: 59.8 us -> 57.9 us (0.968)
  waiting for transfers between devices: 5.49 us -> 2.7 us
  matrix products: 11.5 us -> 10.6 us
  starting transfers between devices: 11.9 us -> 12.8 us
    ppermute x6, waiting for transfers between devices: 5.48 us -> 2.69 us  [rotated(): return lax.ppermute(block, 'coil', pairs)]
    convert_element_type x1 -> x0, local copies, waits for them, and re-layouts: 1.38 us -> none  [forward_residual(): row_placed.astype(jnp.float32)[None]]
    unnamed x26 -> x24, local copies, waits for them, and re-layouts: 1.51 us -> 2.75 us
    dot_general x1, matrix products: 2.06 us -> 1.1 us  [backward_rows(): jnp.einsum('aij,gjr->aigr', row_table, row_select, preferred_element_type...]
    ppermute x6, starting transfers between devices: 9.31 us -> 10.2 us  [rotated(): return lax.ppermute(block, 'coil', pairs)]
    sub x3 -> x2, other arithmetic: 2.14 us -> 1.37 us  [combine_parts(): imaginary = products[0, 1] - direction * products[1, 0]]
    another operation x1, other arithmetic: 0.01 us -> 0.74 us  [body(): jnp.stack([residual] + [rotated(residual, coil_count, shift) for shift in...]
    add x3 -> x2, other arithmetic: 1.49 us -> 1.43 us  [combine_parts(): real_part = products[0, 0] + direction * products[1, 1]]
  transfers between devices with their start and end apart: 8 -> 8, of which waited for: 1 -> 1; matrix products, arithmetic and copies ran while one was open for 22% -> 23% of each run, Pallas kernels for 0% -> 0%
where the time goes in v4:
time: 57.9 us; the launch traced here: 57.4 us
  blocking collectives  16.9 us (29%)
  starting transfers between devices  12.8 us (22%)
  matrix products  10.6 us (18%)
  other arithmetic  10.4 us (18%)
  local copies, waits for them, and re-layouts  3.61 us (6%)
  waiting for transfers between devices  2.7 us (5%)
    all_gather x1, blocking collectives, body(): lax.all_gather(grad_rows, 'coil', axis=1, tiled=True).astype(jnp.float32)  16.9 us
    ppermute x6, starting transfers between devices, rotated(): return lax.ppermute(block, 'coil', pairs)  10.2 us
    dot_general x1, matrix products, backward_rows(): jnp.einsum('aigr,cbgrk->abcik', table_at, placed, preferred_element_type=...  4.72 us
    unnamed x24, local copies, waits for them, and re-layouts  2.75 us
    ppermute x6, waiting for transfers between devices, rotated(): return lax.ppermute(block, 'coil', pairs)  2.69 us
    add x2, other arithmetic, combine_parts(): real_part = products[0, 0] + direction * products[1, 1]  1.43 us
    sub x2, other arithmetic, combine_parts(): imaginary = products[0, 1] - direction * products[1, 0]  1.37 us
    ppermute x1, starting transfers between devices, tv_single(): lax.ppermute(image, 'frame', [(i, i + 1) for i in range(count - 1)])  1.32 us
  transfers between devices with their start and end apart: 8, of which 1 were waited for; matrix products, arithmetic and copies ran while one was open for 23% of the time, Pallas kernels for 0%

profile of v4, /device:TPU:0, one launch (start us, length us, event | category | flops | bytes accessed | tf_op | source)
XLA Modules:
  0.0 57.4 jit_solution(14206039463812558830)
XLA Ops:
  0.0 1.2 %bitcast_convert_fusion.1 = f32[2,384,384]{2,1,0:T(8,128)S(1)} fusion(bf16[1,2,384,384]{3,2,1,0:T(8,128)(2,1)} %param.9), kind=kLoop, calls=%fused_computation.125 | loop fusion | flops 294912 | bytes 1769472 | tf_op jit(solution)/shard_map/convert_element_type | solution.py:140
  1.5 0.9 %copy-done.4 = bf16[2,384,384,1]{2,1,0,3:T(8,128)(2,1)S(1)} copy-done((bf16[2,384,384,1]{2,1,0,3:T(8,128)(2,1)S(1)}, bf16[2,384,384,1]{2,1,0,3:T(8,128)(2,1)}, u32[]{:S(2)}) %copy-start.4) | copy-done | bytes 589848
  2.4 0.8 %convolution_bitcast_fusion.1 = f32[2,2,384,384]{3,2,0,1:T(8,128)S(1)} fusion(bf16[2,384,384,1]{2,1,0,3:T(8,128)(2,1)S(1)} %copy-done.4, bf16[1,384,384]{2,1,0:T(8,128)(2,1)S(1)} %get-tuple-element.12, bf16[1,384,384]{2,1,0:T(8,128)(2,1)S(1)} %get-tuple-element.11), kind=kOutput, calls=%fused_computation.11 | convolution fusion | flops 454164480 | bytes 3538944 | tf_op jit(solution)/shard_map/bij,ajk->abik/dot_general | solution.py:91
  3.3 0.9 %copy-done.2 = bf16[2,384,384]{2,1,0:T(8,128)(2,1)S(1)} copy-done((bf16[2,384,384]{2,1,0:T(8,128)(2,1)S(1)}, bf16[2,384,384]{2,1,0:T(8,128)(2,1)}, u32[]{:S(2)}) %copy-start.2) | copy-done | bytes 589848
  4.4 0.5 copy-done.10
  5.3 0.4 fusion.28
  5.7 0.4 fusion.27
  6.3 0.4 fusion.22
  6.7 0.4 convolution_convert_fusion.3
  7.1 0.8 %convolution_convert_fusion.2 = bf16[768,384]{1,0:T(8,128)(2,1)S(1)} fusion(bf16[768,384]{1,0:T(8,128)(2,1)S(1)} %bitcast.219, bf16[384,384]{1,0:T(8,128)(2,1)S(1)} %get-tuple-element.14, bf16[384,384]{1,0:T(8,128)(2,1)S(1)} %fusion.79, bf16[384,384]{1,0:T(8,128)(2,1)S(1)} %get-tuple-element.13), kind=kOutput, calls=%fused_computation.14 | convolution fusion | flops 457998336 | bytes 2064384 | tf_op jit(solution)/shard_map/dot_general | solution.py:100
  7.9 0.9 %fusion.5 = f32[2,6,128]{2,0,1:T(2,128)S(1)} fusion(bf16[2,384,384,1]{2,1,0,3:T(8,128)(2,1)S(1)} %bitcast.228, f32[6,384,128]{1,2,0:T(8,128)S(1)} %fusion.22, bf16[6,128,384]{2,1,0:T(8,128)(2,1)S(1)} %convolution_convert_fusion.3), kind=kOutput, calls=%fused_computation.8 | convolution fusion | flops 454162944 | bytes 2365440 | tf_op jit(solution)/shard_map/pik,gjk->pgij/dot_general | solution.py:103
  8.8 0.6 %bitcast_subtract_fusion = f32[2,6,128]{2,0,1:T(2,128)} fusion(f32[2,6,128]{2,0,1:T(2,128)S(1)} %fusion.5, f32[1,1,2,6,128]{4,2,3,1,0:T(2,128)S(1)} %copy-done.8), kind=kLoop, calls=%fused_computation.113 | loop fusion | flops 1536 | bytes 18432 | tf_op jit(solution)/shard_map/sub | solution.py:105
  9.4 3.1 %collective-permute-start.5 = (f32[2,6,128]{2,0,1:T(2,128)}, f32[2,6,128]{2,0,1:T(2,128)}, u32[]{:S(2)}, u32[]{:S(2)}) collective-permute-start(f32[2,6,128]{2,0,1:T(2,128)} %bitcast_subtract_fusion), channel_id=1, source_target_pairs={{0,1},{1,0},{2,3},{3,2},{4,5},{5,4},{6,7},{7,6},{8,9},{9,8},{10,11... | collective-permute-start | bytes 18440 | tf_op jit(solution)/shard_map/ppermute | solution.py:56
  12.5 2.6 %collective-permute-start.6 = (f32[2,6,128]{2,0,1:T(2,128)}, f32[2,6,128]{2,0,1:T(2,128)}, u32[]{:S(2)}, u32[]{:S(2)}) collective-permute-start(f32[2,6,128]{2,0,1:T(2,128)} %bitcast_subtract_fusion), channel_id=1, source_target_pairs={{0,2},{1,3},{2,0},{3,1},{4,6},{5,7},{6,4},{7,5},{8,10},{9,11},{10,... | collective-permute-start | bytes 18440 | tf_op jit(solution)/shard_map/ppermute | solution.py:56
  15.0 1.3 %collective-permute-start = (bf16[2,384,384]{2,1,0:T(8,128)(2,1)S(1)}, bf16[2,384,384]{2,1,0:T(8,128)(2,1)S(1)}, u32[]{:S(2)}, u32[]{:S(2)}) collective-permute-start(bf16[2,384,384]{2,1,0:T(8,128)(2,1)S(1)} %bitcast.216), channel_id=1, source_target_pairs={{0,4},{4,8},{8,12},{1,5},{5,9},{9,13},{2,6},{6,10},{10,14},{3,7},{... | collective-permute-start | bytes 1769480 | tf_op jit(solution)/shard_map/ppermute | solution.py:148
  16.4 1.3 %collective-permute-start.1 = (bf16[2,384,384]{2,1,0:T(8,128)(2,1)S(1)}, bf16[2,384,384]{2,1,0:T(8,128)(2,1)S(1)}, u32[]{:S(2)}, u32[]{:S(2)}) collective-permute-start(bf16[2,384,384]{2,1,0:T(8,128)(2,1)S(1)} %bitcast.217), channel_id=1, source_target_pairs={{4,0},{8,4},{12,8},{5,1},{9,5},{13,9},{6,2},{10,6},{14,10},{7,3},{... | collective-permute-start | bytes 1769480 | tf_op jit(solution)/shard_map/ppermute | solution.py:149
  17.7 0.8 %bitcast_convert_fusion = f32[6,128,128]{2,1,0:T(8,128)} fusion(bf16[1,6,128,128]{3,1,2,0:T(8,128)(2,1)S(1)} %fusion.28), kind=kLoop, calls=%fused_computation.100 | loop fusion | flops 98304 | bytes 589824 | tf_op jit(solution)/shard_map/convert_element_type | solution.py:110
  18.5 1.1 %fusion.24 = bf16[2,96,6,128,1,1]{3,1,2,0,5,4:T(8,128)(2,1)} fusion(s32[6,128]{1,0:T(8,128)S(1)} %iota_add_fusion, bf16[2,384,384]{2,1,0:T(8,128)(2,1)S(1)} %copy-done.2, s32[]{:T(128)S(6)} %select_n.13), kind=kOutput, calls=%fused_computation.33 | convolution fusion | flops 113688576 | bytes 446468 | tf_op jit(solution)/shard_map/aij,gjr->aigr/dot_general | solution.py:115
  19.6 0.8 %dynamic-slice_bitcast_fusion.2 = (bf16[2,96,384]{2,1,0:T(8,128)(2,1)}, bf16[2,96,384]{2,1,0:T(8,128)(2,1)}, bf16[2,96,384]{2,1,0:T(8,128)(2,1)}) fusion(bf16[1,2,384,384]{3,2,1,0:T(8,128)(2,1)S(1)} %copy-done.1, s32[]{:T(128)S(6)} %select_n.14, s32[]{:T(128)S(6)} %select_n.15, s32[]{:T(128)S(6)} %select_n.16), kind=kLoop, calls=%fused_computation.108 | loop fusion | bytes 884748 | tf_op jit(solution)/shard_map/dynamic_slice | solution.py:63
  20.4 3.9 %collective-permute-start.4 = (bf16[2,96,384]{2,1,0:T(8,128)(2,1)}, bf16[2,96,384]{2,1,0:T(8,128)(2,1)}, u32[]{:S(2)}, u32[]{:S(2)}) collective-permute-start(bf16[2,96,384]{2,1,0:T(8,128)(2,1)} %get-tuple-element.17), channel_id=1, source_target_pairs={{0,3},{1,2},{2,1},{3,0},{4,7},{5,6},{6,5},{7,4},{8,11},{9,10},{10,... | collective-permute-start | bytes 442376 | tf_op jit(solution)/shard_map/ppermute | solution.py:56
  24.3 0.6 %collective-permute-start.3 = (bf16[2,96,384]{2,1,0:T(8,128)(2,1)}, bf16[2,96,384]{2,1,0:T(8,128)(2,1)}, u32[]{:S(2)}, u32[]{:S(2)}) collective-permute-start(bf16[2,96,384]{2,1,0:T(8,128)(2,1)} %get-tuple-element.16), channel_id=1, source_target_pairs={{0,2},{1,3},{2,0},{3,1},{4,6},{5,7},{6,4},{7,5},{8,10},{9,11},{10,... | collective-permute-start | bytes 442376 | tf_op jit(solution)/shard_map/ppermute | solution.py:56
  24.9 0.7 %pad_maximum_fusion.2 = f32[4,2,6,128]{3,1,2,0:T(2,128)S(1)} fusion(f32[1,2,6,128]{3,1,2,0:T(2,128)} %bitcast.38, f32[1,2,6,128]{3,1,2,0:T(2,128)} %bitcast.37, f32[1,2,6,128]{3,1,2,0:T(2,128)} %bitcast.36, f32[1,2,6,128]{3,1,2,0:T(2,128)S(1)} %bitcast_subtract_fusion.1), kind=kLoop, calls=%fused_computation.112 | loop fusion | flops 18432 | bytes 49152 | tf_op jit(solution)/shard_map/stack | solution.py:182
  25.7 4.7 %fusion.6 = f32[2,2,4,96,384]{4,3,0,1,2:T(8,128)} fusion(bf16[2,96,6,128,1,1]{3,1,2,0,5,4:T(8,128)(2,1)} %fusion.24, f32[4,2,6,128]{3,2,1,0:T(8,128)S(1)} %copy.14, f32[6,128,128]{2,1,0:T(8,128)S(1)} %copy-done.7, bf16[6,128,384]{2,1,0:T(8,128)(2,1)S(1)} %convolution_convert_fusion.3), kind=kOutput, calls=%fused_computation.9 | convolution fusion | flops 1513881600 | bytes 3661824 | tf_op jit(solution)/shard_map/aigr,cbgrk->abcik/dot_general | solution.py:118
  30.4 1.4 %fusion.65 = bf16[1,4,96,384]{3,2,1,0:T(8,128)(2,1)S(1)} fusion(f32[2,2,4,96,384]{4,3,0,1,2:T(8,128)} %fusion.6), kind=kLoop, calls=%fused_computation.95 | loop fusion | flops 442368 | bytes 1474560 | tf_op jit(solution)/shard_map/add | solution.py:43
  31.8 1.3 %fusion.66 = bf16[1,4,96,384]{3,2,1,0:T(8,128)(2,1)S(1)} fusion(f32[2,2,4,96,384]{4,3,0,1,2:T(8,128)} %fusion.6), kind=kLoop, calls=%fused_computation.96 | loop fusion | flops 442368 | bytes 1474560 | tf_op jit(solution)/shard_map/sub | solution.py:44
  33.1 0.8 %convolution_bitcast_fusion = f32[2,2,4,96,384]{4,3,2,1,0:T(8,128)S(1)} fusion(bf16[2,384,384,1,1]{2,1,4,3,0:T(8,128)(2,1)S(1)} %copy-done.3, bf16[1,4,96,384]{3,2,1,0:T(8,128)(2,1)S(1)} %fusion.66, bf16[1,4,96,384]{3,2,1,0:T(8,128)(2,1)S(1)} %fusion.65), kind=kOutput, calls=%fused_computation.10 | convolution fusion | flops 454164480 | bytes 3538944 | tf_op jit(solution)/shard_map/bcij,ajk->abcik/dot_general | solution.py:120
  33.9 2.7 %collective-permute-done.3 = bf16[2,96,384]{2,1,0:T(8,128)(2,1)} collective-permute-done((bf16[2,96,384]{2,1,0:T(8,128)(2,1)}, bf16[2,96,384]{2,1,0:T(8,128)(2,1)}, u32[]{:S(2)}, u32[]{:S(2)}) %collective-permute-start.3) | collective-permute-done | bytes 147488 | tf_op jit(solution)/shard_map/ppermute | solution.py:56
  36.6 1.2 %maximum_convert_fusion = f32[4,2,96,384]{3,2,0,1:T(8,128)S(1)} fusion(bf16[1,2,96,384]{3,2,0,1:T(8,128)(2,1)} %bitcast.10, bf16[1,2,96,384]{3,2,0,1:T(8,128)(2,1)} %bitcast.8, bf16[1,2,96,384]{3,2,0,1:T(8,128)(2,1)} %bitcast.6, bf16[1,2,96,384]{3,2,0,1:T(8,128)(2,1)S(1)} %constant_dynamic-slice_fusion), kind=kLoop, calls=%fused_computation.72 | loop fusion | flops 1179648 | bytes 1769472 | tf_op jit(solution)/shard_map/convert_element_type | solution.py:122
  38.3 0.4 fusion.44
  38.7 0.5 subtract_bitcast_fusion
  39.2 16.9 %all_gather.3 = bf16[2,384,384]{2,1,0:T(8,128)(2,1)S(1)} all-gather(bf16[2,96,384]{2,1,0:T(8,128)(2,1)S(1)} %pad_maximum_fusion.1), channel_id=1, replica_groups=mesh['grp'=2,'frame'=4,'coil'=4] {'coil'}, dimensions={1}, use_global_device_ids=true | all-gather | bytes 737280 | tf_op jit(solution)/shard_map/all_gather | solution.py:189
  56.1 1.3 %fusion.20 = f32[1,2,384,384]{3,2,1,0:T(8,128)} fusion(f32[1,2,384,384]{3,2,1,0:T(8,128)S(1)} %subtract_bitcast_fusion, bf16[1,2,384,384]{3,2,1,0:T(8,128)(2,1)S(1)} %copy-done, bf16[2,384,384]{2,1,0:T(8,128)(2,1)S(1)} %all_gather.3), kind=kLoop, calls=%fused_computation.25 | loop fusion | flops 1474560 | bytes 3538944 | tf_op jit(solution)/shard_map/sub | solution.py:190
  (45 shorter events, 1.6 us)
Async XLA Ops:
  0.0 1.2 %copy-start.1 = (bf16[1,2,384,384]{3,2,1,0:T(8,128)(2,1)S(1)}, bf16[1,2,384,384]{3,2,1,0:T(8,128)(2,1)}, u32[]{:S(2)}) copy-start(bf16[1,2,384,384]{3,2,1,0:T(8,128)(2,1)} %param.10) | copy-start | bytes 1769476
  1.3 1.1 %copy-start.4 = (bf16[2,384,384,1]{2,1,0,3:T(8,128)(2,1)S(1)}, bf16[2,384,384,1]{2,1,0,3:T(8,128)(2,1)}, u32[]{:S(2)}) copy-start(bf16[2,384,384,1]{2,1,0,3:T(8,128)(2,1)} %constant.40) | copy-start | bytes 1769476
  3.2 1.1 %copy-start.2 = (bf16[2,384,384]{2,1,0:T(8,128)(2,1)S(1)}, bf16[2,384,384]{2,1,0:T(8,128)(2,1)}, u32[]{:S(2)}) copy-start(bf16[2,384,384]{2,1,0:T(8,128)(2,1)} %constant.33.clone) | copy-start | bytes 1769476
  4.2 0.7 %copy-start.10 = (s32[1,6]{1,0:T(1,128)S(1)}, s32[1,6]{1,0:T(1,128)}, u32[]{:S(2)}) copy-start(s32[1,6]{1,0:T(1,128)} %param.13) | copy-start | bytes 76
  4.2 1.1 %copy-start.5 = (bf16[16,128,128]{2,1,0:T(8,128)(2,1)S(1)}, bf16[16,128,128]{2,1,0:T(8,128)(2,1)}, u32[]{:S(2)}) copy-start(bf16[16,128,128]{2,1,0:T(8,128)(2,1)} %param.15) | copy-start | bytes 1572868
  4.2 1.1 %copy-start.9 = (s32[1,6]{1,0:T(1,128)S(1)}, s32[1,6]{1,0:T(1,128)}, u32[]{:S(2)}) copy-start(s32[1,6]{1,0:T(1,128)} %param.12) | copy-start | bytes 76
  4.2 1.5 %copy-start.6 = (bf16[16,128,128]{2,1,0:T(8,128)(2,1)S(1)}, bf16[16,128,128]{2,1,0:T(8,128)(2,1)}, u32[]{:S(2)}) copy-start(bf16[16,128,128]{2,1,0:T(8,128)(2,1)} %param.16) | copy-start | bytes 1572868
  4.3 1.8 %copy-start.11 = (s32[1,6]{1,0:T(1,128)S(1)}, s32[1,6]{1,0:T(1,128)}, u32[]{:S(2)}) copy-start(s32[1,6]{1,0:T(1,128)} %param.14) | copy-start | bytes 76
  7.9 0.9 %copy-start.8 = (f32[1,1,2,6,128]{4,2,3,1,0:T(2,128)S(1)}, f32[1,1,2,6,128]{4,2,3,1,0:T(2,128)}, u32[]{:S(2)}) copy-start(f32[1,1,2,6,128]{4,2,3,1,0:T(2,128)} %param.11) | copy-start | bytes 18436
  7.9 7.2 %copy-start = (bf16[1,2,384,384]{3,2,1,0:T(8,128)(2,1)S(1)}, bf16[1,2,384,384]{3,2,1,0:T(8,128)(2,1)}, u32[]{:S(2)}) copy-start(bf16[1,2,384,384]{3,2,1,0:T(8,128)(2,1)} %param.9) | copy-start | bytes 1769476
  9.4 11.0 %collective-permute-start.5 = (f32[2,6,128]{2,0,1:T(2,128)}, f32[2,6,128]{2,0,1:T(2,128)}, u32[]{:S(2)}, u32[]{:S(2)}) collective-permute-start(f32[2,6,128]{2,0,1:T(2,128)} %bitcast_subtract_fusion), channel_id=1, source_target_pairs={{0,1},{1,0},{2,3},{3,2},{4,5},{5,4},{6,7},{7,6},{8,9},{9,8},{10,11... | collective-permute-start | bytes 18440 | tf_op jit(solution)/shard_map/ppermute | solution.py:56
  12.5 11.8 %collective-permute-start.6 = (f32[2,6,128]{2,0,1:T(2,128)}, f32[2,6,128]{2,0,1:T(2,128)}, u32[]{:S(2)}, u32[]{:S(2)}) collective-permute-start(f32[2,6,128]{2,0,1:T(2,128)} %bitcast_subtract_fusion), channel_id=1, source_target_pairs={{0,2},{1,3},{2,0},{3,1},{4,6},{5,7},{6,4},{7,5},{8,10},{9,11},{10,... | collective-permute-start | bytes 18440 | tf_op jit(solution)/shard_map/ppermute | solution.py:56
  15.0 9.2 %collective-permute-start.7 = (f32[2,6,128]{2,0,1:T(2,128)}, f32[2,6,128]{2,0,1:T(2,128)}, u32[]{:S(2)}, u32[]{:S(2)}) collective-permute-start(f32[2,6,128]{2,0,1:T(2,128)} %bitcast_subtract_fusion), channel_id=1, source_target_pairs={{0,3},{1,2},{2,1},{3,0},{4,7},{5,6},{6,5},{7,4},{8,11},{9,10},{10,... | collective-permute-start | bytes 18440 | tf_op jit(solution)/shard_map/ppermute | solution.py:56
  15.0 23.0 %collective-permute-start = (bf16[2,384,384]{2,1,0:T(8,128)(2,1)S(1)}, bf16[2,384,384]{2,1,0:T(8,128)(2,1)S(1)}, u32[]{:S(2)}, u32[]{:S(2)}) collective-permute-start(bf16[2,384,384]{2,1,0:T(8,128)(2,1)S(1)} %bitcast.216), channel_id=1, source_target_pairs={{0,4},{4,8},{8,12},{1,5},{5,9},{9,13},{2,6},{6,10},{10,14},{3,7},{... | collective-permute-start | bytes 1769480 | tf_op jit(solution)/shard_map/ppermute | solution.py:148
  16.4 21.7 %collective-permute-start.1 = (bf16[2,384,384]{2,1,0:T(8,128)(2,1)S(1)}, bf16[2,384,384]{2,1,0:T(8,128)(2,1)S(1)}, u32[]{:S(2)}, u32[]{:S(2)}) collective-permute-start(bf16[2,384,384]{2,1,0:T(8,128)(2,1)S(1)} %bitcast.217), channel_id=1, source_target_pairs={{4,0},{8,4},{12,8},{5,1},{9,5},{13,9},{6,2},{10,6},{14,10},{7,3},{... | collective-permute-start | bytes 1769480 | tf_op jit(solution)/shard_map/ppermute | solution.py:149
  19.6 6.1 %copy-start.7 = (f32[6,128,128]{2,1,0:T(8,128)S(1)}, f32[6,128,128]{2,1,0:T(8,128)}, u32[]{:S(2)}) copy-start(f32[6,128,128]{2,1,0:T(8,128)} %bitcast_convert_fusion) | copy-start | bytes 1179652
  20.4 13.5 %collective-permute-start.4 = (bf16[2,96,384]{2,1,0:T(8,128)(2,1)}, bf16[2,96,384]{2,1,0:T(8,128)(2,1)}, u32[]{:S(2)}, u32[]{:S(2)}) collective-permute-start(bf16[2,96,384]{2,1,0:T(8,128)(2,1)} %get-tuple-element.17), channel_id=1, source_target_pairs={{0,3},{1,2},{2,1},{3,0},{4,7},{5,6},{6,5},{7,4},{8,11},{9,10},{10,... | collective-permute-start | bytes 442376 | tf_op jit(solution)/shard_map/ppermute | solution.py:56
  24.3 9.6 %collective-permute-start.2 = (bf16[2,96,384]{2,1,0:T(8,128)(2,1)}, bf16[2,96,384]{2,1,0:T(8,128)(2,1)}, u32[]{:S(2)}, u32[]{:S(2)}) collective-permute-start(bf16[2,96,384]{2,1,0:T(8,128)(2,1)} %get-tuple-element.15), channel_id=1, source_target_pairs={{0,1},{1,0},{2,3},{3,2},{4,5},{5,4},{6,7},{7,6},{8,9},{9,8},{10,11... | collective-permute-start | bytes 442376 | tf_op jit(solution)/shard_map/ppermute | solution.py:56
  24.3 12.3 %collective-permute-start.3 = (bf16[2,96,384]{2,1,0:T(8,128)(2,1)}, bf16[2,96,384]{2,1,0:T(8,128)(2,1)}, u32[]{:S(2)}, u32[]{:S(2)}) collective-permute-start(bf16[2,96,384]{2,1,0:T(8,128)(2,1)} %get-tuple-element.16), channel_id=1, source_target_pairs={{0,2},{1,3},{2,0},{3,1},{4,6},{5,7},{6,4},{7,5},{8,10},{9,11},{10,... | collective-permute-start | bytes 442376 | tf_op jit(solution)/shard_map/ppermute | solution.py:56
  30.4 2.7 %copy-start.3 = (bf16[2,384,384,1,1]{2,1,4,3,0:T(8,128)(2,1)S(1)}, bf16[2,384,384,1,1]{2,1,4,3,0:T(8,128)(2,1)}, u32[]{:S(2)}) copy-start(bf16[2,384,384,1,1]{2,1,4,3,0:T(8,128)(2,1)} %constant.41) | copy-start | bytes 1769476

commit v5 on v0

--- a/solution.py
+++ b/solution.py
@@ -35,8 +35,11 @@
     phases = (indices[:, None] * indices[None, :] % extent).astype(np.float32)
     angle_values = np.float32(2.0 * math.pi / extent) * phases
     scaling = np.float32(1.0 / math.sqrt(extent))
-    table = np.stack([np.cos(angle_values) * scaling, np.sin(angle_values) * scaling])
-    return jnp.asarray(table.astype(ml_dtypes.bfloat16))
+    cos_t = (np.cos(angle_values) * scaling).astype(ml_dtypes.bfloat16)
+    sin_t = (np.sin(angle_values) * scaling).astype(ml_dtypes.bfloat16)
+    block = np.block([[cos_t, sin_t], [-sin_t, cos_t]])
+    block = lax.optimization_barrier(jnp.asarray(block))
+    return jnp.stack([block[:extent, :extent], block[:extent, extent:]]), block
 
 
 def combine_parts(products, direction):
@@ -72,7 +75,7 @@
     return picked.astype(kernels.dtype).reshape((angle_ids.shape[0],) + kernels.shape[1:])
 
 
-def forward_residual(transform, frame_image, coil_map, measured, row_placed, col_placed):
+def forward_residual(transform, block, frame_image, coil_map, measured, row_placed, col_placed):
     map_planes = coil_map.astype(jnp.float32)
     image_planes = frame_image.astype(jnp.float32)
     coil_image = jnp.stack(
@@ -85,10 +88,12 @@
         "bij,ajk->abik", coil_image, transform, preferred_element_type=jnp.float32
     )
     half_done = combine_parts(products, 1.0).astype(jnp.bfloat16)
-    products = jnp.einsum("aij,bjk->abik", transform, half_done, preferred_element_type=jnp.float32)
-    kspace = combine_parts(products, 1.0).astype(jnp.bfloat16)
+    extent = transform.shape[-1]
+    kspace = jnp.dot(
+        block, half_done.reshape(2 * extent, extent), preferred_element_type=jnp.float32
+    ).astype(jnp.bfloat16).reshape(2, extent, extent)
     contracted = jnp.einsum("pik,gjk->pgij", kspace, col_placed, preferred_element_type=jnp.float32)
-    predicted = jnp.sum(contracted * row_placed.astype(jnp.float32)[None], axis=2)
+    predicted = jnp.sum(contracted * row_placed[None], axis=2)
     return predicted - measured
 
 
@@ -136,7 +141,9 @@
     later = lax.ppermute(image, "frame", [(i + 1, i) for i in range(count - 1)])
     has_earlier = (frame_index >= 1).astype(jnp.float32)
     has_later = (frame_index <= frame_total - 2).astype(jnp.float32)
-    return (normed_change(image, earlier, has_earlier) - normed_change(later, image, has_later))[None]
+    return (
+        normed_change(image, earlier, has_earlier) - normed_change(later, image, has_later)
+    )[None]
 
 
 def body(
@@ -148,7 +155,7 @@
     coil_count = lax.axis_size("coil")
     coil_index = lax.axis_index("coil")
     rows = extent // coil_count
-    transform = transform_table(extent)
+    transform, block = transform_table(extent)
     map_rows = exchange_rows(coil_maps[0], rows, coil_count, coil_index)
     first_frame = lax.axis_index("frame") * frame_count
     frame_total = lax.axis_size("frame") * frame_count
@@ -162,13 +169,12 @@
     col_select = selector(band_col[0], extent, patch_side)
     exact = dict(preferred_element_type=jnp.float32)
     col_placed = jnp.einsum("gjq,gkq->gjk", col_w, col_select, **exact).astype(jnp.bfloat16)
-    row_placed = jnp.einsum("grj,gir->gij", row_w, row_select, **exact).astype(jnp.bfloat16)
+    row_placed = jnp.einsum("grj,gir->gij", row_w, row_select, **exact)
     residual = forward_residual(
-        transform, images[0], coil_maps[0], kspace_data[0, 0], row_placed, col_placed
+        transform, block, images[0], coil_maps[0], kspace_data[0, 0], row_placed, col_placed
     )
-    residuals = jnp.stack(
-        [residual] + [rotated(residual, coil_count, shift) for shift in range(1, coil_count)]
-    )
+    moved = [rotated(residual, coil_count, shift) for shift in range(1, coil_count)]
+    residuals = jnp.stack([residual] + moved)
     grad_rows = backward_rows(
         transform, residuals, map_rows, row_select, row_w, col_placed, coil_index
     )

time: 59.8 us -> 58.8 us (0.983)
  other arithmetic: 9.84 us -> 7.1 us
  local copies, waits for them, and re-layouts: 3.69 us -> 5.18 us
    unnamed x26 -> x18, local copies, waits for them, and re-layouts: 1.51 us -> 2.9 us
    convert_element_type x1 -> x0, local copies, waits for them, and re-layouts: 1.38 us -> none  [forward_residual(): row_placed.astype(jnp.float32)[None]]
    another operation x1 -> x2, local copies, waits for them, and re-layouts: 0.01 us -> 1.18 us  [the longest x1 1.17 us: transform_table(): jnp.stack([block[:extent, :extent], block[:extent, extent:]])]
    convert_element_type x1, other arithmetic: 1.2 us -> 0.08 us  [normed_change(): change = later.astype(jnp.float32) - earlier.astype(jnp.float32)]
    dot_general x2, matrix products: 0.79 us -> 1.84 us  [pick_kernels(): jnp.dot(choice.astype(kernels.dtype), flat, preferred_element_type=jnp.fl...]
    dot_general x1, matrix products: 2.06 us -> 1.11 us  [backward_rows(): jnp.einsum('aij,gjr->aigr', row_table, row_select, preferred_element_type...]
    sub x3 -> x1, other arithmetic: 2.14 us -> 1.31 us  [combine_parts(): imaginary = products[0, 1] - direction * products[1, 0]]
    convert_element_type x1, other arithmetic: 0.77 us -> 0.03 us  [backward_rows(): row_w.astype(jnp.float32)[None, None] * residuals[:, :, :, None, :]]
  transfers between devices with their start and end apart: 8 -> 8, of which waited for: 1 -> 1; matrix products, arithmetic and copies ran while one was open for 22% -> 20% of each run, Pallas kernels for 0% -> 0%
where the time goes in v5:
time: 58.8 us; the launch traced here: 58.4 us
  blocking collectives  16.7 us (28%)
  starting transfers between devices  11.9 us (20%)
  matrix products  11.8 us (20%)
  other arithmetic  7.1 us (12%)
  waiting for transfers between devices  5.38 us (9%)
  local copies, waits for them, and re-layouts  5.18 us (9%)
    all_gather x1, blocking collectives, body(): lax.all_gather(grad_rows, 'coil', axis=1, tiled=True).astype(jnp.float32)  16.7 us
    ppermute x6, starting transfers between devices, rotated(): lax.ppermute(block, 'coil', [(i, (i + shift) % coil_count) for i in range...  9.32 us
    ppermute x6, waiting for transfers between devices, rotated(): lax.ppermute(block, 'coil', [(i, (i + shift) % coil_count) for i in range...  5.37 us
    dot_general x1, matrix products, backward_rows(): jnp.einsum('aigr,cbgrk->abcik', table_at, placed, preferred_element_type=...  4.89 us
    unnamed x18, local copies, waits for them, and re-layouts  2.9 us
    dot_general x2, matrix products, pick_kernels(): jnp.dot(choice.astype(kernels.dtype), flat, preferred_element_type=jnp.fl...  1.84 us
    add x2, other arithmetic, combine_parts(): real_part = products[0, 0] + direction * products[1, 1]  1.43 us
    sub x1, other arithmetic, combine_parts(): imaginary = products[0, 1] - direction * products[1, 0]  1.31 us
  transfers between devices with their start and end apart: 8, of which 1 were waited for; matrix products, arithmetic and copies ran while one was open for 20% of the time, Pallas kernels for 0%

profile of v5, /device:TPU:0, one launch (start us, length us, event | category | flops | bytes accessed | tf_op | source)
XLA Modules:
  0.0 58.4 jit_solution(15721717276831440180)
XLA Ops:
  0.0 1.2 %slice_bitcast_fusion.6 = (bf16[1,384,384]{2,1,0:T(8,128)(2,1)S(1)}, bf16[1,384,384]{2,1,0:T(8,128)(2,1)S(1)}) fusion(bf16[768,768]{1,0:T(8,128)(2,1)} %constant.52.clone), kind=kLoop, calls=%fused_computation.94 | loop fusion | bytes 1179648 | tf_op jit(solution)/shard_map/stack | solution.py:42
  1.3 1.0 %copy-done.1 = bf16[1,2,384,384]{3,2,1,0:T(8,128)(2,1)S(1)} copy-done((bf16[1,2,384,384]{3,2,1,0:T(8,128)(2,1)S(1)}, bf16[1,2,384,384]{3,2,1,0:T(8,128)(2,1)}, u32[]{:S(2)}) %copy-start.1) | copy-done | bytes 589848
  2.6 0.8 %convolution_bitcast_fusion.1 = f32[2,2,384,384]{3,2,1,0:T(8,128)S(1)} fusion(bf16[1,384,384]{2,1,0:T(8,128)(2,1)S(1)} %get-tuple-element.14, bf16[1,384,384]{2,1,0:T(8,128)(2,1)S(1)} %get-tuple-element.13, bf16[1,384,384]{2,1,0:T(8,128)(2,1)S(1)} %get-tuple-element.15, bf16[1,384,384]{2,1,0:T(8,128)(2,1)S(1)} %get-tuple-element.16), kind=kOutput, calls=%fused_computation.11 | convolution fusion | flops 455344128 | bytes 3538944 | tf_op jit(solution)/shard_map/bij,ajk->abik/dot_general | solution.py:87
  3.6 1.2 %copy-done.4 = bf16[768,768]{1,0:T(8,128)(2,1)S(1)} copy-done((bf16[768,768]{1,0:T(8,128)(2,1)S(1)}, bf16[768,768]{1,0:T(8,128)(2,1)}, u32[]{:S(2)}) %copy-start.4) | copy-done | bytes 1179672
  4.7 0.7 %fusion.13 = bf16[768,384]{0,1:T(8,128)(2,1)S(1)} fusion(bf16[768,384]{1,0:T(8,128)(2,1)S(1)} %bitcast.209, bf16[768,768]{1,0:T(8,128)(2,1)S(1)} %copy-done.4), kind=kOutput, calls=%fused_computation.16 | convolution fusion | flops 453279744 | bytes 2359296 | tf_op jit(solution)/shard_map/dot_general | solution.py:92
  5.5 0.3 copy.26
  5.8 0.3 copy-done.7
  6.1 0.3 copy-done.3
  6.5 0.4 fusion.22
  6.9 1.4 %fusion.21 = bf16[1,6,128,128]{3,1,2,0:T(8,128)(2,1)S(1)} fusion(bf16[2,8,128,128]{3,2,1,0:T(8,128)(2,1)} %bitcast.211, s32[6]{0:T(128)S(1)} %bitcast.218), kind=kOutput, calls=%fused_computation.28 | convolution fusion | flops 3244128 | bytes 720920 | tf_op jit(solution)/shard_map/dot_general | solution.py:74
  8.4 0.4 fusion.16
  8.8 0.4 convolution_convert_fusion.3
  9.3 0.9 %fusion.5 = f32[2,6,128]{2,0,1:T(2,128)S(1)} fusion(bf16[2,384,384,1]{2,1,0,3:T(8,128)(2,1)S(1)} %bitcast.208, f32[6,384,128]{1,2,0:T(8,128)S(1)} %fusion.16, bf16[6,128,384]{2,1,0:T(8,128)(2,1)S(1)} %convolution_convert_fusion.3), kind=kOutput, calls=%fused_computation.8 | convolution fusion | flops 454162944 | bytes 2365440 | tf_op jit(solution)/shard_map/pik,gjk->pgij/dot_general | solution.py:95
  10.2 3.1 %collective-permute-start.5 = (f32[2,6,128]{2,0,1:T(2,128)S(1)}, f32[2,6,128]{2,0,1:T(2,128)S(1)}, u32[]{:S(2)}, u32[]{:S(2)}) collective-permute-start(f32[2,6,128]{2,0,1:T(2,128)S(1)} %bitcast_subtract_fusion), channel_id=1, source_target_pairs={{0,1},{1,2},{2,3},{3,0},{4,5},{5,6},{6,7},{7,4},{8,9},{9,10},{10,1... | collective-permute-start | bytes 18440 | tf_op jit(solution)/shard_map/ppermute | solution.py:52
  13.3 2.6 %collective-permute-start.6 = (f32[2,6,128]{2,0,1:T(2,128)S(1)}, f32[2,6,128]{2,0,1:T(2,128)S(1)}, u32[]{:S(2)}, u32[]{:S(2)}) collective-permute-start(f32[2,6,128]{2,0,1:T(2,128)S(1)} %bitcast_subtract_fusion), channel_id=1, source_target_pairs={{0,2},{1,3},{2,0},{3,1},{4,6},{5,7},{6,4},{7,5},{8,10},{9,11},{10,... | collective-permute-start | bytes 18440 | tf_op jit(solution)/shard_map/ppermute | solution.py:52
  15.9 1.3 %collective-permute-start.7 = (f32[2,6,128]{2,0,1:T(2,128)S(1)}, f32[2,6,128]{2,0,1:T(2,128)S(1)}, u32[]{:S(2)}, u32[]{:S(2)}) collective-permute-start(f32[2,6,128]{2,0,1:T(2,128)S(1)} %bitcast_subtract_fusion), channel_id=1, source_target_pairs={{0,3},{1,0},{2,1},{3,2},{4,7},{5,4},{6,5},{7,6},{8,11},{9,8},{10,9... | collective-permute-start | bytes 18440 | tf_op jit(solution)/shard_map/ppermute | solution.py:52
  17.2 1.3 %collective-permute-start = (bf16[2,384,384]{2,1,0:T(8,128)(2,1)S(1)}, bf16[2,384,384]{2,1,0:T(8,128)(2,1)S(1)}, u32[]{:S(2)}, u32[]{:S(2)}) collective-permute-start(bf16[2,384,384]{2,1,0:T(8,128)(2,1)S(1)} %bitcast.205), channel_id=1, source_target_pairs={{0,4},{4,8},{8,12},{1,5},{5,9},{9,13},{2,6},{6,10},{10,14},{3,7},{... | collective-permute-start | bytes 1769480 | tf_op jit(solution)/shard_map/ppermute | solution.py:140
  18.5 1.3 %collective-permute-start.1 = (bf16[2,384,384]{2,1,0:T(8,128)(2,1)S(1)}, bf16[2,384,384]{2,1,0:T(8,128)(2,1)S(1)}, u32[]{:S(2)}, u32[]{:S(2)}) collective-permute-start(bf16[2,384,384]{2,1,0:T(8,128)(2,1)S(1)} %bitcast.206), channel_id=1, source_target_pairs={{4,0},{8,4},{12,8},{5,1},{9,5},{13,9},{6,2},{10,6},{14,10},{7,3},{... | collective-permute-start | bytes 1769480 | tf_op jit(solution)/shard_map/ppermute | solution.py:141
  19.9 1.1 %fusion.18 = bf16[2,96,6,128,1,1]{3,1,2,0,5,4:T(8,128)(2,1)} fusion(s32[6,128]{1,0:T(8,128)S(1)} %iota_add_fusion, s32[]{:T(128)S(6)} %select_n.28, bf16[1,384,384]{2,1,0:T(8,128)(2,1)S(1)} %get-tuple-element.16, bf16[1,384,384]{2,1,0:T(8,128)(2,1)S(1)} %get-tuple-element.15), kind=kOutput, calls=%fused_computation.27 | convolution fusion | flops 113983488 | bytes 887812 | tf_op jit(solution)/shard_map/aij,gjr->aigr/dot_general | solution.py:107
  21.1 0.8 %dynamic-slice_bitcast_fusion.2 = (bf16[2,96,384]{2,1,0:T(8,128)(2,1)}, bf16[2,96,384]{2,1,0:T(8,128)(2,1)}, bf16[2,96,384]{2,1,0:T(8,128)(2,1)}) fusion(bf16[1,2,384,384]{3,2,1,0:T(8,128)(2,1)S(1)} %copy-done.1, s32[]{:T(128)S(6)} %select_n.30, s32[]{:T(128)S(6)} %select_n.32, s32[]{:T(128)S(6)} %select_n.34), kind=kLoop, calls=%fused_computation.105 | loop fusion | bytes 884748 | tf_op jit(solution)/shard_map/dynamic_slice | solution.py:59
  21.9 0.5 collective-permute-start.4
  22.4 1.6 %collective-permute-start.2 = (bf16[2,96,384]{2,1,0:T(8,128)(2,1)}, bf16[2,96,384]{2,1,0:T(8,128)(2,1)}, u32[]{:S(2)}, u32[]{:S(2)}) collective-permute-start(bf16[2,96,384]{2,1,0:T(8,128)(2,1)} %get-tuple-element.17), channel_id=1, source_target_pairs={{0,1},{1,2},{2,3},{3,0},{4,5},{5,6},{6,7},{7,4},{8,9},{9,10},{10,1... | collective-permute-start | bytes 442376 | tf_op jit(solution)/shard_map/ppermute | solution.py:52
  24.2 4.9 %fusion.6 = f32[2,2,4,96,384]{4,3,0,1,2:T(8,128)} fusion(bf16[2,96,6,128,1,1]{3,1,2,0,5,4:T(8,128)(2,1)} %fusion.18, f32[4,2,6,128]{3,2,1,0:T(8,128)S(1)} %copy.13, f32[6,128,128]{2,1,0:T(8,128)S(1)} %bitcast_convert_fusion, bf16[6,128,384]{2,1,0:T(8,128)(2,1)} %copy-done.2), kind=kOutput, calls=%fused_computation.9 | convolution fusion | flops 1513881600 | bytes 3661824 | tf_op jit(solution)/shard_map/aigr,cbgrk->abcik/dot_general | solution.py:110
  29.1 1.3 %fusion.60 = bf16[1,4,96,384]{3,2,1,0:T(8,128)(2,1)S(1)} fusion(f32[2,2,4,96,384]{4,3,0,1,2:T(8,128)} %fusion.6), kind=kLoop, calls=%fused_computation.92 | loop fusion | flops 442368 | bytes 1474560 | tf_op jit(solution)/shard_map/add | solution.py:46
  30.4 1.3 %fusion.61 = bf16[1,4,96,384]{3,2,1,0:T(8,128)(2,1)S(1)} fusion(f32[2,2,4,96,384]{4,3,0,1,2:T(8,128)} %fusion.6), kind=kLoop, calls=%fused_computation.93 | loop fusion | flops 442368 | bytes 1474560 | tf_op jit(solution)/shard_map/sub | solution.py:47
  31.7 0.8 %convolution_bitcast_fusion = f32[2,2,4,96,384]{4,3,2,1,0:T(8,128)S(1)} fusion(bf16[1,4,96,384]{3,2,1,0:T(8,128)(2,1)S(1)} %fusion.61, bf16[1,4,96,384]{3,2,1,0:T(8,128)(2,1)S(1)} %fusion.60, bf16[1,384,384]{2,1,0:T(8,128)(2,1)S(1)} %get-tuple-element.15, bf16[1,384,384]{2,1,0:T(8,128)(2,1)S(1)} %get-tuple-element.16), kind=kOutput, calls=%fused_computation.10 | convolution fusion | flops 455344128 | bytes 3538944 | tf_op jit(solution)/shard_map/bcij,ajk->abcik/dot_general | solution.py:112
  32.5 5.4 %collective-permute-done.3 = bf16[2,96,384]{2,1,0:T(8,128)(2,1)} collective-permute-done((bf16[2,96,384]{2,1,0:T(8,128)(2,1)}, bf16[2,96,384]{2,1,0:T(8,128)(2,1)}, u32[]{:S(2)}, u32[]{:S(2)}) %collective-permute-start.3) | collective-permute-done | bytes 147488 | tf_op jit(solution)/shard_map/ppermute | solution.py:52
  37.9 1.2 %maximum_convert_fusion = f32[4,2,96,384]{3,2,0,1:T(8,128)S(1)} fusion(bf16[1,2,96,384]{3,2,0,1:T(8,128)(2,1)} %bitcast.10, bf16[1,2,96,384]{3,2,0,1:T(8,128)(2,1)} %bitcast.8, bf16[1,2,96,384]{3,2,0,1:T(8,128)(2,1)} %bitcast.6, bf16[1,2,96,384]{3,2,0,1:T(8,128)(2,1)S(1)} %constant_dynamic-slice_fusion), kind=kLoop, calls=%fused_computation.67 | loop fusion | flops 1179648 | bytes 1769472 | tf_op jit(solution)/shard_map/convert_element_type | solution.py:114
  39.6 0.4 fusion.37
  40.0 0.5 subtract_bitcast_fusion
  40.5 16.7 %all_gather.3 = bf16[2,384,384]{2,1,0:T(8,128)(2,1)S(1)} all-gather(bf16[2,96,384]{2,1,0:T(8,128)(2,1)S(1)} %pad_maximum_fusion.4), channel_id=1, replica_groups=mesh['grp'=2,'frame'=4,'coil'=4] {'coil'}, dimensions={1}, use_global_device_ids=true | all-gather | bytes 737280 | tf_op jit(solution)/shard_map/all_gather | solution.py:182
  57.1 1.2 %fusion.14 = f32[1,2,384,384]{3,2,1,0:T(8,128)} fusion(f32[1,2,384,384]{3,2,1,0:T(8,128)S(1)} %subtract_bitcast_fusion, bf16[1,2,384,384]{3,2,1,0:T(8,128)(2,1)S(1)} %copy-done, bf16[2,384,384]{2,1,0:T(8,128)(2,1)S(1)} %all_gather.3), kind=kLoop, calls=%fused_computation.19 | loop fusion | flops 1474560 | bytes 3538944 | tf_op jit(solution)/shard_map/sub | solution.py:183
  (38 shorter events, 1.6 us)
Async XLA Ops:
  0.0 1.2 %copy-start = (bf16[1,2,384,384]{3,2,1,0:T(8,128)(2,1)S(1)}, bf16[1,2,384,384]{3,2,1,0:T(8,128)(2,1)}, u32[]{:S(2)}) copy-start(bf16[1,2,384,384]{3,2,1,0:T(8,128)(2,1)} %param.9) | copy-start | bytes 1769476
  1.2 1.1 %copy-start.1 = (bf16[1,2,384,384]{3,2,1,0:T(8,128)(2,1)S(1)}, bf16[1,2,384,384]{3,2,1,0:T(8,128)(2,1)}, u32[]{:S(2)}) copy-start(bf16[1,2,384,384]{3,2,1,0:T(8,128)(2,1)} %param.10) | copy-start | bytes 1769476
  3.5 1.3 %copy-start.4 = (bf16[768,768]{1,0:T(8,128)(2,1)S(1)}, bf16[768,768]{1,0:T(8,128)(2,1)}, u32[]{:S(2)}) copy-start(bf16[768,768]{1,0:T(8,128)(2,1)} %constant.52.clone) | copy-start | bytes 3538948
  5.4 0.7 %copy-start.7 = (s32[1,6]{1,0:T(1,128)S(1)}, s32[1,6]{1,0:T(1,128)}, u32[]{:S(2)}) copy-start(s32[1,6]{1,0:T(1,128)} %param.13) | copy-start | bytes 76
  5.4 1.0 %copy-start.3 = (bf16[16,128,128]{2,1,0:T(8,128)(2,1)S(1)}, bf16[16,128,128]{2,1,0:T(8,128)(2,1)}, u32[]{:S(2)}) copy-start(bf16[16,128,128]{2,1,0:T(8,128)(2,1)} %param.15) | copy-start | bytes 1572868
  5.4 1.0 %copy-start.6 = (s32[1,6]{1,0:T(1,128)S(1)}, s32[1,6]{1,0:T(1,128)}, u32[]{:S(2)}) copy-start(s32[1,6]{1,0:T(1,128)} %param.12) | copy-start | bytes 76
  5.5 2.9 %copy-start.8 = (s32[1,6]{1,0:T(1,128)S(1)}, s32[1,6]{1,0:T(1,128)}, u32[]{:S(2)}) copy-start(s32[1,6]{1,0:T(1,128)} %param.14) | copy-start | bytes 76
  9.2 0.9 %copy-start.2 = (bf16[6,128,384]{2,1,0:T(8,128)(2,1)}, bf16[6,128,384]{2,1,0:T(8,128)(2,1)S(1)}, u32[]{:S(2)}) copy-start(bf16[6,128,384]{2,1,0:T(8,128)(2,1)S(1)} %convolution_convert_fusion.3) | copy-start | bytes 1769476
  9.2 0.9 %copy-start.5 = (f32[1,1,2,6,128]{4,2,3,1,0:T(2,128)S(1)}, f32[1,1,2,6,128]{4,2,3,1,0:T(2,128)}, u32[]{:S(2)}) copy-start(f32[1,1,2,6,128]{4,2,3,1,0:T(2,128)} %param.11) | copy-start | bytes 18436
  10.2 11.7 %collective-permute-start.5 = (f32[2,6,128]{2,0,1:T(2,128)S(1)}, f32[2,6,128]{2,0,1:T(2,128)S(1)}, u32[]{:S(2)}, u32[]{:S(2)}) collective-permute-start(f32[2,6,128]{2,0,1:T(2,128)S(1)} %bitcast_subtract_fusion), channel_id=1, source_target_pairs={{0,1},{1,2},{2,3},{3,0},{4,5},{5,6},{6,7},{7,4},{8,9},{9,10},{10,1... | collective-permute-start | bytes 18440 | tf_op jit(solution)/shard_map/ppermute | solution.py:52
  13.3 9.1 %collective-permute-start.6 = (f32[2,6,128]{2,0,1:T(2,128)S(1)}, f32[2,6,128]{2,0,1:T(2,128)S(1)}, u32[]{:S(2)}, u32[]{:S(2)}) collective-permute-start(f32[2,6,128]{2,0,1:T(2,128)S(1)} %bitcast_subtract_fusion), channel_id=1, source_target_pairs={{0,2},{1,3},{2,0},{3,1},{4,6},{5,7},{6,4},{7,5},{8,10},{9,11},{10,... | collective-permute-start | bytes 18440 | tf_op jit(solution)/shard_map/ppermute | solution.py:52
  15.9 8.1 %collective-permute-start.7 = (f32[2,6,128]{2,0,1:T(2,128)S(1)}, f32[2,6,128]{2,0,1:T(2,128)S(1)}, u32[]{:S(2)}, u32[]{:S(2)}) collective-permute-start(f32[2,6,128]{2,0,1:T(2,128)S(1)} %bitcast_subtract_fusion), channel_id=1, source_target_pairs={{0,3},{1,0},{2,1},{3,2},{4,7},{5,4},{6,5},{7,6},{8,11},{9,8},{10,9... | collective-permute-start | bytes 18440 | tf_op jit(solution)/shard_map/ppermute | solution.py:52
  17.2 22.1 %collective-permute-start = (bf16[2,384,384]{2,1,0:T(8,128)(2,1)S(1)}, bf16[2,384,384]{2,1,0:T(8,128)(2,1)S(1)}, u32[]{:S(2)}, u32[]{:S(2)}) collective-permute-start(bf16[2,384,384]{2,1,0:T(8,128)(2,1)S(1)} %bitcast.205), channel_id=1, source_target_pairs={{0,4},{4,8},{8,12},{1,5},{5,9},{9,13},{2,6},{6,10},{10,14},{3,7},{... | collective-permute-start | bytes 1769480 | tf_op jit(solution)/shard_map/ppermute | solution.py:140
  18.5 20.8 %collective-permute-start.1 = (bf16[2,384,384]{2,1,0:T(8,128)(2,1)S(1)}, bf16[2,384,384]{2,1,0:T(8,128)(2,1)S(1)}, u32[]{:S(2)}, u32[]{:S(2)}) collective-permute-start(bf16[2,384,384]{2,1,0:T(8,128)(2,1)S(1)} %bitcast.206), channel_id=1, source_target_pairs={{4,0},{8,4},{12,8},{5,1},{9,5},{13,9},{6,2},{10,6},{14,10},{7,3},{... | collective-permute-start | bytes 1769480 | tf_op jit(solution)/shard_map/ppermute | solution.py:141
  21.9 10.6 %collective-permute-start.4 = (bf16[2,96,384]{2,1,0:T(8,128)(2,1)}, bf16[2,96,384]{2,1,0:T(8,128)(2,1)}, u32[]{:S(2)}, u32[]{:S(2)}) collective-permute-start(bf16[2,96,384]{2,1,0:T(8,128)(2,1)} %get-tuple-element.19), channel_id=1, source_target_pairs={{0,3},{1,0},{2,1},{3,2},{4,7},{5,4},{6,5},{7,6},{8,11},{9,8},{10,9... | collective-permute-start | bytes 442376 | tf_op jit(solution)/shard_map/ppermute | solution.py:52
  22.4 10.1 %collective-permute-start.2 = (bf16[2,96,384]{2,1,0:T(8,128)(2,1)}, bf16[2,96,384]{2,1,0:T(8,128)(2,1)}, u32[]{:S(2)}, u32[]{:S(2)}) collective-permute-start(bf16[2,96,384]{2,1,0:T(8,128)(2,1)} %get-tuple-element.17), channel_id=1, source_target_pairs={{0,1},{1,2},{2,3},{3,0},{4,5},{5,6},{6,7},{7,4},{8,9},{9,10},{10,1... | collective-permute-start | bytes 442376 | tf_op jit(solution)/shard_map/ppermute | solution.py:52
  24.0 13.9 %collective-permute-start.3 = (bf16[2,96,384]{2,1,0:T(8,128)(2,1)}, bf16[2,96,384]{2,1,0:T(8,128)(2,1)}, u32[]{:S(2)}, u32[]{:S(2)}) collective-permute-start(bf16[2,96,384]{2,1,0:T(8,128)(2,1)} %get-tuple-element.18), channel_id=1, source_target_pairs={{0,2},{1,3},{2,0},{3,1},{4,6},{5,7},{6,4},{7,5},{8,10},{9,11},{10,... | collective-permute-start | bytes 442376 | tf_op jit(solution)/shard_map/ppermute | solution.py:52

commit v6 on v5

--- a/solution.py
+++ b/solution.py
@@ -35,11 +35,8 @@
     phases = (indices[:, None] * indices[None, :] % extent).astype(np.float32)
     angle_values = np.float32(2.0 * math.pi / extent) * phases
     scaling = np.float32(1.0 / math.sqrt(extent))
-    cos_t = (np.cos(angle_values) * scaling).astype(ml_dtypes.bfloat16)
-    sin_t = (np.sin(angle_values) * scaling).astype(ml_dtypes.bfloat16)
-    block = np.block([[cos_t, sin_t], [-sin_t, cos_t]])
-    block = lax.optimization_barrier(jnp.asarray(block))
-    return jnp.stack([block[:extent, :extent], block[:extent, extent:]]), block
+    table = np.stack([np.cos(angle_values) * scaling, np.sin(angle_values) * scaling])
+    return jnp.asarray(table.astype(ml_dtypes.bfloat16))
 
 
 def combine_parts(products, direction):
@@ -75,7 +72,7 @@
     return picked.astype(kernels.dtype).reshape((angle_ids.shape[0],) + kernels.shape[1:])
 
 
-def forward_residual(transform, block, frame_image, coil_map, measured, row_placed, col_placed):
+def forward_residual(transform, frame_image, coil_map, measured, row_placed, col_placed):
     map_planes = coil_map.astype(jnp.float32)
     image_planes = frame_image.astype(jnp.float32)
     coil_image = jnp.stack(
@@ -88,6 +85,10 @@
         "bij,ajk->abik", coil_image, transform, preferred_element_type=jnp.float32
     )
     half_done = combine_parts(products, 1.0).astype(jnp.bfloat16)
+    cos_t, sin_t = lax.optimization_barrier(transform)
+    block = jnp.concatenate(
+        [jnp.concatenate([cos_t, sin_t], axis=1), jnp.concatenate([-sin_t, cos_t], axis=1)]
+    )
     extent = transform.shape[-1]
     kspace = jnp.dot(
         block, half_done.reshape(2 * extent, extent), preferred_element_type=jnp.float32
@@ -155,7 +156,7 @@
     coil_count = lax.axis_size("coil")
     coil_index = lax.axis_index("coil")
     rows = extent // coil_count
-    transform, block = transform_table(extent)
+    transform = transform_table(extent)
     map_rows = exchange_rows(coil_maps[0], rows, coil_count, coil_index)
     first_frame = lax.axis_index("frame") * frame_count
     frame_total = lax.axis_size("frame") * frame_count
@@ -171,7 +172,7 @@
     col_placed = jnp.einsum("gjq,gkq->gjk", col_w, col_select, **exact).astype(jnp.bfloat16)
     row_placed = jnp.einsum("grj,gir->gij", row_w, row_select, **exact)
     residual = forward_residual(
-        transform, block, images[0], coil_maps[0], kspace_data[0, 0], row_placed, col_placed
+        transform, images[0], coil_maps[0], kspace_data[0, 0], row_placed, col_placed
     )
     moved = [rotated(residual, coil_count, shift) for shift in range(1, coil_count)]
     residuals = jnp.stack([residual] + moved)

time: 58.8 us -> 58.7 us (level)
  other arithmetic: 7.1 us -> 10.4 us
  local copies, waits for them, and re-layouts: 5.18 us -> 3.6 us
  matrix products: 11.8 us -> 10.6 us
  waiting for transfers between devices: 5.38 us -> 4.77 us
    convert_element_type x1, other arithmetic: 0.08 us -> 1.2 us  [normed_change(): change = later.astype(jnp.float32) - earlier.astype(jnp.float32)]
    another operation x1, local copies, waits for them, and re-layouts: 1.17 us -> 0.06 us  [forward_residual(): cos_t, sin_t = lax.optimization_barrier(transform)]
    dot_general x2, matrix products: 1.84 us -> 0.79 us  [pick_kernels(): jnp.dot(choice.astype(kernels.dtype), flat, preferred_element_type=jnp.fl...]
    convert_element_type x1, other arithmetic: 0.03 us -> 0.77 us  [backward_rows(): row_w.astype(jnp.float32)[None, None] * residuals[:, :, :, None, :]]
    another operation x1, other arithmetic: 0.01 us -> 0.74 us  [body(): residuals = jnp.stack([residual] + moved)]
    ppermute x6, waiting for transfers between devices: 5.37 us -> 4.76 us  [rotated(): lax.ppermute(block, 'coil', [(i, (i + shift) % coil_count) for i in range...]
    sub x2, other arithmetic: 0.01 us -> 0.61 us  [forward_residual(): return predicted - measured]
    unnamed x18 -> x24, local copies, waits for them, and re-layouts: 2.9 us -> 2.73 us
  transfers between devices with their start and end apart: 8 -> 8, of which waited for: 1 -> 1; matrix products, arithmetic and copies ran while one was open for 20% -> 22% of each run, Pallas kernels for 0% -> 0%
where the time goes in v6:
time: 58.7 us; the launch traced here: 58.2 us
  blocking collectives  16.7 us (28%)
  starting transfers between devices  11.9 us (20%)
  matrix products  10.6 us (18%)
  other arithmetic  10.4 us (18%)
  waiting for transfers between devices  4.77 us (8%)
  local copies, waits for them, and re-layouts  3.6 us (6%)
    all_gather x1, blocking collectives, body(): lax.all_gather(grad_rows, 'coil', axis=1, tiled=True).astype(jnp.float32)  16.7 us
    ppermute x6, starting transfers between devices, rotated(): lax.ppermute(block, 'coil', [(i, (i + shift) % coil_count) for i in range...  9.25 us
    ppermute x6, waiting for transfers between devices, rotated(): lax.ppermute(block, 'coil', [(i, (i + shift) % coil_count) for i in range...  4.76 us
    dot_general x1, matrix products, backward_rows(): jnp.einsum('aigr,cbgrk->abcik', table_at, placed, preferred_element_type=...  4.72 us
    unnamed x24, local copies, waits for them, and re-layouts  2.73 us
    add x2, other arithmetic, combine_parts(): real_part = products[0, 0] + direction * products[1, 1]  1.43 us
    sub x2, other arithmetic, combine_parts(): imaginary = products[0, 1] - direction * products[1, 0]  1.37 us
    ppermute x1, starting transfers between devices, tv_single(): lax.ppermute(image, 'frame', [(i, i + 1) for i in range(count - 1)])  1.32 us
  transfers between devices with their start and end apart: 8, of which 1 were waited for; matrix products, arithmetic and copies ran while one was open for 22% of the time, Pallas kernels for 0%

profile of v6, /device:TPU:0, one launch (start us, length us, event | category | flops | bytes accessed | tf_op | source)
XLA Modules:
  0.0 58.2 jit_solution(2609800288619859542)
XLA Ops:
  0.0 1.2 %bitcast_convert_fusion.1 = f32[2,384,384]{2,1,0:T(8,128)S(1)} fusion(bf16[1,2,384,384]{3,2,1,0:T(8,128)(2,1)} %param.9), kind=kLoop, calls=%fused_computation.125 | loop fusion | flops 294912 | bytes 1769472 | tf_op jit(solution)/shard_map/convert_element_type | solution.py:133
  1.5 0.9 %copy-done.4 = bf16[2,384,384,1]{2,1,0,3:T(8,128)(2,1)S(1)} copy-done((bf16[2,384,384,1]{2,1,0,3:T(8,128)(2,1)S(1)}, bf16[2,384,384,1]{2,1,0,3:T(8,128)(2,1)}, u32[]{:S(2)}) %copy-start.4) | copy-done | bytes 589848
  2.4 0.8 %convolution_bitcast_fusion.1 = f32[2,2,384,384]{3,2,0,1:T(8,128)S(1)} fusion(bf16[2,384,384,1]{2,1,0,3:T(8,128)(2,1)S(1)} %copy-done.4, bf16[1,384,384]{2,1,0:T(8,128)(2,1)S(1)} %get-tuple-element.12, bf16[1,384,384]{2,1,0:T(8,128)(2,1)S(1)} %get-tuple-element.11), kind=kOutput, calls=%fused_computation.11 | convolution fusion | flops 454164480 | bytes 3538944 | tf_op jit(solution)/shard_map/bij,ajk->abik/dot_general | solution.py:84
  3.3 0.9 %copy-done.2 = bf16[2,384,384]{2,1,0:T(8,128)(2,1)S(1)} copy-done((bf16[2,384,384]{2,1,0:T(8,128)(2,1)S(1)}, bf16[2,384,384]{2,1,0:T(8,128)(2,1)}, u32[]{:S(2)}) %copy-start.2) | copy-done | bytes 589848
  4.4 0.5 copy-done.10
  5.7 0.4 fusion.27
  6.3 0.4 fusion.22
  6.7 0.4 convolution_convert_fusion.3
  7.1 0.8 %convolution_convert_fusion.2 = bf16[768,384]{1,0:T(8,128)(2,1)S(1)} fusion(bf16[768,384]{1,0:T(8,128)(2,1)S(1)} %bitcast.219, bf16[384,384]{1,0:T(8,128)(2,1)S(1)} %get-tuple-element.14, bf16[384,384]{1,0:T(8,128)(2,1)S(1)} %fusion.79, bf16[384,384]{1,0:T(8,128)(2,1)S(1)} %get-tuple-element.13), kind=kOutput, calls=%fused_computation.14 | convolution fusion | flops 457998336 | bytes 2064384 | tf_op jit(solution)/shard_map/dot_general | solution.py:93
  7.9 0.9 %fusion.5 = f32[2,6,128]{2,0,1:T(2,128)S(1)} fusion(bf16[2,384,384,1]{2,1,0,3:T(8,128)(2,1)S(1)} %bitcast.228, f32[6,384,128]{1,2,0:T(8,128)S(1)} %fusion.22, bf16[6,128,384]{2,1,0:T(8,128)(2,1)S(1)} %convolution_convert_fusion.3), kind=kOutput, calls=%fused_computation.8 | convolution fusion | flops 454162944 | bytes 2365440 | tf_op jit(solution)/shard_map/pik,gjk->pgij/dot_general | solution.py:96
  8.8 0.6 %bitcast_subtract_fusion = f32[2,6,128]{2,0,1:T(2,128)} fusion(f32[2,6,128]{2,0,1:T(2,128)S(1)} %fusion.5, f32[1,1,2,6,128]{4,2,3,1,0:T(2,128)S(1)} %copy-done.8), kind=kLoop, calls=%fused_computation.113 | loop fusion | flops 1536 | bytes 18432 | tf_op jit(solution)/shard_map/sub | solution.py:98
  9.4 3.1 %collective-permute-start.5 = (f32[2,6,128]{2,0,1:T(2,128)}, f32[2,6,128]{2,0,1:T(2,128)}, u32[]{:S(2)}, u32[]{:S(2)}) collective-permute-start(f32[2,6,128]{2,0,1:T(2,128)} %bitcast_subtract_fusion), channel_id=1, source_target_pairs={{0,1},{1,2},{2,3},{3,0},{4,5},{5,6},{6,7},{7,4},{8,9},{9,10},{10,1... | collective-permute-start | bytes 18440 | tf_op jit(solution)/shard_map/ppermute | solution.py:49
  12.5 2.6 %collective-permute-start.6 = (f32[2,6,128]{2,0,1:T(2,128)}, f32[2,6,128]{2,0,1:T(2,128)}, u32[]{:S(2)}, u32[]{:S(2)}) collective-permute-start(f32[2,6,128]{2,0,1:T(2,128)} %bitcast_subtract_fusion), channel_id=1, source_target_pairs={{0,2},{1,3},{2,0},{3,1},{4,6},{5,7},{6,4},{7,5},{8,10},{9,11},{10,... | collective-permute-start | bytes 18440 | tf_op jit(solution)/shard_map/ppermute | solution.py:49
  15.1 1.3 %collective-permute-start.7 = (f32[2,6,128]{2,0,1:T(2,128)}, f32[2,6,128]{2,0,1:T(2,128)}, u32[]{:S(2)}, u32[]{:S(2)}) collective-permute-start(f32[2,6,128]{2,0,1:T(2,128)} %bitcast_subtract_fusion), channel_id=1, source_target_pairs={{0,3},{1,0},{2,1},{3,2},{4,7},{5,4},{6,5},{7,6},{8,11},{9,8},{10,9... | collective-permute-start | bytes 18440 | tf_op jit(solution)/shard_map/ppermute | solution.py:49
  16.4 1.3 %collective-permute-start = (bf16[2,384,384]{2,1,0:T(8,128)(2,1)S(1)}, bf16[2,384,384]{2,1,0:T(8,128)(2,1)S(1)}, u32[]{:S(2)}, u32[]{:S(2)}) collective-permute-start(bf16[2,384,384]{2,1,0:T(8,128)(2,1)S(1)} %bitcast.216), channel_id=1, source_target_pairs={{0,4},{4,8},{8,12},{1,5},{5,9},{9,13},{2,6},{6,10},{10,14},{3,7},{... | collective-permute-start | bytes 1769480 | tf_op jit(solution)/shard_map/ppermute | solution.py:141
  17.7 1.3 %collective-permute-start.1 = (bf16[2,384,384]{2,1,0:T(8,128)(2,1)S(1)}, bf16[2,384,384]{2,1,0:T(8,128)(2,1)S(1)}, u32[]{:S(2)}, u32[]{:S(2)}) collective-permute-start(bf16[2,384,384]{2,1,0:T(8,128)(2,1)S(1)} %bitcast.217), channel_id=1, source_target_pairs={{4,0},{8,4},{12,8},{5,1},{9,5},{13,9},{6,2},{10,6},{14,10},{7,3},{... | collective-permute-start | bytes 1769480 | tf_op jit(solution)/shard_map/ppermute | solution.py:142
  19.0 0.8 %bitcast_convert_fusion = f32[6,128,128]{2,1,0:T(8,128)} fusion(bf16[1,6,128,128]{3,1,2,0:T(8,128)(2,1)S(1)} %fusion.28), kind=kLoop, calls=%fused_computation.100 | loop fusion | flops 98304 | bytes 589824 | tf_op jit(solution)/shard_map/convert_element_type | solution.py:103
  19.8 1.1 %fusion.24 = bf16[2,96,6,128,1,1]{3,1,2,0,5,4:T(8,128)(2,1)} fusion(s32[6,128]{1,0:T(8,128)S(1)} %iota_add_fusion, bf16[2,384,384]{2,1,0:T(8,128)(2,1)S(1)} %copy-done.2, s32[]{:T(128)S(6)} %select_n.28), kind=kOutput, calls=%fused_computation.33 | convolution fusion | flops 113688576 | bytes 446468 | tf_op jit(solution)/shard_map/aij,gjr->aigr/dot_general | solution.py:108
  20.9 0.8 %dynamic-slice_bitcast_fusion.2 = (bf16[2,96,384]{2,1,0:T(8,128)(2,1)}, bf16[2,96,384]{2,1,0:T(8,128)(2,1)}, bf16[2,96,384]{2,1,0:T(8,128)(2,1)}) fusion(bf16[1,2,384,384]{3,2,1,0:T(8,128)(2,1)S(1)} %copy-done.1, s32[]{:T(128)S(6)} %select_n.30, s32[]{:T(128)S(6)} %select_n.32, s32[]{:T(128)S(6)} %select_n.34), kind=kLoop, calls=%fused_computation.108 | loop fusion | bytes 884748 | tf_op jit(solution)/shard_map/dynamic_slice | solution.py:56
  21.7 0.5 collective-permute-start.4
  22.2 1.6 %collective-permute-start.2 = (bf16[2,96,384]{2,1,0:T(8,128)(2,1)}, bf16[2,96,384]{2,1,0:T(8,128)(2,1)}, u32[]{:S(2)}, u32[]{:S(2)}) collective-permute-start(bf16[2,96,384]{2,1,0:T(8,128)(2,1)} %get-tuple-element.15), channel_id=1, source_target_pairs={{0,1},{1,2},{2,3},{3,0},{4,5},{5,6},{6,7},{7,4},{8,9},{9,10},{10,1... | collective-permute-start | bytes 442376 | tf_op jit(solution)/shard_map/ppermute | solution.py:49
  24.0 0.7 %pad_maximum_fusion.2 = f32[4,2,6,128]{3,1,2,0:T(2,128)S(1)} fusion(f32[1,2,6,128]{3,1,2,0:T(2,128)} %bitcast.38, f32[1,2,6,128]{3,1,2,0:T(2,128)} %bitcast.37, f32[1,2,6,128]{3,1,2,0:T(2,128)} %bitcast.36, f32[1,2,6,128]{3,1,2,0:T(2,128)S(1)} %bitcast_subtract_fusion.1), kind=kLoop, calls=%fused_computation.112 | loop fusion | flops 18432 | bytes 49152 | tf_op jit(solution)/shard_map/stack | solution.py:178
  24.8 4.7 %fusion.6 = f32[2,2,4,96,384]{4,3,0,1,2:T(8,128)} fusion(bf16[2,96,6,128,1,1]{3,1,2,0,5,4:T(8,128)(2,1)} %fusion.24, f32[4,2,6,128]{3,2,1,0:T(8,128)S(1)} %copy.14, f32[6,128,128]{2,1,0:T(8,128)S(1)} %copy-done.7, bf16[6,128,384]{2,1,0:T(8,128)(2,1)S(1)} %convolution_convert_fusion.3), kind=kOutput, calls=%fused_computation.9 | convolution fusion | flops 1513881600 | bytes 3661824 | tf_op jit(solution)/shard_map/aigr,cbgrk->abcik/dot_general | solution.py:111
  29.5 1.4 %fusion.65 = bf16[1,4,96,384]{3,2,1,0:T(8,128)(2,1)S(1)} fusion(f32[2,2,4,96,384]{4,3,0,1,2:T(8,128)} %fusion.6), kind=kLoop, calls=%fused_computation.95 | loop fusion | flops 442368 | bytes 1474560 | tf_op jit(solution)/shard_map/add | solution.py:43
  30.9 1.3 %fusion.66 = bf16[1,4,96,384]{3,2,1,0:T(8,128)(2,1)S(1)} fusion(f32[2,2,4,96,384]{4,3,0,1,2:T(8,128)} %fusion.6), kind=kLoop, calls=%fused_computation.96 | loop fusion | flops 442368 | bytes 1474560 | tf_op jit(solution)/shard_map/sub | solution.py:44
  32.2 0.8 %convolution_bitcast_fusion = f32[2,2,4,96,384]{4,3,2,1,0:T(8,128)S(1)} fusion(bf16[2,384,384,1,1]{2,1,4,3,0:T(8,128)(2,1)S(1)} %copy-done.3, bf16[1,4,96,384]{3,2,1,0:T(8,128)(2,1)S(1)} %fusion.66, bf16[1,4,96,384]{3,2,1,0:T(8,128)(2,1)S(1)} %fusion.65), kind=kOutput, calls=%fused_computation.10 | convolution fusion | flops 454164480 | bytes 3538944 | tf_op jit(solution)/shard_map/bcij,ajk->abcik/dot_general | solution.py:113
  33.0 4.8 %collective-permute-done.3 = bf16[2,96,384]{2,1,0:T(8,128)(2,1)} collective-permute-done((bf16[2,96,384]{2,1,0:T(8,128)(2,1)}, bf16[2,96,384]{2,1,0:T(8,128)(2,1)}, u32[]{:S(2)}, u32[]{:S(2)}) %collective-permute-start.3) | collective-permute-done | bytes 147488 | tf_op jit(solution)/shard_map/ppermute | solution.py:49
  37.7 1.2 %maximum_convert_fusion = f32[4,2,96,384]{3,2,0,1:T(8,128)S(1)} fusion(bf16[1,2,96,384]{3,2,0,1:T(8,128)(2,1)} %bitcast.10, bf16[1,2,96,384]{3,2,0,1:T(8,128)(2,1)} %bitcast.8, bf16[1,2,96,384]{3,2,0,1:T(8,128)(2,1)} %bitcast.6, bf16[1,2,96,384]{3,2,0,1:T(8,128)(2,1)S(1)} %constant_dynamic-slice_fusion), kind=kLoop, calls=%fused_computation.72 | loop fusion | flops 1179648 | bytes 1769472 | tf_op jit(solution)/shard_map/convert_element_type | solution.py:115
  39.4 0.4 fusion.44
  39.9 0.5 subtract_bitcast_fusion
  40.3 16.7 %all_gather.3 = bf16[2,384,384]{2,1,0:T(8,128)(2,1)S(1)} all-gather(bf16[2,96,384]{2,1,0:T(8,128)(2,1)S(1)} %pad_maximum_fusion.1), channel_id=1, replica_groups=mesh['grp'=2,'frame'=4,'coil'=4] {'coil'}, dimensions={1}, use_global_device_ids=true | all-gather | bytes 737280 | tf_op jit(solution)/shard_map/all_gather | solution.py:183
  57.0 1.3 %fusion.20 = f32[1,2,384,384]{3,2,1,0:T(8,128)} fusion(f32[1,2,384,384]{3,2,1,0:T(8,128)S(1)} %subtract_bitcast_fusion, bf16[1,2,384,384]{3,2,1,0:T(8,128)(2,1)S(1)} %copy-done, bf16[2,384,384]{2,1,0:T(8,128)(2,1)S(1)} %all_gather.3), kind=kLoop, calls=%fused_computation.25 | loop fusion | flops 1474560 | bytes 3538944 | tf_op jit(solution)/shard_map/sub | solution.py:184
  (45 shorter events, 2.2 us)
Async XLA Ops:
  0.0 1.2 %copy-start.1 = (bf16[1,2,384,384]{3,2,1,0:T(8,128)(2,1)S(1)}, bf16[1,2,384,384]{3,2,1,0:T(8,128)(2,1)}, u32[]{:S(2)}) copy-start(bf16[1,2,384,384]{3,2,1,0:T(8,128)(2,1)} %param.10) | copy-start | bytes 1769476
  1.3 1.1 %copy-start.4 = (bf16[2,384,384,1]{2,1,0,3:T(8,128)(2,1)S(1)}, bf16[2,384,384,1]{2,1,0,3:T(8,128)(2,1)}, u32[]{:S(2)}) copy-start(bf16[2,384,384,1]{2,1,0,3:T(8,128)(2,1)} %constant.59) | copy-start | bytes 1769476
  3.2 1.1 %copy-start.2 = (bf16[2,384,384]{2,1,0:T(8,128)(2,1)S(1)}, bf16[2,384,384]{2,1,0:T(8,128)(2,1)}, u32[]{:S(2)}) copy-start(bf16[2,384,384]{2,1,0:T(8,128)(2,1)} %constant.52.clone) | copy-start | bytes 1769476
  4.2 0.7 %copy-start.10 = (s32[1,6]{1,0:T(1,128)S(1)}, s32[1,6]{1,0:T(1,128)}, u32[]{:S(2)}) copy-start(s32[1,6]{1,0:T(1,128)} %param.13) | copy-start | bytes 76
  4.2 1.1 %copy-start.5 = (bf16[16,128,128]{2,1,0:T(8,128)(2,1)S(1)}, bf16[16,128,128]{2,1,0:T(8,128)(2,1)}, u32[]{:S(2)}) copy-start(bf16[16,128,128]{2,1,0:T(8,128)(2,1)} %param.15) | copy-start | bytes 1572868
  4.2 1.1 %copy-start.9 = (s32[1,6]{1,0:T(1,128)S(1)}, s32[1,6]{1,0:T(1,128)}, u32[]{:S(2)}) copy-start(s32[1,6]{1,0:T(1,128)} %param.12) | copy-start | bytes 76
  4.2 1.5 %copy-start.6 = (bf16[16,128,128]{2,1,0:T(8,128)(2,1)S(1)}, bf16[16,128,128]{2,1,0:T(8,128)(2,1)}, u32[]{:S(2)}) copy-start(bf16[16,128,128]{2,1,0:T(8,128)(2,1)} %param.16) | copy-start | bytes 1572868
  4.3 1.8 %copy-start.11 = (s32[1,6]{1,0:T(1,128)S(1)}, s32[1,6]{1,0:T(1,128)}, u32[]{:S(2)}) copy-start(s32[1,6]{1,0:T(1,128)} %param.14) | copy-start | bytes 76
  7.9 0.9 %copy-start.8 = (f32[1,1,2,6,128]{4,2,3,1,0:T(2,128)S(1)}, f32[1,1,2,6,128]{4,2,3,1,0:T(2,128)}, u32[]{:S(2)}) copy-start(f32[1,1,2,6,128]{4,2,3,1,0:T(2,128)} %param.11) | copy-start | bytes 18436
  7.9 8.5 %copy-start = (bf16[1,2,384,384]{3,2,1,0:T(8,128)(2,1)S(1)}, bf16[1,2,384,384]{3,2,1,0:T(8,128)(2,1)}, u32[]{:S(2)}) copy-start(bf16[1,2,384,384]{3,2,1,0:T(8,128)(2,1)} %param.9) | copy-start | bytes 1769476
  9.4 12.3 %collective-permute-start.5 = (f32[2,6,128]{2,0,1:T(2,128)}, f32[2,6,128]{2,0,1:T(2,128)}, u32[]{:S(2)}, u32[]{:S(2)}) collective-permute-start(f32[2,6,128]{2,0,1:T(2,128)} %bitcast_subtract_fusion), channel_id=1, source_target_pairs={{0,1},{1,2},{2,3},{3,0},{4,5},{5,6},{6,7},{7,4},{8,9},{9,10},{10,1... | collective-permute-start | bytes 18440 | tf_op jit(solution)/shard_map/ppermute | solution.py:49
  12.5 9.8 %collective-permute-start.6 = (f32[2,6,128]{2,0,1:T(2,128)}, f32[2,6,128]{2,0,1:T(2,128)}, u32[]{:S(2)}, u32[]{:S(2)}) collective-permute-start(f32[2,6,128]{2,0,1:T(2,128)} %bitcast_subtract_fusion), channel_id=1, source_target_pairs={{0,2},{1,3},{2,0},{3,1},{4,6},{5,7},{6,4},{7,5},{8,10},{9,11},{10,... | collective-permute-start | bytes 18440 | tf_op jit(solution)/shard_map/ppermute | solution.py:49
  15.1 8.8 %collective-permute-start.7 = (f32[2,6,128]{2,0,1:T(2,128)}, f32[2,6,128]{2,0,1:T(2,128)}, u32[]{:S(2)}, u32[]{:S(2)}) collective-permute-start(f32[2,6,128]{2,0,1:T(2,128)} %bitcast_subtract_fusion), channel_id=1, source_target_pairs={{0,3},{1,0},{2,1},{3,2},{4,7},{5,4},{6,5},{7,6},{8,11},{9,8},{10,9... | collective-permute-start | bytes 18440 | tf_op jit(solution)/shard_map/ppermute | solution.py:49
  16.4 22.8 %collective-permute-start = (bf16[2,384,384]{2,1,0:T(8,128)(2,1)S(1)}, bf16[2,384,384]{2,1,0:T(8,128)(2,1)S(1)}, u32[]{:S(2)}, u32[]{:S(2)}) collective-permute-start(bf16[2,384,384]{2,1,0:T(8,128)(2,1)S(1)} %bitcast.216), channel_id=1, source_target_pairs={{0,4},{4,8},{8,12},{1,5},{5,9},{9,13},{2,6},{6,10},{10,14},{3,7},{... | collective-permute-start | bytes 1769480 | tf_op jit(solution)/shard_map/ppermute | solution.py:141
  17.7 21.5 %collective-permute-start.1 = (bf16[2,384,384]{2,1,0:T(8,128)(2,1)S(1)}, bf16[2,384,384]{2,1,0:T(8,128)(2,1)S(1)}, u32[]{:S(2)}, u32[]{:S(2)}) collective-permute-start(bf16[2,384,384]{2,1,0:T(8,128)(2,1)S(1)} %bitcast.217), channel_id=1, source_target_pairs={{4,0},{8,4},{12,8},{5,1},{9,5},{13,9},{6,2},{10,6},{14,10},{7,3},{... | collective-permute-start | bytes 1769480 | tf_op jit(solution)/shard_map/ppermute | solution.py:142
  20.9 3.9 %copy-start.7 = (f32[6,128,128]{2,1,0:T(8,128)S(1)}, f32[6,128,128]{2,1,0:T(8,128)}, u32[]{:S(2)}) copy-start(f32[6,128,128]{2,1,0:T(8,128)} %bitcast_convert_fusion) | copy-start | bytes 1179652
  21.7 11.2 %collective-permute-start.4 = (bf16[2,96,384]{2,1,0:T(8,128)(2,1)}, bf16[2,96,384]{2,1,0:T(8,128)(2,1)}, u32[]{:S(2)}, u32[]{:S(2)}) collective-permute-start(bf16[2,96,384]{2,1,0:T(8,128)(2,1)} %get-tuple-element.17), channel_id=1, source_target_pairs={{0,3},{1,0},{2,1},{3,2},{4,7},{5,4},{6,5},{7,6},{8,11},{9,8},{10,9... | collective-permute-start | bytes 442376 | tf_op jit(solution)/shard_map/ppermute | solution.py:49
  22.2 10.7 %collective-permute-start.2 = (bf16[2,96,384]{2,1,0:T(8,128)(2,1)}, bf16[2,96,384]{2,1,0:T(8,128)(2,1)}, u32[]{:S(2)}, u32[]{:S(2)}) collective-permute-start(bf16[2,96,384]{2,1,0:T(8,128)(2,1)} %get-tuple-element.15), channel_id=1, source_target_pairs={{0,1},{1,2},{2,3},{3,0},{4,5},{5,6},{6,7},{7,4},{8,9},{9,10},{10,1... | collective-permute-start | bytes 442376 | tf_op jit(solution)/shard_map/ppermute | solution.py:49
  23.8 13.9 %collective-permute-start.3 = (bf16[2,96,384]{2,1,0:T(8,128)(2,1)}, bf16[2,96,384]{2,1,0:T(8,128)(2,1)}, u32[]{:S(2)}, u32[]{:S(2)}) collective-permute-start(bf16[2,96,384]{2,1,0:T(8,128)(2,1)} %get-tuple-element.16), channel_id=1, source_target_pairs={{0,2},{1,3},{2,0},{3,1},{4,6},{5,7},{6,4},{7,5},{8,10},{9,11},{10,... | collective-permute-start | bytes 442376 | tf_op jit(solution)/shard_map/ppermute | solution.py:49
  29.5 2.7 %copy-start.3 = (bf16[2,384,384,1,1]{2,1,4,3,0:T(8,128)(2,1)S(1)}, bf16[2,384,384,1,1]{2,1,4,3,0:T(8,128)(2,1)}, u32[]{:S(2)}) copy-start(bf16[2,384,384,1,1]{2,1,4,3,0:T(8,128)(2,1)} %constant.60) | copy-start | bytes 1769476

commit v7 on v5

--- a/solution.py
+++ b/solution.py
@@ -37,9 +37,7 @@
     scaling = np.float32(1.0 / math.sqrt(extent))
     cos_t = (np.cos(angle_values) * scaling).astype(ml_dtypes.bfloat16)
     sin_t = (np.sin(angle_values) * scaling).astype(ml_dtypes.bfloat16)
-    block = np.block([[cos_t, sin_t], [-sin_t, cos_t]])
-    block = lax.optimization_barrier(jnp.asarray(block))
-    return jnp.stack([block[:extent, :extent], block[:extent, extent:]]), block
+    return lax.optimization_barrier(jnp.asarray(np.block([[cos_t, sin_t], [-sin_t, cos_t]])))
 
 
 def combine_parts(products, direction):
@@ -75,7 +73,7 @@
     return picked.astype(kernels.dtype).reshape((angle_ids.shape[0],) + kernels.shape[1:])
 
 
-def forward_residual(transform, block, frame_image, coil_map, measured, row_placed, col_placed):
+def forward_residual(block, frame_image, coil_map, measured, row_placed, col_placed):
     map_planes = coil_map.astype(jnp.float32)
     image_planes = frame_image.astype(jnp.float32)
     coil_image = jnp.stack(
@@ -84,11 +82,14 @@
             map_planes[0] * image_planes[1] + map_planes[1] * image_planes[0],
         ]
     ).astype(jnp.bfloat16)
-    products = jnp.einsum(
-        "bij,ajk->abik", coil_image, transform, preferred_element_type=jnp.float32
-    )
-    half_done = combine_parts(products, 1.0).astype(jnp.bfloat16)
-    extent = transform.shape[-1]
+    extent = block.shape[0] // 2
+    side = block[:extent]
+    out = jnp.dot(
+        coil_image.reshape(2 * extent, extent), side, preferred_element_type=jnp.float32
+    ).reshape(2, extent, 2, extent)
+    half_done = jnp.stack(
+        [out[0, :, 0] + out[1, :, 1], out[1, :, 0] - out[0, :, 1]]
+    ).astype(jnp.bfloat16)
     kspace = jnp.dot(
         block, half_done.reshape(2 * extent, extent), preferred_element_type=jnp.float32
     ).astype(jnp.bfloat16).reshape(2, extent, extent)
@@ -97,20 +98,28 @@
     return predicted - measured
 
 
-def backward_rows(transform, residuals, map_rows, row_select, row_w, col_placed, coil_index):
+def backward_rows(block, residuals, map_rows, row_select, row_w, col_placed, coil_index):
     rows = map_rows.shape[2]
     spread = (row_w.astype(jnp.float32)[None, None] * residuals[:, :, :, None, :]).astype(jnp.bfloat16)
     placed = jnp.einsum(
         "cpgrj,gjk->cpgrk", spread, col_placed, preferred_element_type=jnp.float32
     ).astype(jnp.bfloat16)
-    row_table = lax.dynamic_slice_in_dim(transform, coil_index * rows, rows, axis=1)
+    extent = block.shape[0] // 2
+    row_table = lax.dynamic_slice_in_dim(block[:extent], coil_index * rows, rows, axis=0)
     table_at = jnp.einsum(
-        "aij,gjr->aigr", row_table, row_select, preferred_element_type=jnp.float32
+        "iaj,gjr->aigr", row_table.reshape(rows, 2, extent), row_select,
+        preferred_element_type=jnp.float32,
     ).astype(jnp.bfloat16)
     products = jnp.einsum("aigr,cbgrk->abcik", table_at, placed, preferred_element_type=jnp.float32)
     half_back = combine_parts(products, -1.0).astype(jnp.bfloat16)
-    products = jnp.einsum("bcij,ajk->abcik", half_back, transform, preferred_element_type=jnp.float32)
-    coil_back = combine_parts(products, -1.0)
+    planes, coil_count = half_back.shape[:2]
+    out = jnp.dot(
+        half_back.reshape(planes * coil_count * rows, extent), block[:extent],
+        preferred_element_type=jnp.float32,
+    ).reshape(planes, coil_count, rows, 2, extent)
+    coil_back = jnp.stack(
+        [out[0, :, :, 0] - out[1, :, :, 1], out[1, :, :, 0] + out[0, :, :, 1]]
+    )
     maps = map_rows.astype(jnp.float32)
     real_part = jnp.sum(maps[:, 0] * coil_back[0] + maps[:, 1] * coil_back[1], axis=0)
     imaginary = jnp.sum(maps[:, 0] * coil_back[1] - maps[:, 1] * coil_back[0], axis=0)
@@ -141,9 +150,7 @@
     later = lax.ppermute(image, "frame", [(i + 1, i) for i in range(count - 1)])
     has_earlier = (frame_index >= 1).astype(jnp.float32)
     has_later = (frame_index <= frame_total - 2).astype(jnp.float32)
-    return (
-        normed_change(image, earlier, has_earlier) - normed_change(later, image, has_later)
-    )[None]
+    return (normed_change(image, earlier, has_earlier) - normed_change(later, image, has_later))[None]
 
 
 def body(
@@ -155,7 +162,7 @@
     coil_count = lax.axis_size("coil")
     coil_index = lax.axis_index("coil")
     rows = extent // coil_count
-    transform, block = transform_table(extent)
+    block = transform_table(extent)
     map_rows = exchange_rows(coil_maps[0], rows, coil_count, coil_index)
     first_frame = lax.axis_index("frame") * frame_count
     frame_total = lax.axis_size("frame") * frame_count
@@ -171,12 +178,13 @@
     col_placed = jnp.einsum("gjq,gkq->gjk", col_w, col_select, **exact).astype(jnp.bfloat16)
     row_placed = jnp.einsum("grj,gir->gij", row_w, row_select, **exact)
     residual = forward_residual(
-        transform, block, images[0], coil_maps[0], kspace_data[0, 0], row_placed, col_placed
-    )
-    moved = [rotated(residual, coil_count, shift) for shift in range(1, coil_count)]
-    residuals = jnp.stack([residual] + moved)
+        block, images[0], coil_maps[0], kspace_data[0, 0], row_placed, col_placed
+    )
+    residuals = jnp.stack(
+        [residual] + [rotated(residual, coil_count, shift) for shift in range(1, coil_count)]
+    )
     grad_rows = backward_rows(
-        transform, residuals, map_rows, row_select, row_w, col_placed, coil_index
+        block, residuals, map_rows, row_select, row_w, col_placed, coil_index
     )
     tv_grad, grad_rows = lax.optimization_barrier((tv_grad, grad_rows.astype(jnp.bfloat16)))
     data_grad = lax.all_gather(grad_rows, "coil", axis=1, tiled=True).astype(jnp.float32)[None]

time: 58.8 us -> 58.9 us (level)
    slice x0 -> x1, local copies, waits for them, and re-layouts: none -> 1.19 us  [forward_residual(): side = block[:extent]]
    another operation x2 -> x1, local copies, waits for them, and re-layouts: 1.18 us -> 0.01 us  [body(): jnp.stack([residual] + [rotated(residual, coil_count, shift) for shift in...]
    add x2 -> x1, other arithmetic: 1.43 us -> 1.31 us  [combine_parts(): real_part = products[0, 0] + direction * products[1, 1]]
where the time goes in v7:
time: 58.9 us; the launch traced here: 58.5 us
  blocking collectives  16.7 us (28%)
  starting transfers between devices  11.9 us (20%)
  matrix products  11.8 us (20%)
  other arithmetic  7.07 us (12%)
  waiting for transfers between devices  5.36 us (9%)
  local copies, waits for them, and re-layouts  5.32 us (9%)
    all_gather x1, blocking collectives, body(): lax.all_gather(grad_rows, 'coil', axis=1, tiled=True).astype(jnp.float32)  16.7 us
    ppermute x6, starting transfers between devices, rotated(): lax.ppermute(block, 'coil', [(i, (i + shift) % coil_count) for i in range...  9.32 us
    ppermute x6, waiting for transfers between devices, rotated(): lax.ppermute(block, 'coil', [(i, (i + shift) % coil_count) for i in range...  5.35 us
    dot_general x1, matrix products, backward_rows(): jnp.einsum('aigr,cbgrk->abcik', table_at, placed, preferred_element_type=...  4.9 us
    unnamed x18, local copies, waits for them, and re-layouts  2.89 us
    dot_general x2, matrix products, pick_kernels(): jnp.dot(choice.astype(kernels.dtype), flat, preferred_element_type=jnp.fl...  1.84 us
    sub x1, other arithmetic, combine_parts(): imaginary = products[0, 1] - direction * products[1, 0]  1.31 us
    ppermute x1, starting transfers between devices, tv_single(): lax.ppermute(image, 'frame', [(i, i + 1) for i in range(count - 1)])  1.31 us
  transfers between devices with their start and end apart: 8, of which 1 were waited for; matrix products, arithmetic and copies ran while one was open for 20% of the time, Pallas kernels for 0%

profile of v7, /device:TPU:0, one launch (start us, length us, event | category | flops | bytes accessed | tf_op | source)
XLA Modules:
  0.0 58.5 jit_solution(2020601276245939758)
XLA Ops:
  0.0 1.2 %slice.121 = bf16[384,768]{0,1:T(8,128)(2,1)S(1)} slice(bf16[768,768]{0,1:T(8,128)(2,1)} %constant.52.clone), slice={[0:384], [0:768]} | slice | bytes 1179648 | tf_op jit(solution)/shard_map/slice | solution.py:86
  1.3 1.0 %copy-done.1 = bf16[1,2,384,384]{3,2,1,0:T(8,128)(2,1)S(1)} copy-done((bf16[1,2,384,384]{3,2,1,0:T(8,128)(2,1)S(1)}, bf16[1,2,384,384]{3,2,1,0:T(8,128)(2,1)}, u32[]{:S(2)}) %copy-start.1) | copy-done | bytes 589848
  2.6 0.8 %fusion.41 = f32[2,384,2,384]{3,1,2,0:T(8,128)S(1)} fusion(bf16[2,384,384,1]{2,1,0,3:T(8,128)(2,1)S(1)} %bitcast.225, bf16[1,384,384]{2,1,0:T(8,128)(2,1)S(1)} %get-tuple-element.14, bf16[1,384,384]{2,1,0:T(8,128)(2,1)S(1)} %get-tuple-element.13), kind=kOutput, calls=%fused_computation.64 | convolution fusion | flops 454164480 | bytes 3538944 | tf_op jit(solution)/shard_map/dot_general | solution.py:87
  3.6 1.2 %copy-done.4 = bf16[768,768]{0,1:T(8,128)(2,1)S(1)} copy-done((bf16[768,768]{0,1:T(8,128)(2,1)S(1)}, bf16[768,768]{0,1:T(8,128)(2,1)}, u32[]{:S(2)}) %copy-start.4) | copy-done | bytes 1179672
  4.8 0.7 %fusion.13 = bf16[768,384]{0,1:T(8,128)(2,1)S(1)} fusion(bf16[768,384]{1,0:T(8,128)(2,1)S(1)} %bitcast.229, bf16[768,768]{0,1:T(8,128)(2,1)S(1)} %copy-done.4), kind=kOutput, calls=%fused_computation.14 | convolution fusion | flops 453279744 | bytes 2359296 | tf_op jit(solution)/shard_map/dot_general | solution.py:93
  5.5 0.3 copy.29
  5.8 0.3 copy-done.7
  6.1 0.3 copy-done.3
  6.5 0.4 fusion.22
  6.9 1.4 %fusion.21 = bf16[1,6,128,128]{3,1,2,0:T(8,128)(2,1)S(1)} fusion(bf16[2,8,128,128]{3,2,1,0:T(8,128)(2,1)} %bitcast.231, s32[6]{0:T(128)S(1)} %bitcast.239), kind=kOutput, calls=%fused_computation.26 | convolution fusion | flops 3244128 | bytes 720920 | tf_op jit(solution)/shard_map/dot_general | solution.py:72
  8.4 0.4 fusion.16
  8.8 0.4 convolution_convert_fusion.3
  9.2 0.9 %fusion.5 = f32[2,6,128]{2,0,1:T(2,128)S(1)} fusion(bf16[2,384,384,1]{2,1,0,3:T(8,128)(2,1)S(1)} %bitcast.228, f32[6,384,128]{1,2,0:T(8,128)S(1)} %fusion.16, bf16[6,128,384]{2,1,0:T(8,128)(2,1)S(1)} %convolution_convert_fusion.3), kind=kOutput, calls=%fused_computation.8 | convolution fusion | flops 454162944 | bytes 2365440 | tf_op jit(solution)/shard_map/pik,gjk->pgij/dot_general | solution.py:96
  10.2 3.1 %collective-permute-start.5 = (f32[2,6,128]{2,0,1:T(2,128)S(1)}, f32[2,6,128]{2,0,1:T(2,128)S(1)}, u32[]{:S(2)}, u32[]{:S(2)}) collective-permute-start(f32[2,6,128]{2,0,1:T(2,128)S(1)} %bitcast_subtract_fusion), channel_id=1, source_target_pairs={{0,1},{1,2},{2,3},{3,0},{4,5},{5,6},{6,7},{7,4},{8,9},{9,10},{10,1... | collective-permute-start | bytes 18440 | tf_op jit(solution)/shard_map/ppermute | solution.py:50
  13.3 2.6 %collective-permute-start.6 = (f32[2,6,128]{2,0,1:T(2,128)S(1)}, f32[2,6,128]{2,0,1:T(2,128)S(1)}, u32[]{:S(2)}, u32[]{:S(2)}) collective-permute-start(f32[2,6,128]{2,0,1:T(2,128)S(1)} %bitcast_subtract_fusion), channel_id=1, source_target_pairs={{0,2},{1,3},{2,0},{3,1},{4,6},{5,7},{6,4},{7,5},{8,10},{9,11},{10,... | collective-permute-start | bytes 18440 | tf_op jit(solution)/shard_map/ppermute | solution.py:50
  15.9 1.3 %collective-permute-start.7 = (f32[2,6,128]{2,0,1:T(2,128)S(1)}, f32[2,6,128]{2,0,1:T(2,128)S(1)}, u32[]{:S(2)}, u32[]{:S(2)}) collective-permute-start(f32[2,6,128]{2,0,1:T(2,128)S(1)} %bitcast_subtract_fusion), channel_id=1, source_target_pairs={{0,3},{1,0},{2,1},{3,2},{4,7},{5,4},{6,5},{7,6},{8,11},{9,8},{10,9... | collective-permute-start | bytes 18440 | tf_op jit(solution)/shard_map/ppermute | solution.py:50
  17.2 1.3 %collective-permute-start = (bf16[2,384,384]{2,1,0:T(8,128)(2,1)S(1)}, bf16[2,384,384]{2,1,0:T(8,128)(2,1)S(1)}, u32[]{:S(2)}, u32[]{:S(2)}) collective-permute-start(bf16[2,384,384]{2,1,0:T(8,128)(2,1)S(1)} %bitcast.223), channel_id=1, source_target_pairs={{0,4},{4,8},{8,12},{1,5},{5,9},{9,13},{2,6},{6,10},{10,14},{3,7},{... | collective-permute-start | bytes 1769480 | tf_op jit(solution)/shard_map/ppermute | solution.py:149
  18.5 1.3 %collective-permute-start.1 = (bf16[2,384,384]{2,1,0:T(8,128)(2,1)S(1)}, bf16[2,384,384]{2,1,0:T(8,128)(2,1)S(1)}, u32[]{:S(2)}, u32[]{:S(2)}) collective-permute-start(bf16[2,384,384]{2,1,0:T(8,128)(2,1)S(1)} %bitcast.224), channel_id=1, source_target_pairs={{4,0},{8,4},{12,8},{5,1},{9,5},{13,9},{6,2},{10,6},{14,10},{7,3},{... | collective-permute-start | bytes 1769480 | tf_op jit(solution)/shard_map/ppermute | solution.py:150
  20.1 1.1 %fusion.18 = bf16[2,96,6,128,1,1]{3,1,2,0,5,4:T(8,128)(2,1)} fusion(bf16[96,2,384,1]{0,2,3,1:T(8,128)(2,1)S(1)} %bitcast.234, s32[6,128]{1,0:T(8,128)S(1)} %iota_add_fusion), kind=kOutput, calls=%fused_computation.25 | convolution fusion | flops 113688576 | bytes 445440 | tf_op jit(solution)/shard_map/iaj,gjr->aigr/dot_general | solution.py:109
  21.2 0.8 %dynamic-slice_bitcast_fusion.2 = (bf16[2,96,384]{2,1,0:T(8,128)(2,1)}, bf16[2,96,384]{2,1,0:T(8,128)(2,1)}, bf16[2,96,384]{2,1,0:T(8,128)(2,1)}) fusion(bf16[1,2,384,384]{3,2,1,0:T(8,128)(2,1)S(1)} %copy-done.1, s32[]{:T(128)S(6)} %select_n.30, s32[]{:T(128)S(6)} %select_n.32, s32[]{:T(128)S(6)} %select_n.34), kind=kLoop, calls=%fused_computation.96 | loop fusion | bytes 884748 | tf_op jit(solution)/shard_map/dynamic_slice | solution.py:57
  22.0 0.5 collective-permute-start.4
  22.5 1.6 %collective-permute-start.2 = (bf16[2,96,384]{2,1,0:T(8,128)(2,1)}, bf16[2,96,384]{2,1,0:T(8,128)(2,1)}, u32[]{:S(2)}, u32[]{:S(2)}) collective-permute-start(bf16[2,96,384]{2,1,0:T(8,128)(2,1)} %get-tuple-element.15), channel_id=1, source_target_pairs={{0,1},{1,2},{2,3},{3,0},{4,5},{5,6},{6,7},{7,4},{8,9},{9,10},{10,1... | collective-permute-start | bytes 442376 | tf_op jit(solution)/shard_map/ppermute | solution.py:50
  24.4 4.9 %fusion.6 = f32[2,2,4,96,384]{4,3,0,1,2:T(8,128)} fusion(bf16[2,96,6,128,1,1]{3,1,2,0,5,4:T(8,128)(2,1)} %fusion.18, f32[4,2,6,128]{3,2,1,0:T(8,128)S(1)} %copy.13, f32[6,128,128]{2,1,0:T(8,128)S(1)} %bitcast_convert_fusion, bf16[6,128,384]{2,1,0:T(8,128)(2,1)} %copy-done.2), kind=kOutput, calls=%fused_computation.9 | convolution fusion | flops 1513881600 | bytes 3661824 | tf_op jit(solution)/shard_map/aigr,cbgrk->abcik/dot_general | solution.py:113
  29.3 1.3 %fusion.59 = bf16[1,4,96,384]{3,2,1,0:T(8,128)(2,1)S(1)} fusion(f32[2,2,4,96,384]{4,3,0,1,2:T(8,128)} %fusion.6), kind=kLoop, calls=%fused_computation.87 | loop fusion | flops 442368 | bytes 1474560 | tf_op jit(solution)/shard_map/add | solution.py:44
  30.6 1.3 %fusion.60 = bf16[1,4,96,384]{3,2,1,0:T(8,128)(2,1)S(1)} fusion(f32[2,2,4,96,384]{4,3,0,1,2:T(8,128)} %fusion.6), kind=kLoop, calls=%fused_computation.88 | loop fusion | flops 442368 | bytes 1474560 | tf_op jit(solution)/shard_map/sub | solution.py:45
  31.9 0.8 %fusion.44 = f32[2,4,96,2,384]{4,2,3,1,0:T(8,128)S(1)} fusion(bf16[2,384,384,1,1]{2,1,0,4,3:T(8,128)(2,1)S(1)} %bitcast.226, bf16[1,4,96,384]{3,2,1,0:T(8,128)(2,1)S(1)} %fusion.60, bf16[1,4,96,384]{3,2,1,0:T(8,128)(2,1)S(1)} %fusion.59), kind=kOutput, calls=%fused_computation.69 | convolution fusion | flops 454164480 | bytes 3538944 | tf_op jit(solution)/shard_map/dot_general | solution.py:116
  32.7 5.3 %collective-permute-done.3 = bf16[2,96,384]{2,1,0:T(8,128)(2,1)} collective-permute-done((bf16[2,96,384]{2,1,0:T(8,128)(2,1)}, bf16[2,96,384]{2,1,0:T(8,128)(2,1)}, u32[]{:S(2)}, u32[]{:S(2)}) %collective-permute-start.3) | collective-permute-done | bytes 147488 | tf_op jit(solution)/shard_map/ppermute | solution.py:50
  38.0 1.2 %maximum_convert_fusion = f32[4,2,96,384]{3,2,0,1:T(8,128)S(1)} fusion(bf16[1,2,96,384]{3,2,0,1:T(8,128)(2,1)} %bitcast.10, bf16[1,2,96,384]{3,2,0,1:T(8,128)(2,1)} %bitcast.8, bf16[1,2,96,384]{3,2,0,1:T(8,128)(2,1)} %bitcast.6, bf16[1,2,96,384]{3,2,0,1:T(8,128)(2,1)S(1)} %constant_dynamic-slice_fusion.1), kind=kLoop, calls=%fused_computation.62 | loop fusion | flops 1179648 | bytes 1769472 | tf_op jit(solution)/shard_map/convert_element_type | solution.py:123
  39.7 0.4 fusion.36
  40.1 0.5 subtract_bitcast_fusion
  40.6 16.7 %all_gather.3 = bf16[2,384,384]{2,1,0:T(8,128)(2,1)S(1)} all-gather(bf16[2,96,384]{2,1,0:T(8,128)(2,1)S(1)} %pad_maximum_fusion.1), channel_id=1, replica_groups=mesh['grp'=2,'frame'=4,'coil'=4] {'coil'}, dimensions={1}, use_global_device_ids=true | all-gather | bytes 737280 | tf_op jit(solution)/shard_map/all_gather | solution.py:190
  57.3 1.2 %fusion.14 = f32[1,2,384,384]{3,2,1,0:T(8,128)} fusion(f32[1,2,384,384]{3,2,1,0:T(8,128)S(1)} %subtract_bitcast_fusion, bf16[1,2,384,384]{3,2,1,0:T(8,128)(2,1)S(1)} %copy-done, bf16[2,384,384]{2,1,0:T(8,128)(2,1)S(1)} %all_gather.3), kind=kLoop, calls=%fused_computation.17 | loop fusion | flops 1474560 | bytes 3538944 | tf_op jit(solution)/shard_map/sub | solution.py:191
  (39 shorter events, 1.7 us)
Async XLA Ops:
  0.0 1.2 %copy-start = (bf16[1,2,384,384]{3,2,1,0:T(8,128)(2,1)S(1)}, bf16[1,2,384,384]{3,2,1,0:T(8,128)(2,1)}, u32[]{:S(2)}) copy-start(bf16[1,2,384,384]{3,2,1,0:T(8,128)(2,1)} %param.9) | copy-start | bytes 1769476
  1.2 1.1 %copy-start.1 = (bf16[1,2,384,384]{3,2,1,0:T(8,128)(2,1)S(1)}, bf16[1,2,384,384]{3,2,1,0:T(8,128)(2,1)}, u32[]{:S(2)}) copy-start(bf16[1,2,384,384]{3,2,1,0:T(8,128)(2,1)} %param.10) | copy-start | bytes 1769476
  3.5 1.3 %copy-start.4 = (bf16[768,768]{0,1:T(8,128)(2,1)S(1)}, bf16[768,768]{0,1:T(8,128)(2,1)}, u32[]{:S(2)}) copy-start(bf16[768,768]{0,1:T(8,128)(2,1)} %constant.52.clone) | copy-start | bytes 3538948
  5.4 0.7 %copy-start.7 = (s32[1,6]{1,0:T(1,128)S(1)}, s32[1,6]{1,0:T(1,128)}, u32[]{:S(2)}) copy-start(s32[1,6]{1,0:T(1,128)} %param.13) | copy-start | bytes 76
  5.4 1.0 %copy-start.3 = (bf16[16,128,128]{2,1,0:T(8,128)(2,1)S(1)}, bf16[16,128,128]{2,1,0:T(8,128)(2,1)}, u32[]{:S(2)}) copy-start(bf16[16,128,128]{2,1,0:T(8,128)(2,1)} %param.15) | copy-start | bytes 1572868
  5.4 1.0 %copy-start.6 = (s32[1,6]{1,0:T(1,128)S(1)}, s32[1,6]{1,0:T(1,128)}, u32[]{:S(2)}) copy-start(s32[1,6]{1,0:T(1,128)} %param.12) | copy-start | bytes 76
  5.5 2.9 %copy-start.8 = (s32[1,6]{1,0:T(1,128)S(1)}, s32[1,6]{1,0:T(1,128)}, u32[]{:S(2)}) copy-start(s32[1,6]{1,0:T(1,128)} %param.14) | copy-start | bytes 76
  9.2 0.9 %copy-start.2 = (bf16[6,128,384]{2,1,0:T(8,128)(2,1)}, bf16[6,128,384]{2,1,0:T(8,128)(2,1)S(1)}, u32[]{:S(2)}) copy-start(bf16[6,128,384]{2,1,0:T(8,128)(2,1)S(1)} %convolution_convert_fusion.3) | copy-start | bytes 1769476
  9.2 0.9 %copy-start.5 = (f32[1,1,2,6,128]{4,2,3,1,0:T(2,128)S(1)}, f32[1,1,2,6,128]{4,2,3,1,0:T(2,128)}, u32[]{:S(2)}) copy-start(f32[1,1,2,6,128]{4,2,3,1,0:T(2,128)} %param.11) | copy-start | bytes 18436
  10.2 11.8 %collective-permute-start.5 = (f32[2,6,128]{2,0,1:T(2,128)S(1)}, f32[2,6,128]{2,0,1:T(2,128)S(1)}, u32[]{:S(2)}, u32[]{:S(2)}) collective-permute-start(f32[2,6,128]{2,0,1:T(2,128)S(1)} %bitcast_subtract_fusion), channel_id=1, source_target_pairs={{0,1},{1,2},{2,3},{3,0},{4,5},{5,6},{6,7},{7,4},{8,9},{9,10},{10,1... | collective-permute-start | bytes 18440 | tf_op jit(solution)/shard_map/ppermute | solution.py:50
  13.3 9.3 %collective-permute-start.6 = (f32[2,6,128]{2,0,1:T(2,128)S(1)}, f32[2,6,128]{2,0,1:T(2,128)S(1)}, u32[]{:S(2)}, u32[]{:S(2)}) collective-permute-start(f32[2,6,128]{2,0,1:T(2,128)S(1)} %bitcast_subtract_fusion), channel_id=1, source_target_pairs={{0,2},{1,3},{2,0},{3,1},{4,6},{5,7},{6,4},{7,5},{8,10},{9,11},{10,... | collective-permute-start | bytes 18440 | tf_op jit(solution)/shard_map/ppermute | solution.py:50
  15.9 8.2 %collective-permute-start.7 = (f32[2,6,128]{2,0,1:T(2,128)S(1)}, f32[2,6,128]{2,0,1:T(2,128)S(1)}, u32[]{:S(2)}, u32[]{:S(2)}) collective-permute-start(f32[2,6,128]{2,0,1:T(2,128)S(1)} %bitcast_subtract_fusion), channel_id=1, source_target_pairs={{0,3},{1,0},{2,1},{3,2},{4,7},{5,4},{6,5},{7,6},{8,11},{9,8},{10,9... | collective-permute-start | bytes 18440 | tf_op jit(solution)/shard_map/ppermute | solution.py:50
  17.2 22.3 %collective-permute-start = (bf16[2,384,384]{2,1,0:T(8,128)(2,1)S(1)}, bf16[2,384,384]{2,1,0:T(8,128)(2,1)S(1)}, u32[]{:S(2)}, u32[]{:S(2)}) collective-permute-start(bf16[2,384,384]{2,1,0:T(8,128)(2,1)S(1)} %bitcast.223), channel_id=1, source_target_pairs={{0,4},{4,8},{8,12},{1,5},{5,9},{9,13},{2,6},{6,10},{10,14},{3,7},{... | collective-permute-start | bytes 1769480 | tf_op jit(solution)/shard_map/ppermute | solution.py:149
  18.5 21.0 %collective-permute-start.1 = (bf16[2,384,384]{2,1,0:T(8,128)(2,1)S(1)}, bf16[2,384,384]{2,1,0:T(8,128)(2,1)S(1)}, u32[]{:S(2)}, u32[]{:S(2)}) collective-permute-start(bf16[2,384,384]{2,1,0:T(8,128)(2,1)S(1)} %bitcast.224), channel_id=1, source_target_pairs={{4,0},{8,4},{12,8},{5,1},{9,5},{13,9},{6,2},{10,6},{14,10},{7,3},{... | collective-permute-start | bytes 1769480 | tf_op jit(solution)/shard_map/ppermute | solution.py:150
  22.0 10.6 %collective-permute-start.4 = (bf16[2,96,384]{2,1,0:T(8,128)(2,1)}, bf16[2,96,384]{2,1,0:T(8,128)(2,1)}, u32[]{:S(2)}, u32[]{:S(2)}) collective-permute-start(bf16[2,96,384]{2,1,0:T(8,128)(2,1)} %get-tuple-element.17), channel_id=1, source_target_pairs={{0,3},{1,0},{2,1},{3,2},{4,7},{5,4},{6,5},{7,6},{8,11},{9,8},{10,9... | collective-permute-start | bytes 442376 | tf_op jit(solution)/shard_map/ppermute | solution.py:50
  22.5 10.1 %collective-permute-start.2 = (bf16[2,96,384]{2,1,0:T(8,128)(2,1)}, bf16[2,96,384]{2,1,0:T(8,128)(2,1)}, u32[]{:S(2)}, u32[]{:S(2)}) collective-permute-start(bf16[2,96,384]{2,1,0:T(8,128)(2,1)} %get-tuple-element.15), channel_id=1, source_target_pairs={{0,1},{1,2},{2,3},{3,0},{4,5},{5,6},{6,7},{7,4},{8,9},{9,10},{10,1... | collective-permute-start | bytes 442376 | tf_op jit(solution)/shard_map/ppermute | solution.py:50
  24.1 13.9 %collective-permute-start.3 = (bf16[2,96,384]{2,1,0:T(8,128)(2,1)}, bf16[2,96,384]{2,1,0:T(8,128)(2,1)}, u32[]{:S(2)}, u32[]{:S(2)}) collective-permute-start(bf16[2,96,384]{2,1,0:T(8,128)(2,1)} %get-tuple-element.16), channel_id=1, source_target_pairs={{0,2},{1,3},{2,0},{3,1},{4,6},{5,7},{6,4},{7,5},{8,10},{9,11},{10,... | collective-permute-start | bytes 442376 | tf_op jit(solution)/shard_map/ppermute | solution.py:50

commit v8 on v6

--- a/solution.py
+++ b/solution.py
@@ -56,6 +56,41 @@
         block = lax.dynamic_slice_in_dim(coil_map, target * rows, rows, axis=1)
         received.append(rotated(block, coil_count, shift))
     return jnp.stack(received)
+
+
+def exchange_all(image, coil_map, rows, coil_count, coil_index, frame_count):
+    extent = image.shape[-1]
+
+    def flat(f, c):
+        return f * coil_count + c
+
+    def block_for(shift):
+        target = (coil_index + shift) % coil_count
+        return lax.dynamic_slice_in_dim(coil_map, target * rows, rows, axis=1)
+
+    def carried(frame_step, coil_step):
+        pairs = [
+            (flat(f, c), flat((f + frame_step) % frame_count, (c + coil_step) % coil_count))
+            for f in range(frame_count)
+            for c in range(coil_count)
+        ]
+        payload = jnp.concatenate([image, block_for(coil_step % coil_count)], axis=1)
+        moved = lax.ppermute(payload, ("frame", "coil"), pairs)
+        return moved[:, :extent], moved[:, extent:]
+
+    received = [None] * coil_count
+    received[0] = block_for(0)
+    earlier, received[1] = carried(1, 1)
+    later, received[coil_count - 1] = carried(-1, -1)
+    for shift in range(2, coil_count - 1):
+        received[shift] = rotated(block_for(shift), coil_count, shift)
+    return earlier, later, jnp.stack(received)
+
+
+def tv_from(image, earlier, later, frame_index, frame_total):
+    has_earlier = (frame_index >= 1).astype(jnp.float32)
+    has_later = (frame_index <= frame_total - 2).astype(jnp.float32)
+    return (normed_change(image, earlier, has_earlier) - normed_change(later, image, has_later))[None]
 
 
 def selector(first_index, extent, patch_side):
@@ -142,9 +177,7 @@
     later = lax.ppermute(image, "frame", [(i + 1, i) for i in range(count - 1)])
     has_earlier = (frame_index >= 1).astype(jnp.float32)
     has_later = (frame_index <= frame_total - 2).astype(jnp.float32)
-    return (
-        normed_change(image, earlier, has_earlier) - normed_change(later, image, has_later)
-    )[None]
+    return (normed_change(image, earlier, has_earlier) - normed_change(later, image, has_later))[None]
 
 
 def body(
@@ -157,13 +190,20 @@
     coil_index = lax.axis_index("coil")
     rows = extent // coil_count
     transform = transform_table(extent)
-    map_rows = exchange_rows(coil_maps[0], rows, coil_count, coil_index)
     first_frame = lax.axis_index("frame") * frame_count
     frame_total = lax.axis_size("frame") * frame_count
-    if frame_count == 1:
-        tv_grad = tv_single(images, first_frame, frame_total)
+    if frame_count == 1 and coil_count >= 3:
+        earlier, later, map_rows = exchange_all(
+            images[0], coil_maps[0], rows, coil_count, coil_index,
+            lax.axis_size("frame"),
+        )
+        tv_grad = tv_from(images[0], earlier, later, first_frame, frame_total)
     else:
-        tv_grad = tv_term(padded(images, (("frame", 0),), 1), first_frame, frame_total)
+        map_rows = exchange_rows(coil_maps[0], rows, coil_count, coil_index)
+        if frame_count == 1:
+            tv_grad = tv_single(images, first_frame, frame_total)
+        else:
+            tv_grad = tv_term(padded(images, (("frame", 0),), 1), first_frame, frame_total)
     row_w = pick_kernels(kernel_rows, spoke_angle[0])
     col_w = pick_kernels(kernel_cols, spoke_angle[0])
     row_select = selector(band_row[0], extent, patch_side)
@@ -174,8 +214,9 @@
     residual = forward_residual(
         transform, images[0], coil_maps[0], kspace_data[0, 0], row_placed, col_placed
     )
-    moved = [rotated(residual, coil_count, shift) for shift in range(1, coil_count)]
-    residuals = jnp.stack([residual] + moved)
+    residuals = jnp.stack(
+        [residual] + [rotated(residual, coil_count, shift) for shift in range(1, coil_count)]
+    )
     grad_rows = backward_rows(
         transform, residuals, map_rows, row_select, row_w, col_placed, coil_index
     )

time: 58.7 us -> 80.1 us (1.36)
  waiting for transfers between devices: 4.77 us -> 28 us
  starting transfers between devices: 11.9 us -> 8.92 us
  matrix products: 10.6 us -> 13.5 us
  other arithmetic: 10.4 us -> 9.18 us
    ppermute x2, waiting for transfers between devices: 0.01 us -> 22.3 us  [carried(): moved = lax.ppermute(payload, ('frame', 'coil'), pairs)]
    dot_general x1, matrix products: 1.1 us -> 3.49 us  [backward_rows(): jnp.einsum('cpgrj,gjk->cpgrk', spread, col_placed, preferred_element_type...]
    ppermute x6 -> x4, starting transfers between devices: 9.25 us -> 7.18 us  [rotated(): lax.ppermute(block, 'coil', [(i, (i + shift) % coil_count) for i in range...]
    sub x2 -> x1, other arithmetic: 1.37 us -> 0.06 us  [combine_parts(): imaginary = products[0, 1] - direction * products[1, 0]]
    concatenate x0 -> x1, other arithmetic: none -> 1.23 us  [carried(): jnp.concatenate([image, block_for(coil_step % coil_count)], axis=1)]
    ppermute x6 -> x4, waiting for transfers between devices: 4.76 us -> 5.73 us  [rotated(): lax.ppermute(block, 'coil', [(i, (i + shift) % coil_count) for i in range...]
    ppermute x2, starting transfers between devices: 2.61 us -> 1.75 us  [carried(): moved = lax.ppermute(payload, ('frame', 'coil'), pairs)]
  transfers between devices with their start and end apart: 8 -> 6, of which waited for: 1 -> 3; matrix products, arithmetic and copies ran while one was open for 22% -> 17% of each run, Pallas kernels for 0% -> 0%
where the time goes in v8:
time: 80.1 us; the launch traced here: 79.8 us
  waiting for transfers between devices  28 us (35%)
  blocking collectives  16.3 us (20%)
  matrix products  13.5 us (17%)
  other arithmetic  9.18 us (11%)
  starting transfers between devices  8.92 us (11%)
  local copies, waits for them, and re-layouts  3.64 us (5%)
    ppermute x2, waiting for transfers between devices, carried(): moved = lax.ppermute(payload, ('frame', 'coil'), pairs)  22.3 us
    all_gather x1, blocking collectives, body(): lax.all_gather(grad_rows, 'coil', axis=1, tiled=True).astype(jnp.float32)  16.3 us
    ppermute x4, starting transfers between devices, rotated(): lax.ppermute(block, 'coil', [(i, (i + shift) % coil_count) for i in range...  7.18 us
    ppermute x4, waiting for transfers between devices, rotated(): lax.ppermute(block, 'coil', [(i, (i + shift) % coil_count) for i in range...  5.73 us
    dot_general x1, matrix products, backward_rows(): jnp.einsum('aigr,cbgrk->abcik', table_at, placed, preferred_element_type=...  5.15 us
    dot_general x1, matrix products, backward_rows(): jnp.einsum('cpgrj,gjk->cpgrk', spread, col_placed, preferred_element_type...  3.49 us
    unnamed x24, local copies, waits for them, and re-layouts  2.74 us
    add x2, other arithmetic, combine_parts(): real_part = products[0, 0] + direction * products[1, 1]  1.86 us
  transfers between devices with their start and end apart: 6, of which 3 were waited for; matrix products, arithmetic and copies ran while one was open for 17% of the time, Pallas kernels for 0%

profile of v8, /device:TPU:0, one launch (start us, length us, event | category | flops | bytes accessed | tf_op | source)
XLA Modules:
  0.0 79.8 jit_solution(2644204095758025588)
XLA Ops:
  0.0 1.2 %bitcast_convert_fusion.1 = f32[2,384,384]{2,1,0:T(8,128)S(1)} fusion(bf16[1,2,384,384]{3,2,1,0:T(8,128)(2,1)} %param.9), kind=kLoop, calls=%fused_computation.126 | loop fusion | flops 294912 | bytes 1769472 | tf_op jit(solution)/shard_map/convert_element_type | solution.py:168
  1.5 0.9 %copy-done.5 = bf16[2,384,384,1]{2,1,0,3:T(8,128)(2,1)S(1)} copy-done((bf16[2,384,384,1]{2,1,0,3:T(8,128)(2,1)S(1)}, bf16[2,384,384,1]{2,1,0,3:T(8,128)(2,1)}, u32[]{:S(2)}) %copy-start.5) | copy-done | bytes 589848
  2.4 0.8 convolution_bitcast_fusion.1
  3.3 0.9 %copy-done.2 = bf16[2,384,384]{2,1,0:T(8,128)(2,1)S(1)} copy-done((bf16[2,384,384]{2,1,0:T(8,128)(2,1)S(1)}, bf16[2,384,384]{2,1,0:T(8,128)(2,1)}, u32[]{:S(2)}) %copy-start.2) | copy-done | bytes 589848
  4.4 0.5 copy-done.10
  5.0 0.3 copy-done.6
  5.3 0.4 fusion.23
  5.7 0.4 fusion.22
  6.3 0.4 fusion.17
  6.7 0.4 convolution_convert_fusion.3
  7.1 0.8 convolution_convert_fusion.2
  7.9 0.9 %fusion.2 = f32[2,6,128]{2,0,1:T(2,128)S(1)} fusion(bf16[2,384,384,1]{2,1,0,3:T(8,128)(2,1)S(1)} %bitcast.209, f32[6,384,128]{1,2,0:T(8,128)S(1)} %fusion.17, bf16[6,128,384]{2,1,0:T(8,128)(2,1)S(1)} %convolution_convert_fusion.3), kind=kOutput, calls=%fused_computation.7 | convolution fusion | flops 454162944 | bytes 2365440 | tf_op jit(solution)/shard_map/pik,gjk->pgij/dot_general | solution.py:131
  8.8 0.6 bitcast_subtract_fusion
  9.4 3.1 %collective-permute-start.3 = (f32[2,6,128]{2,0,1:T(2,128)}, f32[2,6,128]{2,0,1:T(2,128)S(1)}, u32[]{:S(2)}, u32[]{:S(2)}) collective-permute-start(f32[2,6,128]{2,0,1:T(2,128)} %bitcast_subtract_fusion), channel_id=1, source_target_pairs={{0,1},{1,2},{2,3},{3,0},{4,5},{5,6},{6,7},{7,4},{8,9},{9,10},{10,1... | collective-permute-start | bytes 18440 | tf_op jit(solution)/shard_map/ppermute | solution.py:49
  12.5 2.6 %collective-permute-start.4 = (f32[2,6,128]{2,0,1:T(2,128)}, f32[2,6,128]{2,0,1:T(2,128)S(1)}, u32[]{:S(2)}, u32[]{:S(2)}) collective-permute-start(f32[2,6,128]{2,0,1:T(2,128)} %bitcast_subtract_fusion), channel_id=1, source_target_pairs={{0,2},{1,3},{2,0},{3,1},{4,6},{5,7},{6,4},{7,5},{8,10},{9,11},{10,... | collective-permute-start | bytes 18440 | tf_op jit(solution)/shard_map/ppermute | solution.py:49
  15.1 1.3 %collective-permute-start.5 = (f32[2,6,128]{2,0,1:T(2,128)}, f32[2,6,128]{2,0,1:T(2,128)S(1)}, u32[]{:S(2)}, u32[]{:S(2)}) collective-permute-start(f32[2,6,128]{2,0,1:T(2,128)} %bitcast_subtract_fusion), channel_id=1, source_target_pairs={{0,3},{1,0},{2,1},{3,2},{4,7},{5,4},{6,5},{7,6},{8,11},{9,8},{10,9... | collective-permute-start | bytes 18440 | tf_op jit(solution)/shard_map/ppermute | solution.py:49
  16.4 0.8 %constant_dynamic-slice_fusion = (bf16[1,2,96,384]{3,2,1,0:T(8,128)(2,1)}, bf16[2,96,384]{2,1,0:T(8,128)(2,1)S(1)}, bf16[2,96,384]{2,1,0:T(8,128)(2,1)S(1)}, bf16[2,96,384]{2,1,0:T(8,128)(2,1)}) fusion(bf16[1,2,384,384]{3,2,1,0:T(8,128)(2,1)S(1)} %copy-done.1, s32[]{:T(128)S(6)} %select_n.39, s32[]{:T(128)S(6)} %select_n.37, s32[]{:T(128)S(6)} %select_n.35, ...), kind=kLoop, calls=%fused_computation.122 | loop fusion | bytes 1179664 | tf_op jit(solution)/shard_map/dynamic_slice | solution.py:69
  17.2 1.2 %pad_maximum_fusion = (bf16[2,480,384]{2,1,0:T(8,128)(2,1)}, bf16[2,480,384]{2,1,0:T(8,128)(2,1)}) fusion(bf16[2,96,384]{2,1,0:T(8,128)(2,1)S(1)} %get-tuple-element.19, bf16[2,384,384]{2,1,0:T(8,128)(2,1)S(1)} %bitcast.196, bf16[2,96,384]{2,1,0:T(8,128)(2,1)S(1)} %get-tuple-element.18), kind=kLoop, calls=%fused_computation.35 | loop fusion | flops 2580480 | bytes 2359296 | tf_op jit(solution)/shard_map/concatenate | solution.py:77
  18.4 1.7 %collective-permute-start = (bf16[2,480,384]{2,1,0:T(8,128)(2,1)}, bf16[2,480,384]{2,1,0:T(8,128)(2,1)S(1)}, u32[]{:S(2)}, u32[]{:S(2)}) collective-permute-start(bf16[2,480,384]{2,1,0:T(8,128)(2,1)} %get-tuple-element.23), channel_id=1, source_target_pairs={{0,5},{1,6},{2,7},{3,4},{4,9},{5,10},{6,11},{7,8},{8,13},{9,14},{1... | collective-permute-start | bytes 2211848 | tf_op jit(solution)/shard_map/ppermute | solution.py:78
  20.5 3.5 %convert_bitcast_fusion = bf16[4,2,6,128,384,1]{4,3,2,1,0,5:T(8,128)(2,1)} fusion(f32[4,2,6,128]{3,2,1,0:T(8,128)S(1)} %copy.14, f32[6,128,128]{2,1,0:T(8,128)S(1)} %bitcast_convert_fusion, bf16[6,128,384]{2,1,0:T(8,128)(2,1)S(1)} %convolution_convert_fusion.3), kind=kOutput, calls=%fused_computation.4 | convolution fusion | flops 607911936 | bytes 5726208 | tf_op jit(solution)/shard_map/cpgrj,gjk->cpgrk/dot_general | solution.py:139
  24.0 5.1 %fusion.3 = f32[2,2,4,96,384]{4,3,2,1,0:T(8,128)} fusion(bf16[4,2,6,128,384,1]{4,3,2,1,0,5:T(8,128)(2,1)} %convert_bitcast_fusion, s32[6,128]{1,0:T(8,128)S(1)} %iota_add_fusion, bf16[2,384,384]{2,1,0:T(8,128)(2,1)} %constant.56.clone, s32[]{:T(128)S(6)} %select_n.42), kind=kOutput, calls=%fused_computation.8 | convolution fusion | flops 1019658240 | bytes 7228420 | tf_op jit(solution)/shard_map/aigr,cbgrk->abcik/dot_general | solution.py:146
  29.1 1.8 %fusion.60 = (bf16[1,4,96,384]{3,2,1,0:T(8,128)(2,1)S(1)}, bf16[1,4,96,384]{3,2,1,0:T(8,128)(2,1)S(1)}) fusion(f32[2,2,4,96,384]{4,3,2,1,0:T(8,128)} %fusion.3), kind=kLoop, calls=%fused_computation.94 | loop fusion | flops 884736 | bytes 2949120 | tf_op jit(solution)/shard_map/add | solution.py:43
  30.9 0.8 convolution_bitcast_fusion
  31.7 21.3 %collective-permute-done.1 = bf16[2,480,384]{2,1,0:T(8,128)(2,1)S(1)} collective-permute-done((bf16[2,480,384]{2,1,0:T(8,128)(2,1)}, bf16[2,480,384]{2,1,0:T(8,128)(2,1)S(1)}, u32[]{:S(2)}, u32[]{:S(2)}) %collective-permute-start.1) | collective-permute-done | bytes 737312 | tf_op jit(solution)/shard_map/ppermute | solution.py:78
  53.0 1.0 %collective-permute-done = bf16[2,480,384]{2,1,0:T(8,128)(2,1)S(1)} collective-permute-done((bf16[2,480,384]{2,1,0:T(8,128)(2,1)}, bf16[2,480,384]{2,1,0:T(8,128)(2,1)S(1)}, u32[]{:S(2)}, u32[]{:S(2)}) %collective-permute-start) | collective-permute-done | bytes 737312 | tf_op jit(solution)/shard_map/ppermute | solution.py:78
  54.1 5.7 %collective-permute-done.2 = bf16[2,96,384]{2,1,0:T(8,128)(2,1)} collective-permute-done((bf16[2,96,384]{2,1,0:T(8,128)(2,1)}, bf16[2,96,384]{2,1,0:T(8,128)(2,1)}, u32[]{:S(2)}, u32[]{:S(2)}) %collective-permute-start.2) | collective-permute-done | bytes 147488 | tf_op jit(solution)/shard_map/ppermute | solution.py:49
  59.8 1.0 %maximum_convert_fusion = f32[4,2,96,384]{3,2,1,0:T(8,128)S(1)} fusion(bf16[1,2,96,384]{3,2,1,0:T(8,128)(2,1)S(1)} %slice_bitcast_fusion.8, bf16[1,2,96,384]{3,2,1,0:T(8,128)(2,1)} %bitcast.8, bf16[1,2,96,384]{3,2,1,0:T(8,128)(2,1)S(1)} %slice_bitcast_fusion.9, bf16[1,2,96,384]{3,2,1,0:T(8,128)(2,1)S(1)} %copy-done.3), kind=kLoop, calls=%fused_computation.71 | loop fusion | flops 1179648 | bytes 1769472 | tf_op jit(solution)/shard_map/convert_element_type | solution.py:150
  60.8 0.3 add_reduce_fusion
  61.4 0.4 fusion.38
  61.8 0.4 subtract_bitcast_fusion
  62.2 16.3 %all_gather.3 = bf16[2,384,384]{2,1,0:T(8,128)(2,1)S(1)} all-gather(bf16[2,96,384]{2,1,0:T(8,128)(2,1)S(1)} %pad_maximum_fusion.3), channel_id=1, replica_groups=mesh['grp'=2,'frame'=4,'coil'=4] {'coil'}, dimensions={1}, use_global_device_ids=true | all-gather | bytes 737280 | tf_op jit(solution)/shard_map/all_gather | solution.py:224
  78.5 1.3 %fusion.15 = f32[1,2,384,384]{3,2,1,0:T(8,128)} fusion(f32[1,2,384,384]{3,2,1,0:T(8,128)S(1)} %subtract_bitcast_fusion, bf16[1,2,384,384]{3,2,1,0:T(8,128)(2,1)S(1)} %copy-done, bf16[2,384,384]{2,1,0:T(8,128)(2,1)S(1)} %all_gather.3), kind=kLoop, calls=%fused_computation.24 | loop fusion | flops 1474560 | bytes 3538944 | tf_op jit(solution)/shard_map/sub | solution.py:225
  (42 shorter events, 1.3 us)
Async XLA Ops:
  0.0 1.2 %copy-start.1 = (bf16[1,2,384,384]{3,2,1,0:T(8,128)(2,1)S(1)}, bf16[1,2,384,384]{3,2,1,0:T(8,128)(2,1)}, u32[]{:S(2)}) copy-start(bf16[1,2,384,384]{3,2,1,0:T(8,128)(2,1)} %param.10) | copy-start | bytes 1769476
  1.3 1.1 %copy-start.5 = (bf16[2,384,384,1]{2,1,0,3:T(8,128)(2,1)S(1)}, bf16[2,384,384,1]{2,1,0,3:T(8,128)(2,1)}, u32[]{:S(2)}) copy-start(bf16[2,384,384,1]{2,1,0,3:T(8,128)(2,1)} %constant.63) | copy-start | bytes 1769476
  3.2 1.1 %copy-start.2 = (bf16[2,384,384]{2,1,0:T(8,128)(2,1)S(1)}, bf16[2,384,384]{2,1,0:T(8,128)(2,1)}, u32[]{:S(2)}) copy-start(bf16[2,384,384]{2,1,0:T(8,128)(2,1)} %constant.56.clone) | copy-start | bytes 1769476
  4.2 0.7 copy-start.10
  4.2 1.1 %copy-start.6 = (bf16[16,128,128]{2,1,0:T(8,128)(2,1)S(1)}, bf16[16,128,128]{2,1,0:T(8,128)(2,1)}, u32[]{:S(2)}) copy-start(bf16[16,128,128]{2,1,0:T(8,128)(2,1)} %param.15) | copy-start | bytes 1572868
  4.2 1.1 %copy-start.9 = (s32[1,6]{1,0:T(1,128)S(1)}, s32[1,6]{1,0:T(1,128)}, u32[]{:S(2)}) copy-start(s32[1,6]{1,0:T(1,128)} %param.12) | copy-start | bytes 76
  4.2 1.5 %copy-start.7 = (bf16[16,128,128]{2,1,0:T(8,128)(2,1)S(1)}, bf16[16,128,128]{2,1,0:T(8,128)(2,1)}, u32[]{:S(2)}) copy-start(bf16[16,128,128]{2,1,0:T(8,128)(2,1)} %param.16) | copy-start | bytes 1572868
  4.3 1.8 %copy-start.11 = (s32[1,6]{1,0:T(1,128)S(1)}, s32[1,6]{1,0:T(1,128)}, u32[]{:S(2)}) copy-start(s32[1,6]{1,0:T(1,128)} %param.14) | copy-start | bytes 76
  7.9 0.9 %copy-start.8 = (f32[1,1,2,6,128]{4,2,3,1,0:T(2,128)S(1)}, f32[1,1,2,6,128]{4,2,3,1,0:T(2,128)}, u32[]{:S(2)}) copy-start(f32[1,1,2,6,128]{4,2,3,1,0:T(2,128)} %param.11) | copy-start | bytes 18436
  8.8 8.4 %copy-start = (bf16[1,2,384,384]{3,2,1,0:T(8,128)(2,1)S(1)}, bf16[1,2,384,384]{3,2,1,0:T(8,128)(2,1)}, u32[]{:S(2)}) copy-start(bf16[1,2,384,384]{3,2,1,0:T(8,128)(2,1)} %param.9) | copy-start | bytes 1769476
  9.4 10.8 %collective-permute-start.3 = (f32[2,6,128]{2,0,1:T(2,128)}, f32[2,6,128]{2,0,1:T(2,128)S(1)}, u32[]{:S(2)}, u32[]{:S(2)}) collective-permute-start(f32[2,6,128]{2,0,1:T(2,128)} %bitcast_subtract_fusion), channel_id=1, source_target_pairs={{0,1},{1,2},{2,3},{3,0},{4,5},{5,6},{6,7},{7,4},{8,9},{9,10},{10,1... | collective-permute-start | bytes 18440 | tf_op jit(solution)/shard_map/ppermute | solution.py:49
  12.5 8.0 %collective-permute-start.4 = (f32[2,6,128]{2,0,1:T(2,128)}, f32[2,6,128]{2,0,1:T(2,128)S(1)}, u32[]{:S(2)}, u32[]{:S(2)}) collective-permute-start(f32[2,6,128]{2,0,1:T(2,128)} %bitcast_subtract_fusion), channel_id=1, source_target_pairs={{0,2},{1,3},{2,0},{3,1},{4,6},{5,7},{6,4},{7,5},{8,10},{9,11},{10,... | collective-permute-start | bytes 18440 | tf_op jit(solution)/shard_map/ppermute | solution.py:49
  15.1 5.4 %collective-permute-start.5 = (f32[2,6,128]{2,0,1:T(2,128)}, f32[2,6,128]{2,0,1:T(2,128)S(1)}, u32[]{:S(2)}, u32[]{:S(2)}) collective-permute-start(f32[2,6,128]{2,0,1:T(2,128)} %bitcast_subtract_fusion), channel_id=1, source_target_pairs={{0,3},{1,0},{2,1},{3,2},{4,7},{5,4},{6,5},{7,6},{8,11},{9,8},{10,9... | collective-permute-start | bytes 18440 | tf_op jit(solution)/shard_map/ppermute | solution.py:49
  18.4 34.5 %collective-permute-start.1 = (bf16[2,480,384]{2,1,0:T(8,128)(2,1)}, bf16[2,480,384]{2,1,0:T(8,128)(2,1)S(1)}, u32[]{:S(2)}, u32[]{:S(2)}) collective-permute-start(bf16[2,480,384]{2,1,0:T(8,128)(2,1)} %get-tuple-element.24), channel_id=1, source_target_pairs={{0,15},{1,12},{2,13},{3,14},{4,3},{5,0},{6,1},{7,2},{8,7},{9,4},{1... | collective-permute-start | bytes 2211848 | tf_op jit(solution)/shard_map/ppermute | solution.py:78
  18.4 35.6 %collective-permute-start = (bf16[2,480,384]{2,1,0:T(8,128)(2,1)}, bf16[2,480,384]{2,1,0:T(8,128)(2,1)S(1)}, u32[]{:S(2)}, u32[]{:S(2)}) collective-permute-start(bf16[2,480,384]{2,1,0:T(8,128)(2,1)} %get-tuple-element.23), channel_id=1, source_target_pairs={{0,5},{1,6},{2,7},{3,4},{4,9},{5,10},{6,11},{7,8},{8,13},{9,14},{1... | collective-permute-start | bytes 2211848 | tf_op jit(solution)/shard_map/ppermute | solution.py:78
  20.3 39.5 %collective-permute-start.2 = (bf16[2,96,384]{2,1,0:T(8,128)(2,1)}, bf16[2,96,384]{2,1,0:T(8,128)(2,1)}, u32[]{:S(2)}, u32[]{:S(2)}) collective-permute-start(bf16[2,96,384]{2,1,0:T(8,128)(2,1)} %get-tuple-element.20), channel_id=1, source_target_pairs={{0,2},{1,3},{2,0},{3,1},{4,6},{5,7},{6,4},{7,5},{8,10},{9,11},{10,... | collective-permute-start | bytes 442376 | tf_op jit(solution)/shard_map/ppermute | solution.py:49
  29.1 1.8 %copy-start.4 = (bf16[2,384,384,1,1]{2,1,4,3,0:T(8,128)(2,1)S(1)}, bf16[2,384,384,1,1]{2,1,4,3,0:T(8,128)(2,1)}, u32[]{:S(2)}) copy-start(bf16[2,384,384,1,1]{2,1,4,3,0:T(8,128)(2,1)} %constant.64) | copy-start | bytes 1769476
  30.9 28.8 %copy-start.3 = (bf16[1,2,96,384]{3,2,1,0:T(8,128)(2,1)S(1)}, bf16[1,2,96,384]{3,2,1,0:T(8,128)(2,1)}, u32[]{:S(2)}) copy-start(bf16[1,2,96,384]{3,2,1,0:T(8,128)(2,1)} %get-tuple-element.17) | copy-start | bytes 442372

commit v9 on v6

--- a/solution.py
+++ b/solution.py
@@ -100,16 +100,23 @@
 
 def backward_rows(transform, residuals, map_rows, row_select, row_w, col_placed, coil_index):
     rows = map_rows.shape[2]
-    spread = (row_w.astype(jnp.float32)[None, None] * residuals[:, :, :, None, :]).astype(jnp.bfloat16)
-    placed = jnp.einsum(
-        "cpgrj,gjk->cpgrk", spread, col_placed, preferred_element_type=jnp.float32
-    ).astype(jnp.bfloat16)
     row_table = lax.dynamic_slice_in_dim(transform, coil_index * rows, rows, axis=1)
     table_at = jnp.einsum(
         "aij,gjr->aigr", row_table, row_select, preferred_element_type=jnp.float32
     ).astype(jnp.bfloat16)
-    products = jnp.einsum("aigr,cbgrk->abcik", table_at, placed, preferred_element_type=jnp.float32)
-    half_back = combine_parts(products, -1.0).astype(jnp.bfloat16)
+    halves = []
+    for source in range(residuals.shape[0]):
+        spread = (row_w.astype(jnp.float32)[None] * residuals[source][:, :, None, :]).astype(
+            jnp.bfloat16
+        )
+        placed = jnp.einsum(
+            "pgrj,gjk->pgrk", spread, col_placed, preferred_element_type=jnp.float32
+        ).astype(jnp.bfloat16)
+        products = jnp.einsum(
+            "aigr,bgrk->abik", table_at, placed, preferred_element_type=jnp.float32
+        )
+        halves.append(combine_parts(products, -1.0).astype(jnp.bfloat16))
+    half_back = jnp.stack(halves, axis=1)
     products = jnp.einsum("bcij,ajk->abcik", half_back, transform, preferred_element_type=jnp.float32)
     coil_back = combine_parts(products, -1.0)
     maps = map_rows.astype(jnp.float32)
@@ -142,9 +149,7 @@
     later = lax.ppermute(image, "frame", [(i + 1, i) for i in range(count - 1)])
     has_earlier = (frame_index >= 1).astype(jnp.float32)
     has_later = (frame_index <= frame_total - 2).astype(jnp.float32)
-    return (
-        normed_change(image, earlier, has_earlier) - normed_change(later, image, has_later)
-    )[None]
+    return (normed_change(image, earlier, has_earlier) - normed_change(later, image, has_later))[None]
 
 
 def body(
@@ -174,8 +179,9 @@
     residual = forward_residual(
         transform, images[0], coil_maps[0], kspace_data[0, 0], row_placed, col_placed
     )
-    moved = [rotated(residual, coil_count, shift) for shift in range(1, coil_count)]
-    residuals = jnp.stack([residual] + moved)
+    residuals = jnp.stack(
+        [residual] + [rotated(residual, coil_count, shift) for shift in range(1, coil_count)]
+    )
     grad_rows = backward_rows(
         transform, residuals, map_rows, row_select, row_w, col_placed, coil_index
     )

time: 58.7 us -> 66.5 us (1.13)
  matrix products: 10.6 us -> 13.6 us
  local copies, waits for them, and re-layouts: 3.6 us -> 5.49 us
  other arithmetic: 10.4 us -> 12.1 us
  waiting for transfers between devices: 4.77 us -> 5.91 us
    another operation x2 -> x5, other arithmetic: 0.91 us -> 6.77 us  [the longest x1 0.74 us: body(): residuals = jnp.stack([residual] + moved)]
    dot_general x1 -> x4, matrix products: 4.72 us -> 6.21 us  [backward_rows(): jnp.einsum('aigr,bgrk->abik', table_at, placed, preferred_element_type=jn...]
    add x2 -> x1, other arithmetic: 1.43 us -> 0.06 us  [combine_parts(): real_part = products[0, 0] + direction * products[1, 1]]
    sub x2 -> x1, other arithmetic: 1.37 us -> 0.06 us  [combine_parts(): imaginary = products[0, 1] - direction * products[1, 0]]
    dot_general x1, matrix products: 0.77 us -> 2.06 us  [backward_rows(): jnp.einsum('bcij,ajk->abcik', half_back, transform, preferred_element_typ...]
    ppermute x6, waiting for transfers between devices: 4.76 us -> 5.9 us  [rotated(): lax.ppermute(block, 'coil', [(i, (i + shift) % coil_count) for i in range...]
    dynamic_slice x1, local copies, waits for them, and re-layouts: 0.78 us -> 1.83 us  [exchange_rows(): block = lax.dynamic_slice_in_dim(coil_map, target * rows, rows, axis=1)]
    dynamic_slice x1, local copies, waits for them, and re-layouts: 0.02 us -> 0.93 us  [exchange_rows(): lax.dynamic_slice_in_dim(coil_map, coil_index * rows, rows, axis=1)]
  transfers between devices with their start and end apart: 8 -> 8, of which waited for: 1 -> 1; matrix products, arithmetic and copies ran while one was open for 22% -> 31% of each run, Pallas kernels for 0% -> 0%
where the time goes in v9:
time: 66.5 us; the launch traced here: 66 us
  blocking collectives  16.7 us (25%)
  matrix products  13.6 us (20%)
  other arithmetic  12.1 us (18%)
  starting transfers between devices  11.9 us (18%)
  waiting for transfers between devices  5.91 us (9%)
  local copies, waits for them, and re-layouts  5.49 us (8%)
    all_gather x1, blocking collectives, body(): lax.all_gather(grad_rows, 'coil', axis=1, tiled=True).astype(jnp.float32)  16.7 us
    ppermute x6, starting transfers between devices, rotated(): lax.ppermute(block, 'coil', [(i, (i + shift) % coil_count) for i in range...  9.32 us
    another operation x5, other arithmetic  6.77 us
    dot_general x4, matrix products, backward_rows(): jnp.einsum('aigr,bgrk->abik', table_at, placed, preferred_element_type=jn...  6.21 us
    ppermute x6, waiting for transfers between devices, rotated(): lax.ppermute(block, 'coil', [(i, (i + shift) % coil_count) for i in range...  5.9 us
    unnamed x20, local copies, waits for them, and re-layouts  2.67 us
    dot_general x1, matrix products, backward_rows(): jnp.einsum('bcij,ajk->abcik', half_back, transform, preferred_element_typ...  2.06 us
    dynamic_slice x1, local copies, waits for them, and re-layouts, exchange_rows(): block = lax.dynamic_slice_in_dim(coil_map, target * rows, rows, axis=1)  1.83 us
  transfers between devices with their start and end apart: 8, of which 1 were waited for; matrix products, arithmetic and copies ran while one was open for 31% of the time, Pallas kernels for 0%

profile of v9, /device:TPU:0, one launch (start us, length us, event | category | flops | bytes accessed | tf_op | source)
XLA Modules:
  0.0 66.0 jit_solution(6796103615269285315)
XLA Ops:
  0.0 1.2 %bitcast_convert_fusion.1 = f32[2,384,384]{2,1,0:T(8,128)S(1)} fusion(bf16[1,2,384,384]{3,2,1,0:T(8,128)(2,1)} %param.9), kind=kLoop, calls=%fused_computation.156 | loop fusion | flops 294912 | bytes 1769472 | tf_op jit(solution)/shard_map/convert_element_type | solution.py:140
  1.5 0.9 %copy-done.3 = bf16[2,384,384,1]{2,1,0,3:T(8,128)(2,1)S(1)} copy-done((bf16[2,384,384,1]{2,1,0,3:T(8,128)(2,1)S(1)}, bf16[2,384,384,1]{2,1,0,3:T(8,128)(2,1)}, u32[]{:S(2)}) %copy-start.3) | copy-done | bytes 589848
  2.4 0.8 %convolution_bitcast_fusion.1 = f32[2,2,384,384]{3,2,0,1:T(8,128)S(1)} fusion(bf16[2,384,384,1]{2,1,0,3:T(8,128)(2,1)S(1)} %copy-done.3, bf16[1,384,384]{2,1,0:T(8,128)(2,1)S(1)} %get-tuple-element.12, bf16[1,384,384]{2,1,0:T(8,128)(2,1)S(1)} %get-tuple-element.11), kind=kOutput, calls=%fused_computation.5 | convolution fusion | flops 454164480 | bytes 3538944 | tf_op jit(solution)/shard_map/bij,ajk->abik/dot_general | solution.py:84
  3.3 0.9 %copy-done.2 = bf16[2,384,384]{2,1,0:T(8,128)(2,1)S(1)} copy-done((bf16[2,384,384]{2,1,0:T(8,128)(2,1)S(1)}, bf16[2,384,384]{2,1,0:T(8,128)(2,1)}, u32[]{:S(2)}) %copy-start.2) | copy-done | bytes 589848
  4.4 0.5 copy-done.8
  7.0 0.8 %convolution_convert_fusion.6 = bf16[768,384]{1,0:T(8,128)(2,1)S(1)} fusion(bf16[768,384]{1,0:T(8,128)(2,1)S(1)} %bitcast.260, bf16[384,384]{1,0:T(8,128)(2,1)S(1)} %get-tuple-element.22, bf16[384,384]{1,0:T(8,128)(2,1)S(1)} %fusion.101, bf16[384,384]{1,0:T(8,128)(2,1)S(1)} %get-tuple-element.21), kind=kOutput, calls=%fused_computation.14 | convolution fusion | flops 457998336 | bytes 2064384 | tf_op jit(solution)/shard_map/dot_general | solution.py:93
  7.8 0.9 %fusion = f32[2,6,128]{2,0,1:T(2,128)S(1)} fusion(bf16[2,384,384,1]{2,1,0,3:T(8,128)(2,1)S(1)} %bitcast.271, f32[6,384,128]{1,2,0:T(8,128)S(1)} %fusion.14, bf16[6,128,384]{2,1,0:T(8,128)(2,1)S(1)} %convolution_convert_fusion.7), kind=kOutput, calls=%fused_computation.3 | convolution fusion | flops 454162944 | bytes 2365440 | tf_op jit(solution)/shard_map/pik,gjk->pgij/dot_general | solution.py:96
  8.7 3.1 %collective-permute-start.5 = (f32[2,6,128]{2,0,1:T(2,128)S(1)}, f32[2,6,128]{2,0,1:T(2,128)S(1)}, u32[]{:S(2)}, u32[]{:S(2)}) collective-permute-start(f32[2,6,128]{2,0,1:T(2,128)S(1)} %bitcast_subtract_fusion), channel_id=1, source_target_pairs={{0,1},{1,2},{2,3},{3,0},{4,5},{5,6},{6,7},{7,4},{8,9},{9,10},{10,1... | collective-permute-start | bytes 18440 | tf_op jit(solution)/shard_map/ppermute | solution.py:49
  11.8 2.6 %collective-permute-start.6 = (f32[2,6,128]{2,0,1:T(2,128)S(1)}, f32[2,6,128]{2,0,1:T(2,128)S(1)}, u32[]{:S(2)}, u32[]{:S(2)}) collective-permute-start(f32[2,6,128]{2,0,1:T(2,128)S(1)} %bitcast_subtract_fusion), channel_id=1, source_target_pairs={{0,2},{1,3},{2,0},{3,1},{4,6},{5,7},{6,4},{7,5},{8,10},{9,11},{10,... | collective-permute-start | bytes 18440 | tf_op jit(solution)/shard_map/ppermute | solution.py:49
  14.4 1.3 %collective-permute-start.7 = (f32[2,6,128]{2,0,1:T(2,128)S(1)}, f32[2,6,128]{2,0,1:T(2,128)S(1)}, u32[]{:S(2)}, u32[]{:S(2)}) collective-permute-start(f32[2,6,128]{2,0,1:T(2,128)S(1)} %bitcast_subtract_fusion), channel_id=1, source_target_pairs={{0,3},{1,0},{2,1},{3,2},{4,7},{5,4},{6,5},{7,6},{8,11},{9,8},{10,9... | collective-permute-start | bytes 18440 | tf_op jit(solution)/shard_map/ppermute | solution.py:49
  15.8 1.3 %collective-permute-start = (bf16[2,384,384]{2,1,0:T(8,128)(2,1)S(1)}, bf16[2,384,384]{2,1,0:T(8,128)(2,1)S(1)}, u32[]{:S(2)}, u32[]{:S(2)}) collective-permute-start(bf16[2,384,384]{2,1,0:T(8,128)(2,1)S(1)} %bitcast.257), channel_id=1, source_target_pairs={{0,4},{4,8},{8,12},{1,5},{5,9},{9,13},{2,6},{6,10},{10,14},{3,7},{... | collective-permute-start | bytes 1769480 | tf_op jit(solution)/shard_map/ppermute | solution.py:148
  17.1 1.3 %collective-permute-start.1 = (bf16[2,384,384]{2,1,0:T(8,128)(2,1)S(1)}, bf16[2,384,384]{2,1,0:T(8,128)(2,1)S(1)}, u32[]{:S(2)}, u32[]{:S(2)}) collective-permute-start(bf16[2,384,384]{2,1,0:T(8,128)(2,1)S(1)} %bitcast.258), channel_id=1, source_target_pairs={{4,0},{8,4},{12,8},{5,1},{9,5},{13,9},{6,2},{10,6},{14,10},{7,3},{... | collective-permute-start | bytes 1769480 | tf_op jit(solution)/shard_map/ppermute | solution.py:149
  18.5 1.3 %fusion.16 = bf16[2,96,6,128,1]{3,1,2,0,4:T(8,128)(2,1)S(1)} fusion(s32[6,128]{1,0:T(8,128)S(1)} %iota_add_fusion, bf16[2,384,384]{2,1,0:T(8,128)(2,1)} %constant.53.clone, s32[]{:T(128)S(6)} %select_n.28), kind=kOutput, calls=%fused_computation.37 | convolution fusion | flops 113688576 | bytes 445444 | tf_op jit(solution)/shard_map/aij,gjr->aigr/dot_general | solution.py:104
  19.8 1.6 %convolution_bitcast_fusion.5 = f32[2,2,96,384]{3,2,0,1:T(8,128)} fusion(bf16[2,96,6,128,1]{3,1,2,0,4:T(8,128)(2,1)S(1)} %fusion.16, bf16[6,128,384]{2,1,0:T(8,128)(2,1)S(1)} %convolution_convert_fusion.7, f32[2,6,128]{2,1,0:T(8,128)S(1)} %copy.14, f32[6,128,128]{2,1,0:T(8,128)S(1)} %bitcast_convert_fusion), kind=kOutput, calls=%fused_computation.19 | convolution fusion | flops 378470400 | bytes 1873920 | tf_op jit(solution)/shard_map/aigr,bgrk->abik/dot_general | solution.py:115
  21.4 1.8 %fusion.92 = (bf16[1,1,96,384]{3,2,0,1:T(8,128)(2,1)}, bf16[1,1,96,384]{3,2,0,1:T(8,128)(2,1)}) fusion(f32[2,2,96,384]{3,2,0,1:T(8,128)} %convolution_bitcast_fusion.5), kind=kLoop, calls=%fused_computation.136 | loop fusion | flops 221184 | bytes 737280 | tf_op jit(solution)/shard_map/convert.11
  23.2 1.8 %dynamic-slice_bitcast_fusion.2 = (bf16[2,96,384]{2,1,0:T(8,128)(2,1)}, bf16[2,96,384]{2,1,0:T(8,128)(2,1)}, bf16[2,96,384]{2,1,0:T(8,128)(2,1)}) fusion(bf16[1,2,384,384]{3,2,1,0:T(8,128)(2,1)} %param.10, s32[]{:T(128)S(6)} %select_n.30, s32[]{:T(128)S(6)} %select_n.32, s32[]{:T(128)S(6)} %select_n.34), kind=kLoop, calls=%fused_computation.142 | loop fusion | bytes 884748 | tf_op jit(solution)/shard_map/dynamic_slice | solution.py:56
  25.0 0.9 %constant_dynamic-slice_fusion = bf16[1,2,96,384]{3,2,0,1:T(8,128)(2,1)S(1)} fusion(bf16[1,2,384,384]{3,2,0,1:T(8,128)(2,1)} %bitcast.259, s32[]{:T(128)S(6)} %select_n.28), kind=kLoop, calls=%fused_computation.153 | loop fusion | bytes 294916 | tf_op jit(solution)/shard_map/dynamic_slice | solution.py:53
  26.0 0.5 collective-permute-start.4
  26.5 1.6 %convolution_bitcast_fusion.4 = f32[2,2,96,384]{3,2,0,1:T(8,128)} fusion(bf16[2,96,6,128,1]{3,1,2,0,4:T(8,128)(2,1)S(1)} %fusion.16, bf16[6,128,384]{2,1,0:T(8,128)(2,1)S(1)} %convolution_convert_fusion.7, f32[2,6,128]{2,1,0:T(8,128)S(1)} %copy.15, f32[6,128,128]{2,1,0:T(8,128)S(1)} %bitcast_convert_fusion), kind=kOutput, calls=%fused_computation.18 | convolution fusion | flops 378470400 | bytes 1873920 | tf_op jit(solution)/shard_map/aigr,bgrk->abik/dot_general | solution.py:115
  28.0 1.8 %fusion.88 = (bf16[1,1,96,384]{3,2,0,1:T(8,128)(2,1)}, bf16[1,1,96,384]{3,2,0,1:T(8,128)(2,1)}) fusion(f32[2,2,96,384]{3,2,0,1:T(8,128)} %convolution_bitcast_fusion.4), kind=kLoop, calls=%fused_computation.130 | loop fusion | flops 221184 | bytes 737280 | tf_op jit(solution)/shard_map/convert.9
  29.8 1.6 %collective-permute-start.2 = (bf16[2,96,384]{2,1,0:T(8,128)(2,1)}, bf16[2,96,384]{2,1,0:T(8,128)(2,1)S(1)}, u32[]{:S(2)}, u32[]{:S(2)}) collective-permute-start(bf16[2,96,384]{2,1,0:T(8,128)(2,1)} %get-tuple-element.23), channel_id=1, source_target_pairs={{0,1},{1,2},{2,3},{3,0},{4,5},{5,6},{6,7},{7,4},{8,9},{9,10},{10,1... | collective-permute-start | bytes 442376 | tf_op jit(solution)/shard_map/ppermute | solution.py:49
  31.4 1.6 %convolution_bitcast_fusion.3 = f32[2,2,96,384]{3,2,0,1:T(8,128)} fusion(bf16[2,96,6,128,1]{3,1,2,0,4:T(8,128)(2,1)S(1)} %fusion.16, bf16[6,128,384]{2,1,0:T(8,128)(2,1)S(1)} %convolution_convert_fusion.7, f32[2,6,128]{2,1,0:T(8,128)S(1)} %copy.16, f32[6,128,128]{2,1,0:T(8,128)S(1)} %bitcast_convert_fusion), kind=kOutput, calls=%fused_computation.17 | convolution fusion | flops 378470400 | bytes 1873920 | tf_op jit(solution)/shard_map/aigr,bgrk->abik/dot_general | solution.py:115
  33.0 1.8 %fusion.84 = (bf16[1,1,96,384]{3,2,0,1:T(8,128)(2,1)}, bf16[1,1,96,384]{3,2,0,1:T(8,128)(2,1)}) fusion(f32[2,2,96,384]{3,2,0,1:T(8,128)} %convolution_bitcast_fusion.3), kind=kLoop, calls=%fused_computation.124 | loop fusion | flops 221184 | bytes 737280 | tf_op jit(solution)/shard_map/convert.7
  35.0 1.6 %convolution_bitcast_fusion.2 = f32[2,2,96,384]{3,2,0,1:T(8,128)} fusion(bf16[2,96,6,128,1]{3,1,2,0,4:T(8,128)(2,1)S(1)} %fusion.16, bf16[6,128,384]{2,1,0:T(8,128)(2,1)S(1)} %convolution_convert_fusion.7, f32[2,6,128]{2,1,0:T(8,128)S(1)} %copy.17, f32[6,128,128]{2,1,0:T(8,128)S(1)} %bitcast_convert_fusion), kind=kOutput, calls=%fused_computation.16 | convolution fusion | flops 378470400 | bytes 1873920 | tf_op jit(solution)/shard_map/aigr,bgrk->abik/dot_general | solution.py:115
  36.5 1.2 %fusion.80 = (bf16[1,1,96,384]{3,2,0,1:T(8,128)(2,1)S(1)}, bf16[1,1,96,384]{3,2,0,1:T(8,128)(2,1)S(1)}) fusion(f32[2,2,96,384]{3,2,0,1:T(8,128)} %convolution_bitcast_fusion.2), kind=kLoop, calls=%fused_computation.118 | loop fusion | flops 221184 | bytes 737280 | tf_op jit(solution)/shard_map/convert.5
  37.7 2.1 %convolution_bitcast_fusion = f32[2,2,4,96,384]{4,3,0,2,1:T(8,128)S(1)} fusion(bf16[2,384,384,1,1]{2,1,0,4,3:T(8,128)(2,1)} %constant.61, bf16[1,1,96,384]{3,2,0,1:T(8,128)(2,1)S(1)} %get-tuple-element.20, bf16[1,1,96,384]{3,2,0,1:T(8,128)(2,1)S(1)} %get-tuple-element.19, bf16[1,1,96,384]{3,2,0,1:T(8,128)(2,1)} %get-tuple-element.18, ...), kind=kOutput, calls=%fused_computation.4 | convolution fusion | flops 455049216 | bytes 3538944 | tf_op jit(solution)/shard_map/bcij,ajk->abcik/dot_general | solution.py:120
  39.8 5.9 %collective-permute-done.3 = bf16[2,96,384]{2,1,0:T(8,128)(2,1)} collective-permute-done((bf16[2,96,384]{2,1,0:T(8,128)(2,1)}, bf16[2,96,384]{2,1,0:T(8,128)(2,1)}, u32[]{:S(2)}, u32[]{:S(2)}) %collective-permute-start.3) | collective-permute-done | bytes 147488 | tf_op jit(solution)/shard_map/ppermute | solution.py:49
  45.7 1.0 %maximum_convert_fusion = f32[4,2,96,384]{3,2,0,1:T(8,128)S(1)} fusion(bf16[1,2,96,384]{3,2,0,1:T(8,128)(2,1)S(1)} %bitcast.265, bf16[1,2,96,384]{3,2,0,1:T(8,128)(2,1)} %bitcast.8, bf16[1,2,96,384]{3,2,0,1:T(8,128)(2,1)S(1)} %bitcast.266, bf16[1,2,96,384]{3,2,0,1:T(8,128)(2,1)S(1)} %constant_dynamic-slice_fusion), kind=kLoop, calls=%fused_computation.74 | loop fusion | flops 1179648 | bytes 1769472 | tf_op jit(solution)/shard_map/convert_element_type | solution.py:122
  47.2 0.4 fusion.32
  47.7 0.5 subtract_bitcast_fusion
  48.1 16.7 %all_gather.3 = bf16[2,384,384]{2,1,0:T(8,128)(2,1)S(1)} all-gather(bf16[2,96,384]{2,1,0:T(8,128)(2,1)S(1)} %pad_maximum_fusion.1), channel_id=1, replica_groups=mesh['grp'=2,'frame'=4,'coil'=4] {'coil'}, dimensions={1}, use_global_device_ids=true | all-gather | bytes 737280 | tf_op jit(solution)/shard_map/all_gather | solution.py:189
  64.8 1.2 %fusion.12 = f32[1,2,384,384]{3,2,1,0:T(8,128)} fusion(f32[1,2,384,384]{3,2,1,0:T(8,128)S(1)} %subtract_bitcast_fusion, bf16[1,2,384,384]{3,2,1,0:T(8,128)(2,1)S(1)} %copy-done, bf16[2,384,384]{2,1,0:T(8,128)(2,1)S(1)} %all_gather.3), kind=kLoop, calls=%fused_computation.29 | loop fusion | flops 1474560 | bytes 3538944 | tf_op jit(solution)/shard_map/sub | solution.py:190
  (47 shorter events, 3.4 us)
Async XLA Ops:
  0.0 1.2 %copy-start.1 = (bf16[1,2,384,384]{3,2,1,0:T(8,128)(2,1)S(1)}, bf16[1,2,384,384]{3,2,1,0:T(8,128)(2,1)}, u32[]{:S(2)}) copy-start(bf16[1,2,384,384]{3,2,1,0:T(8,128)(2,1)} %param.10) | copy-start | bytes 1769476
  1.3 1.1 %copy-start.3 = (bf16[2,384,384,1]{2,1,0,3:T(8,128)(2,1)S(1)}, bf16[2,384,384,1]{2,1,0,3:T(8,128)(2,1)}, u32[]{:S(2)}) copy-start(bf16[2,384,384,1]{2,1,0,3:T(8,128)(2,1)} %constant.60) | copy-start | bytes 1769476
  3.2 1.1 %copy-start.2 = (bf16[2,384,384]{2,1,0:T(8,128)(2,1)S(1)}, bf16[2,384,384]{2,1,0:T(8,128)(2,1)}, u32[]{:S(2)}) copy-start(bf16[2,384,384]{2,1,0:T(8,128)(2,1)} %constant.53.clone) | copy-start | bytes 1769476
  4.2 0.7 copy-start.8
  4.2 0.7 %copy-start.9 = (s32[1,6]{1,0:T(1,128)S(1)}, s32[1,6]{1,0:T(1,128)}, u32[]{:S(2)}) copy-start(s32[1,6]{1,0:T(1,128)} %param.14) | copy-start | bytes 76
  4.2 1.1 %copy-start.4 = (bf16[16,128,128]{2,1,0:T(8,128)(2,1)S(1)}, bf16[16,128,128]{2,1,0:T(8,128)(2,1)}, u32[]{:S(2)}) copy-start(bf16[16,128,128]{2,1,0:T(8,128)(2,1)} %param.16) | copy-start | bytes 1572868
  4.2 1.1 %copy-start.7 = (s32[1,6]{1,0:T(1,128)S(1)}, s32[1,6]{1,0:T(1,128)}, u32[]{:S(2)}) copy-start(s32[1,6]{1,0:T(1,128)} %param.12) | copy-start | bytes 76
  4.2 1.5 %copy-start.5 = (bf16[16,128,128]{2,1,0:T(8,128)(2,1)S(1)}, bf16[16,128,128]{2,1,0:T(8,128)(2,1)}, u32[]{:S(2)}) copy-start(bf16[16,128,128]{2,1,0:T(8,128)(2,1)} %param.15) | copy-start | bytes 1572868
  7.8 0.9 %copy-start.6 = (f32[1,1,2,6,128]{4,2,3,1,0:T(2,128)S(1)}, f32[1,1,2,6,128]{4,2,3,1,0:T(2,128)}, u32[]{:S(2)}) copy-start(f32[1,1,2,6,128]{4,2,3,1,0:T(2,128)} %param.11) | copy-start | bytes 18436
  7.8 8.0 %copy-start = (bf16[1,2,384,384]{3,2,1,0:T(8,128)(2,1)S(1)}, bf16[1,2,384,384]{3,2,1,0:T(8,128)(2,1)}, u32[]{:S(2)}) copy-start(bf16[1,2,384,384]{3,2,1,0:T(8,128)(2,1)} %param.9) | copy-start | bytes 1769476
  8.7 17.2 %collective-permute-start.5 = (f32[2,6,128]{2,0,1:T(2,128)S(1)}, f32[2,6,128]{2,0,1:T(2,128)S(1)}, u32[]{:S(2)}, u32[]{:S(2)}) collective-permute-start(f32[2,6,128]{2,0,1:T(2,128)S(1)} %bitcast_subtract_fusion), channel_id=1, source_target_pairs={{0,1},{1,2},{2,3},{3,0},{4,5},{5,6},{6,7},{7,4},{8,9},{9,10},{10,1... | collective-permute-start | bytes 18440 | tf_op jit(solution)/shard_map/ppermute | solution.py:49
  11.8 18.0 %collective-permute-start.6 = (f32[2,6,128]{2,0,1:T(2,128)S(1)}, f32[2,6,128]{2,0,1:T(2,128)S(1)}, u32[]{:S(2)}, u32[]{:S(2)}) collective-permute-start(f32[2,6,128]{2,0,1:T(2,128)S(1)} %bitcast_subtract_fusion), channel_id=1, source_target_pairs={{0,2},{1,3},{2,0},{3,1},{4,6},{5,7},{6,4},{7,5},{8,10},{9,11},{10,... | collective-permute-start | bytes 18440 | tf_op jit(solution)/shard_map/ppermute | solution.py:49
  14.4 20.4 %collective-permute-start.7 = (f32[2,6,128]{2,0,1:T(2,128)S(1)}, f32[2,6,128]{2,0,1:T(2,128)S(1)}, u32[]{:S(2)}, u32[]{:S(2)}) collective-permute-start(f32[2,6,128]{2,0,1:T(2,128)S(1)} %bitcast_subtract_fusion), channel_id=1, source_target_pairs={{0,3},{1,0},{2,1},{3,2},{4,7},{5,4},{6,5},{7,6},{8,11},{9,8},{10,9... | collective-permute-start | bytes 18440 | tf_op jit(solution)/shard_map/ppermute | solution.py:49
  15.8 31.2 %collective-permute-start = (bf16[2,384,384]{2,1,0:T(8,128)(2,1)S(1)}, bf16[2,384,384]{2,1,0:T(8,128)(2,1)S(1)}, u32[]{:S(2)}, u32[]{:S(2)}) collective-permute-start(bf16[2,384,384]{2,1,0:T(8,128)(2,1)S(1)} %bitcast.257), channel_id=1, source_target_pairs={{0,4},{4,8},{8,12},{1,5},{5,9},{9,13},{2,6},{6,10},{10,14},{3,7},{... | collective-permute-start | bytes 1769480 | tf_op jit(solution)/shard_map/ppermute | solution.py:148
  17.1 29.9 %collective-permute-start.1 = (bf16[2,384,384]{2,1,0:T(8,128)(2,1)S(1)}, bf16[2,384,384]{2,1,0:T(8,128)(2,1)S(1)}, u32[]{:S(2)}, u32[]{:S(2)}) collective-permute-start(bf16[2,384,384]{2,1,0:T(8,128)(2,1)S(1)} %bitcast.258), channel_id=1, source_target_pairs={{4,0},{8,4},{12,8},{5,1},{9,5},{13,9},{6,2},{10,6},{14,10},{7,3},{... | collective-permute-start | bytes 1769480 | tf_op jit(solution)/shard_map/ppermute | solution.py:149
  26.0 13.8 %collective-permute-start.4 = (bf16[2,96,384]{2,1,0:T(8,128)(2,1)}, bf16[2,96,384]{2,1,0:T(8,128)(2,1)S(1)}, u32[]{:S(2)}, u32[]{:S(2)}) collective-permute-start(bf16[2,96,384]{2,1,0:T(8,128)(2,1)} %get-tuple-element.25), channel_id=1, source_target_pairs={{0,3},{1,0},{2,1},{3,2},{4,7},{5,4},{6,5},{7,6},{8,11},{9,8},{10,9... | collective-permute-start | bytes 442376 | tf_op jit(solution)/shard_map/ppermute | solution.py:49
  29.8 9.9 %collective-permute-start.2 = (bf16[2,96,384]{2,1,0:T(8,128)(2,1)}, bf16[2,96,384]{2,1,0:T(8,128)(2,1)S(1)}, u32[]{:S(2)}, u32[]{:S(2)}) collective-permute-start(bf16[2,96,384]{2,1,0:T(8,128)(2,1)} %get-tuple-element.23), channel_id=1, source_target_pairs={{0,1},{1,2},{2,3},{3,0},{4,5},{5,6},{6,7},{7,4},{8,9},{9,10},{10,1... | collective-permute-start | bytes 442376 | tf_op jit(solution)/shard_map/ppermute | solution.py:49
  34.8 10.9 %collective-permute-start.3 = (bf16[2,96,384]{2,1,0:T(8,128)(2,1)}, bf16[2,96,384]{2,1,0:T(8,128)(2,1)}, u32[]{:S(2)}, u32[]{:S(2)}) collective-permute-start(bf16[2,96,384]{2,1,0:T(8,128)(2,1)} %get-tuple-element.24), channel_id=1, source_target_pairs={{0,2},{1,3},{2,0},{3,1},{4,6},{5,7},{6,4},{7,5},{8,10},{9,11},{10,... | collective-permute-start | bytes 442376 | tf_op jit(solution)/shard_map/ppermute | solution.py:49

commit v10 on v6

--- a/solution.py
+++ b/solution.py
@@ -109,7 +109,9 @@
         "aij,gjr->aigr", row_table, row_select, preferred_element_type=jnp.float32
     ).astype(jnp.bfloat16)
     products = jnp.einsum("aigr,cbgrk->abcik", table_at, placed, preferred_element_type=jnp.float32)
-    half_back = combine_parts(products, -1.0).astype(jnp.bfloat16)
+    pairs = products.reshape((4,) + products.shape[2:])
+    signs = jnp.array([-1.0, 1.0], jnp.float32).reshape((2,) + (1,) * (pairs.ndim - 1))
+    half_back = (pairs[:2] + signs * jnp.flip(pairs, 0)[:2]).astype(jnp.bfloat16)
     products = jnp.einsum("bcij,ajk->abcik", half_back, transform, preferred_element_type=jnp.float32)
     coil_back = combine_parts(products, -1.0)
     maps = map_rows.astype(jnp.float32)
@@ -142,9 +144,7 @@
     later = lax.ppermute(image, "frame", [(i + 1, i) for i in range(count - 1)])
     has_earlier = (frame_index >= 1).astype(jnp.float32)
     has_later = (frame_index <= frame_total - 2).astype(jnp.float32)
-    return (
-        normed_change(image, earlier, has_earlier) - normed_change(later, image, has_later)
-    )[None]
+    return (normed_change(image, earlier, has_earlier) - normed_change(later, image, has_later))[None]
 
 
 def body(
@@ -174,8 +174,9 @@
     residual = forward_residual(
         transform, images[0], coil_maps[0], kspace_data[0, 0], row_placed, col_placed
     )
-    moved = [rotated(residual, coil_count, shift) for shift in range(1, coil_count)]
-    residuals = jnp.stack([residual] + moved)
+    residuals = jnp.stack(
+        [residual] + [rotated(residual, coil_count, shift) for shift in range(1, coil_count)]
+    )
     grad_rows = backward_rows(
         transform, residuals, map_rows, row_select, row_w, col_placed, coil_index
     )

time: 58.7 us -> 57.5 us (0.980)
  other arithmetic: 10.4 us -> 6.9 us
  local copies, waits for them, and re-layouts: 3.6 us -> 6.46 us
    slice x0 -> x1, local copies, waits for them, and re-layouts: none -> 1.5 us  [backward_rows(): jnp.flip(pairs, 0)[:2]]
    add x2 -> x1, other arithmetic: 1.43 us -> 0.06 us  [combine_parts(): real_part = products[0, 0] + direction * products[1, 1]]
    unnamed x24 -> x28, local copies, waits for them, and re-layouts: 2.73 us -> 4.09 us
    sub x2 -> x1, other arithmetic: 1.37 us -> 0.06 us  [combine_parts(): imaginary = products[0, 1] - direction * products[1, 0]]
    convert_element_type x1, other arithmetic: 1.15 us -> 0.1 us  [backward_rows(): maps = map_rows.astype(jnp.float32)]
  transfers between devices with their start and end apart: 8 -> 8, of which waited for: 1 -> 1; matrix products, arithmetic and copies ran while one was open for 22% -> 19% of each run, Pallas kernels for 0% -> 0%
where the time goes in v10:
time: 57.5 us; the launch traced here: 57.1 us
  blocking collectives  16.7 us (29%)
  starting transfers between devices  11.9 us (21%)
  matrix products  10.6 us (18%)
  other arithmetic  6.9 us (12%)
  local copies, waits for them, and re-layouts  6.46 us (11%)
  waiting for transfers between devices  4.28 us (7%)
    all_gather x1, blocking collectives, body(): lax.all_gather(grad_rows, 'coil', axis=1, tiled=True).astype(jnp.float32)  16.7 us
    ppermute x6, starting transfers between devices, rotated(): lax.ppermute(block, 'coil', [(i, (i + shift) % coil_count) for i in range...  9.26 us
    dot_general x1, matrix products, backward_rows(): jnp.einsum('aigr,cbgrk->abcik', table_at, placed, preferred_element_type=...  4.71 us
    ppermute x6, waiting for transfers between devices, rotated(): lax.ppermute(block, 'coil', [(i, (i + shift) % coil_count) for i in range...  4.27 us
    unnamed x28, local copies, waits for them, and re-layouts  4.09 us
    slice x1, local copies, waits for them, and re-layouts, backward_rows(): jnp.flip(pairs, 0)[:2]  1.5 us
    ppermute x1, starting transfers between devices, tv_single(): lax.ppermute(image, 'frame', [(i, i + 1) for i in range(count - 1)])  1.32 us
    ppermute x1, starting transfers between devices, tv_single(): later = lax.ppermute(image, 'frame', [(i + 1, i) for i in range(count - 1)])  1.29 us
  transfers between devices with their start and end apart: 8, of which 1 were waited for; matrix products, arithmetic and copies ran while one was open for 19% of the time, Pallas kernels for 0%

profile of v10, /device:TPU:0, one launch (start us, length us, event | category | flops | bytes accessed | tf_op | source)
XLA Modules:
  0.0 57.1 jit_solution(14012004263745508153)
XLA Ops:
  0.0 1.2 %bitcast_convert_fusion.1 = f32[2,384,384]{2,1,0:T(8,128)S(1)} fusion(bf16[1,2,384,384]{3,2,1,0:T(8,128)(2,1)} %param.10), kind=kLoop, calls=%fused_computation.119 | loop fusion | flops 294912 | bytes 1769472 | tf_op jit(solution)/shard_map/convert_element_type | solution.py:135
  1.5 0.9 %copy-done.5 = bf16[2,384,384,1]{2,1,0,3:T(8,128)(2,1)S(1)} copy-done((bf16[2,384,384,1]{2,1,0,3:T(8,128)(2,1)S(1)}, bf16[2,384,384,1]{2,1,0,3:T(8,128)(2,1)}, u32[]{:S(2)}) %copy-start.5) | copy-done | bytes 589848
  2.4 0.8 %convolution_bitcast_fusion.1 = f32[2,2,384,384]{3,2,0,1:T(8,128)S(1)} fusion(bf16[2,384,384,1]{2,1,0,3:T(8,128)(2,1)S(1)} %copy-done.5, bf16[1,384,384]{2,1,0:T(8,128)(2,1)S(1)} %get-tuple-element.12, bf16[1,384,384]{2,1,0:T(8,128)(2,1)S(1)} %get-tuple-element.11), kind=kOutput, calls=%fused_computation.11 | convolution fusion | flops 454164480 | bytes 3538944 | tf_op jit(solution)/shard_map/bij,ajk->abik/dot_general | solution.py:84
  3.3 0.9 %copy-done.3 = bf16[2,384,384]{2,1,0:T(8,128)(2,1)S(1)} copy-done((bf16[2,384,384]{2,1,0:T(8,128)(2,1)S(1)}, bf16[2,384,384]{2,1,0:T(8,128)(2,1)}, u32[]{:S(2)}) %copy-start.3) | copy-done | bytes 589848
  4.4 0.5 copy-done.12
  5.7 0.4 fusion.29
  6.3 0.4 fusion.24
  6.7 0.4 convolution_convert_fusion.3
  7.1 0.8 %convolution_convert_fusion.2 = bf16[768,384]{1,0:T(8,128)(2,1)S(1)} fusion(bf16[768,384]{1,0:T(8,128)(2,1)S(1)} %bitcast.232, bf16[384,384]{1,0:T(8,128)(2,1)S(1)} %get-tuple-element.14, bf16[384,384]{1,0:T(8,128)(2,1)S(1)} %fusion.74, bf16[384,384]{1,0:T(8,128)(2,1)S(1)} %get-tuple-element.13), kind=kOutput, calls=%fused_computation.14 | convolution fusion | flops 457998336 | bytes 2064384 | tf_op jit(solution)/shard_map/dot_general | solution.py:93
  7.9 0.9 %fusion.5 = f32[2,6,128]{2,0,1:T(2,128)S(1)} fusion(bf16[2,384,384,1]{2,1,0,3:T(8,128)(2,1)S(1)} %bitcast.244, f32[6,384,128]{1,2,0:T(8,128)S(1)} %fusion.24, bf16[6,128,384]{2,1,0:T(8,128)(2,1)S(1)} %convolution_convert_fusion.3), kind=kOutput, calls=%fused_computation.8 | convolution fusion | flops 454162944 | bytes 2365440 | tf_op jit(solution)/shard_map/pik,gjk->pgij/dot_general | solution.py:96
  8.8 0.6 %bitcast_subtract_fusion = f32[2,6,128]{2,0,1:T(2,128)} fusion(f32[2,6,128]{2,0,1:T(2,128)S(1)} %fusion.5, f32[1,1,2,6,128]{4,2,3,1,0:T(2,128)S(1)} %copy-done.9), kind=kLoop, calls=%fused_computation.108 | loop fusion | flops 1536 | bytes 18432 | tf_op jit(solution)/shard_map/sub | solution.py:98
  9.4 3.1 %collective-permute-start.5 = (f32[2,6,128]{2,0,1:T(2,128)}, f32[2,6,128]{2,0,1:T(2,128)}, u32[]{:S(2)}, u32[]{:S(2)}) collective-permute-start(f32[2,6,128]{2,0,1:T(2,128)} %bitcast_subtract_fusion), channel_id=1, source_target_pairs={{0,1},{1,2},{2,3},{3,0},{4,5},{5,6},{6,7},{7,4},{8,9},{9,10},{10,1... | collective-permute-start | bytes 18440 | tf_op jit(solution)/shard_map/ppermute | solution.py:49
  12.4 2.6 %collective-permute-start.6 = (f32[2,6,128]{2,0,1:T(2,128)}, f32[2,6,128]{2,0,1:T(2,128)}, u32[]{:S(2)}, u32[]{:S(2)}) collective-permute-start(f32[2,6,128]{2,0,1:T(2,128)} %bitcast_subtract_fusion), channel_id=1, source_target_pairs={{0,2},{1,3},{2,0},{3,1},{4,6},{5,7},{6,4},{7,5},{8,10},{9,11},{10,... | collective-permute-start | bytes 18440 | tf_op jit(solution)/shard_map/ppermute | solution.py:49
  15.0 1.3 %collective-permute-start.7 = (f32[2,6,128]{2,0,1:T(2,128)}, f32[2,6,128]{2,0,1:T(2,128)}, u32[]{:S(2)}, u32[]{:S(2)}) collective-permute-start(f32[2,6,128]{2,0,1:T(2,128)} %bitcast_subtract_fusion), channel_id=1, source_target_pairs={{0,3},{1,0},{2,1},{3,2},{4,7},{5,4},{6,5},{7,6},{8,11},{9,8},{10,9... | collective-permute-start | bytes 18440 | tf_op jit(solution)/shard_map/ppermute | solution.py:49
  16.4 1.3 %collective-permute-start = (bf16[2,384,384]{2,1,0:T(8,128)(2,1)S(1)}, bf16[2,384,384]{2,1,0:T(8,128)(2,1)S(1)}, u32[]{:S(2)}, u32[]{:S(2)}) collective-permute-start(bf16[2,384,384]{2,1,0:T(8,128)(2,1)S(1)} %bitcast.229), channel_id=1, source_target_pairs={{0,4},{4,8},{8,12},{1,5},{5,9},{9,13},{2,6},{6,10},{10,14},{3,7},{... | collective-permute-start | bytes 1769480 | tf_op jit(solution)/shard_map/ppermute | solution.py:143
  17.7 1.3 %collective-permute-start.1 = (bf16[2,384,384]{2,1,0:T(8,128)(2,1)S(1)}, bf16[2,384,384]{2,1,0:T(8,128)(2,1)S(1)}, u32[]{:S(2)}, u32[]{:S(2)}) collective-permute-start(bf16[2,384,384]{2,1,0:T(8,128)(2,1)S(1)} %bitcast.230), channel_id=1, source_target_pairs={{4,0},{8,4},{12,8},{5,1},{9,5},{13,9},{6,2},{10,6},{14,10},{7,3},{... | collective-permute-start | bytes 1769480 | tf_op jit(solution)/shard_map/ppermute | solution.py:144
  19.0 0.8 %bitcast_convert_fusion = f32[6,128,128]{2,1,0:T(8,128)} fusion(bf16[1,6,128,128]{3,1,2,0:T(8,128)(2,1)S(1)} %fusion.30), kind=kLoop, calls=%fused_computation.95 | loop fusion | flops 98304 | bytes 589824 | tf_op jit(solution)/shard_map/convert_element_type | solution.py:103
  19.8 1.1 %fusion.26 = bf16[2,96,6,128,1,1]{3,1,2,0,5,4:T(8,128)(2,1)} fusion(s32[6,128]{1,0:T(8,128)S(1)} %iota_add_fusion, bf16[2,384,384]{2,1,0:T(8,128)(2,1)S(1)} %copy-done.3, s32[]{:T(128)S(6)} %select_n.28), kind=kOutput, calls=%fused_computation.37 | convolution fusion | flops 113688576 | bytes 446468 | tf_op jit(solution)/shard_map/aij,gjr->aigr/dot_general | solution.py:108
  20.9 0.8 %dynamic-slice_bitcast_fusion.2 = (bf16[2,96,384]{2,1,0:T(8,128)(2,1)}, bf16[2,96,384]{2,1,0:T(8,128)(2,1)}, bf16[2,96,384]{2,1,0:T(8,128)(2,1)}) fusion(bf16[1,2,384,384]{3,2,1,0:T(8,128)(2,1)S(1)} %copy-done.2, s32[]{:T(128)S(6)} %select_n.30, s32[]{:T(128)S(6)} %select_n.32, s32[]{:T(128)S(6)} %select_n.34), kind=kLoop, calls=%fused_computation.103 | loop fusion | bytes 884748 | tf_op jit(solution)/shard_map/dynamic_slice | solution.py:56
  21.7 0.5 collective-permute-start.4
  22.2 1.6 %collective-permute-start.2 = (bf16[2,96,384]{2,1,0:T(8,128)(2,1)}, bf16[2,96,384]{2,1,0:T(8,128)(2,1)S(1)}, u32[]{:S(2)}, u32[]{:S(2)}) collective-permute-start(bf16[2,96,384]{2,1,0:T(8,128)(2,1)} %get-tuple-element.15), channel_id=1, source_target_pairs={{0,1},{1,2},{2,3},{3,0},{4,5},{5,6},{6,7},{7,4},{8,9},{9,10},{10,1... | collective-permute-start | bytes 442376 | tf_op jit(solution)/shard_map/ppermute | solution.py:49
  24.0 0.7 %pad_maximum_fusion.2 = f32[4,2,6,128]{3,1,2,0:T(2,128)S(1)} fusion(f32[1,2,6,128]{3,1,2,0:T(2,128)} %bitcast.38, f32[1,2,6,128]{3,1,2,0:T(2,128)} %bitcast.37, f32[1,2,6,128]{3,1,2,0:T(2,128)} %bitcast.36, f32[1,2,6,128]{3,1,2,0:T(2,128)S(1)} %bitcast_subtract_fusion.1), kind=kLoop, calls=%fused_computation.107 | loop fusion | flops 18432 | bytes 49152 | tf_op jit(solution)/shard_map/stack | solution.py:177
  24.8 4.7 %fusion.6 = f32[2,2,4,96,384]{4,3,0,1,2:T(8,128)} fusion(bf16[2,96,6,128,1,1]{3,1,2,0,5,4:T(8,128)(2,1)} %fusion.26, f32[4,2,6,128]{3,2,1,0:T(8,128)S(1)} %copy.15, f32[6,128,128]{2,1,0:T(8,128)S(1)} %copy-done.8, bf16[6,128,384]{2,1,0:T(8,128)(2,1)S(1)} %convolution_convert_fusion.3), kind=kOutput, calls=%fused_computation.9 | convolution fusion | flops 1513881600 | bytes 3661824 | tf_op jit(solution)/shard_map/aigr,cbgrk->abcik/dot_general | solution.py:111
  29.5 1.5 %slice_bitcast_fusion = f32[2,4,96,384]{3,2,0,1:T(8,128)S(1)} fusion(f32[2,2,4,96,384]{4,3,0,1,2:T(8,128)} %fusion.6), kind=kLoop, calls=%fused_computation.17 | loop fusion | bytes 2359296 | tf_op jit(solution)/shard_map/slice | solution.py:114
  31.0 0.5 copy-done.1
  31.7 0.8 %copy-done.4 = bf16[2,384,384,1,1]{2,1,0,4,3:T(8,128)(2,1)S(1)} copy-done((bf16[2,384,384,1,1]{2,1,0,4,3:T(8,128)(2,1)S(1)}, bf16[2,384,384,1,1]{2,1,0,4,3:T(8,128)(2,1)}, u32[]{:S(2)}) %copy-start.4) | copy-done | bytes 589848
  32.6 0.8 %convolution_bitcast_fusion = f32[2,2,4,96,384]{4,3,0,2,1:T(8,128)S(1)} fusion(bf16[2,384,384,1,1]{2,1,0,4,3:T(8,128)(2,1)S(1)} %copy-done.4, bf16[2,4,96,384,1]{3,2,0,1,4:T(8,128)(2,1)S(1)} %fusion.31), kind=kOutput, calls=%fused_computation.10 | convolution fusion | flops 452984832 | bytes 3538944 | tf_op jit(solution)/shard_map/bcij,ajk->abcik/dot_general | solution.py:115
  33.4 4.3 %collective-permute-done.3 = bf16[2,96,384]{2,1,0:T(8,128)(2,1)S(1)} collective-permute-done((bf16[2,96,384]{2,1,0:T(8,128)(2,1)}, bf16[2,96,384]{2,1,0:T(8,128)(2,1)S(1)}, u32[]{:S(2)}, u32[]{:S(2)}) %collective-permute-start.3) | collective-permute-done | bytes 147488 | tf_op jit(solution)/shard_map/ppermute | solution.py:49
  38.3 0.4 fusion.43
  38.7 0.5 subtract_bitcast_fusion
  39.2 16.7 %all_gather.3 = bf16[2,384,384]{2,1,0:T(8,128)(2,1)S(1)} all-gather(bf16[2,96,384]{2,1,0:T(8,128)(2,1)S(1)} %pad_maximum_fusion.1), channel_id=1, replica_groups=mesh['grp'=2,'frame'=4,'coil'=4] {'coil'}, dimensions={1}, use_global_device_ids=true | all-gather | bytes 737280 | tf_op jit(solution)/shard_map/all_gather | solution.py:184
  55.9 1.3 %fusion.22 = f32[1,2,384,384]{3,2,1,0:T(8,128)} fusion(f32[1,2,384,384]{3,2,1,0:T(8,128)S(1)} %subtract_bitcast_fusion, bf16[1,2,384,384]{3,2,1,0:T(8,128)(2,1)S(1)} %copy-done, bf16[2,384,384]{2,1,0:T(8,128)(2,1)S(1)} %all_gather.3), kind=kLoop, calls=%fused_computation.29 | loop fusion | flops 1474560 | bytes 3538944 | tf_op jit(solution)/shard_map/sub | solution.py:185
  (49 shorter events, 2.5 us)
Async XLA Ops:
  0.0 1.2 %copy-start.2 = (bf16[1,2,384,384]{3,2,1,0:T(8,128)(2,1)S(1)}, bf16[1,2,384,384]{3,2,1,0:T(8,128)(2,1)}, u32[]{:S(2)}) copy-start(bf16[1,2,384,384]{3,2,1,0:T(8,128)(2,1)} %param.11) | copy-start | bytes 1769476
  1.3 1.1 %copy-start.5 = (bf16[2,384,384,1]{2,1,0,3:T(8,128)(2,1)S(1)}, bf16[2,384,384,1]{2,1,0,3:T(8,128)(2,1)}, u32[]{:S(2)}) copy-start(bf16[2,384,384,1]{2,1,0,3:T(8,128)(2,1)} %constant.62) | copy-start | bytes 1769476
  3.2 1.1 %copy-start.3 = (bf16[2,384,384]{2,1,0:T(8,128)(2,1)S(1)}, bf16[2,384,384]{2,1,0:T(8,128)(2,1)}, u32[]{:S(2)}) copy-start(bf16[2,384,384]{2,1,0:T(8,128)(2,1)} %constant.54.clone) | copy-start | bytes 1769476
  4.2 0.7 %copy-start.12 = (s32[1,6]{1,0:T(1,128)S(1)}, s32[1,6]{1,0:T(1,128)}, u32[]{:S(2)}) copy-start(s32[1,6]{1,0:T(1,128)} %param.14) | copy-start | bytes 76
  4.2 1.1 %copy-start.6 = (bf16[16,128,128]{2,1,0:T(8,128)(2,1)S(1)}, bf16[16,128,128]{2,1,0:T(8,128)(2,1)}, u32[]{:S(2)}) copy-start(bf16[16,128,128]{2,1,0:T(8,128)(2,1)} %param.16) | copy-start | bytes 1572868
  4.2 1.1 %copy-start.10 = (s32[1,6]{1,0:T(1,128)S(1)}, s32[1,6]{1,0:T(1,128)}, u32[]{:S(2)}) copy-start(s32[1,6]{1,0:T(1,128)} %param.13) | copy-start | bytes 76
  4.2 1.5 %copy-start.7 = (bf16[16,128,128]{2,1,0:T(8,128)(2,1)S(1)}, bf16[16,128,128]{2,1,0:T(8,128)(2,1)}, u32[]{:S(2)}) copy-start(bf16[16,128,128]{2,1,0:T(8,128)(2,1)} %param.17) | copy-start | bytes 1572868
  4.3 1.8 %copy-start.13 = (s32[1,6]{1,0:T(1,128)S(1)}, s32[1,6]{1,0:T(1,128)}, u32[]{:S(2)}) copy-start(s32[1,6]{1,0:T(1,128)} %param.15) | copy-start | bytes 76
  7.9 0.9 %copy-start.9 = (f32[1,1,2,6,128]{4,2,3,1,0:T(2,128)S(1)}, f32[1,1,2,6,128]{4,2,3,1,0:T(2,128)}, u32[]{:S(2)}) copy-start(f32[1,1,2,6,128]{4,2,3,1,0:T(2,128)} %param.12) | copy-start | bytes 18436
  7.9 8.5 %copy-start = (bf16[1,2,384,384]{3,2,1,0:T(8,128)(2,1)S(1)}, bf16[1,2,384,384]{3,2,1,0:T(8,128)(2,1)}, u32[]{:S(2)}) copy-start(bf16[1,2,384,384]{3,2,1,0:T(8,128)(2,1)} %param.10) | copy-start | bytes 1769476
  9.4 12.3 %collective-permute-start.5 = (f32[2,6,128]{2,0,1:T(2,128)}, f32[2,6,128]{2,0,1:T(2,128)}, u32[]{:S(2)}, u32[]{:S(2)}) collective-permute-start(f32[2,6,128]{2,0,1:T(2,128)} %bitcast_subtract_fusion), channel_id=1, source_target_pairs={{0,1},{1,2},{2,3},{3,0},{4,5},{5,6},{6,7},{7,4},{8,9},{9,10},{10,1... | collective-permute-start | bytes 18440 | tf_op jit(solution)/shard_map/ppermute | solution.py:49
  12.4 9.8 %collective-permute-start.6 = (f32[2,6,128]{2,0,1:T(2,128)}, f32[2,6,128]{2,0,1:T(2,128)}, u32[]{:S(2)}, u32[]{:S(2)}) collective-permute-start(f32[2,6,128]{2,0,1:T(2,128)} %bitcast_subtract_fusion), channel_id=1, source_target_pairs={{0,2},{1,3},{2,0},{3,1},{4,6},{5,7},{6,4},{7,5},{8,10},{9,11},{10,... | collective-permute-start | bytes 18440 | tf_op jit(solution)/shard_map/ppermute | solution.py:49
  15.0 8.8 %collective-permute-start.7 = (f32[2,6,128]{2,0,1:T(2,128)}, f32[2,6,128]{2,0,1:T(2,128)}, u32[]{:S(2)}, u32[]{:S(2)}) collective-permute-start(f32[2,6,128]{2,0,1:T(2,128)} %bitcast_subtract_fusion), channel_id=1, source_target_pairs={{0,3},{1,0},{2,1},{3,2},{4,7},{5,4},{6,5},{7,6},{8,11},{9,8},{10,9... | collective-permute-start | bytes 18440 | tf_op jit(solution)/shard_map/ppermute | solution.py:49
  16.4 21.7 %collective-permute-start = (bf16[2,384,384]{2,1,0:T(8,128)(2,1)S(1)}, bf16[2,384,384]{2,1,0:T(8,128)(2,1)S(1)}, u32[]{:S(2)}, u32[]{:S(2)}) collective-permute-start(bf16[2,384,384]{2,1,0:T(8,128)(2,1)S(1)} %bitcast.229), channel_id=1, source_target_pairs={{0,4},{4,8},{8,12},{1,5},{5,9},{9,13},{2,6},{6,10},{10,14},{3,7},{... | collective-permute-start | bytes 1769480 | tf_op jit(solution)/shard_map/ppermute | solution.py:143
  17.7 20.4 %collective-permute-start.1 = (bf16[2,384,384]{2,1,0:T(8,128)(2,1)S(1)}, bf16[2,384,384]{2,1,0:T(8,128)(2,1)S(1)}, u32[]{:S(2)}, u32[]{:S(2)}) collective-permute-start(bf16[2,384,384]{2,1,0:T(8,128)(2,1)S(1)} %bitcast.230), channel_id=1, source_target_pairs={{4,0},{8,4},{12,8},{5,1},{9,5},{13,9},{6,2},{10,6},{14,10},{7,3},{... | collective-permute-start | bytes 1769480 | tf_op jit(solution)/shard_map/ppermute | solution.py:144
  20.9 3.9 %copy-start.8 = (f32[6,128,128]{2,1,0:T(8,128)S(1)}, f32[6,128,128]{2,1,0:T(8,128)}, u32[]{:S(2)}) copy-start(f32[6,128,128]{2,1,0:T(8,128)} %bitcast_convert_fusion) | copy-start | bytes 1179652
  21.7 11.6 %collective-permute-start.4 = (bf16[2,96,384]{2,1,0:T(8,128)(2,1)}, bf16[2,96,384]{2,1,0:T(8,128)(2,1)S(1)}, u32[]{:S(2)}, u32[]{:S(2)}) collective-permute-start(bf16[2,96,384]{2,1,0:T(8,128)(2,1)} %get-tuple-element.17), channel_id=1, source_target_pairs={{0,3},{1,0},{2,1},{3,2},{4,7},{5,4},{6,5},{7,6},{8,11},{9,8},{10,9... | collective-permute-start | bytes 442376 | tf_op jit(solution)/shard_map/ppermute | solution.py:49
  22.2 11.1 %collective-permute-start.2 = (bf16[2,96,384]{2,1,0:T(8,128)(2,1)}, bf16[2,96,384]{2,1,0:T(8,128)(2,1)S(1)}, u32[]{:S(2)}, u32[]{:S(2)}) collective-permute-start(bf16[2,96,384]{2,1,0:T(8,128)(2,1)} %get-tuple-element.15), channel_id=1, source_target_pairs={{0,1},{1,2},{2,3},{3,0},{4,5},{5,6},{6,7},{7,4},{8,9},{9,10},{10,1... | collective-permute-start | bytes 442376 | tf_op jit(solution)/shard_map/ppermute | solution.py:49
  23.8 13.8 %collective-permute-start.3 = (bf16[2,96,384]{2,1,0:T(8,128)(2,1)}, bf16[2,96,384]{2,1,0:T(8,128)(2,1)S(1)}, u32[]{:S(2)}, u32[]{:S(2)}) collective-permute-start(bf16[2,96,384]{2,1,0:T(8,128)(2,1)} %get-tuple-element.16), channel_id=1, source_target_pairs={{0,2},{1,3},{2,0},{3,1},{4,6},{5,7},{6,4},{7,5},{8,10},{9,11},{10,... | collective-permute-start | bytes 442376 | tf_op jit(solution)/shard_map/ppermute | solution.py:49
  24.8 6.2 %copy-start.11 = (f32[2]{0:T(128)S(1)}, f32[2]{0:T(128)}, u32[]{:S(2)}) copy-start(f32[2]{0:T(128)} %constant.55.clone) | copy-start | bytes 28
  29.5 2.0 %copy-start.1 = (f32[2,2,4,96,384]{4,3,0,1,2:T(8,128)S(1)}, f32[2,2,4,96,384]{4,3,0,1,2:T(8,128)}, u32[]{:S(2)}) copy-start(f32[2,2,4,96,384]{4,3,0,1,2:T(8,128)} %fusion.6) | copy-start | bytes 7077892
  31.5 1.1 %copy-start.4 = (bf16[2,384,384,1,1]{2,1,0,4,3:T(8,128)(2,1)S(1)}, bf16[2,384,384,1,1]{2,1,0,4,3:T(8,128)(2,1)}, u32[]{:S(2)}) copy-start(bf16[2,384,384,1,1]{2,1,0,4,3:T(8,128)(2,1)} %constant.63) | copy-start | bytes 1769476

commit v11 on v10

--- a/solution.py
+++ b/solution.py
@@ -109,9 +109,11 @@
         "aij,gjr->aigr", row_table, row_select, preferred_element_type=jnp.float32
     ).astype(jnp.bfloat16)
     products = jnp.einsum("aigr,cbgrk->abcik", table_at, placed, preferred_element_type=jnp.float32)
-    pairs = products.reshape((4,) + products.shape[2:])
-    signs = jnp.array([-1.0, 1.0], jnp.float32).reshape((2,) + (1,) * (pairs.ndim - 1))
-    half_back = (pairs[:2] + signs * jnp.flip(pairs, 0)[:2]).astype(jnp.bfloat16)
+    signs = jnp.array([[1.0, 0.0, 0.0, -1.0], [0.0, 1.0, 1.0, 0.0]], jnp.float32)
+    half_back = jnp.einsum(
+        "oq,qcik->ocik", signs, products.reshape((4,) + products.shape[2:]),
+        precision=lax.Precision.HIGHEST,
+    ).astype(jnp.bfloat16)
     products = jnp.einsum("bcij,ajk->abcik", half_back, transform, preferred_element_type=jnp.float32)
     coil_back = combine_parts(products, -1.0)
     maps = map_rows.astype(jnp.float32)

time: 57.5 us -> 59.6 us (1.037)
  the two profiles are of different devices: /device:TPU:0 before, /device:TPU:2 now
where the time goes in v11:
time: 59.6 us; the launch traced here: 59.2 us
  blocking collectives  16.6 us (28%)
  matrix products  15.5 us (26%)
  starting transfers between devices  13.5 us (23%)
  other arithmetic  7.73 us (13%)
  local copies, waits for them, and re-layouts  5.5 us (9%)
    all_gather x1, blocking collectives, body(): lax.all_gather(grad_rows, 'coil', axis=1, tiled=True).astype(jnp.float32)  16.6 us
    ppermute x6, starting transfers between devices, rotated(): lax.ppermute(block, 'coil', [(i, (i + shift) % coil_count) for i in range...  7.93 us
    dot_general x1, matrix products, backward_rows(): jnp.einsum('oq,qcik->ocik', signs, products.reshape((4,) + products.shape...  4.87 us
    dot_general x1, matrix products, backward_rows(): jnp.einsum('aigr,cbgrk->abcik', table_at, placed, preferred_element_type=...  4.7 us
    ppermute x1, starting transfers between devices, tv_single(): later = lax.ppermute(image, 'frame', [(i + 1, i) for i in range(count - 1)])  3.64 us
    unnamed x30, local copies, waits for them, and re-layouts  2.78 us
    ppermute x1, starting transfers between devices, tv_single(): lax.ppermute(image, 'frame', [(i, i + 1) for i in range(count - 1)])  1.91 us
    transpose x1, local copies, waits for them, and re-layouts, backward_rows(): jnp.einsum('aigr,cbgrk->abcik', table_at, placed, preferred_element_type=...  1.84 us
  transfers between devices with their start and end apart: 8, of which 0 were waited for; matrix products, arithmetic and copies ran while one was open for 29% of the time, Pallas kernels for 0%

profile of v11, /device:TPU:2, one launch (start us, length us, event | category | flops | bytes accessed | tf_op | source)
XLA Modules:
  0.0 59.2 jit_solution(10103743166099576700)
XLA Ops:
  0.0 1.2 %bitcast_convert_fusion.1 = f32[2,384,384]{2,1,0:T(8,128)S(1)} fusion(bf16[1,2,384,384]{3,2,1,0:T(8,128)(2,1)} %param.10), kind=kLoop, calls=%fused_computation.117 | loop fusion | flops 294912 | bytes 1769472 | tf_op jit(solution)/shard_map/convert_element_type | solution.py:137
  1.5 0.9 %copy-done.4 = bf16[2,384,384,1]{2,1,0,3:T(8,128)(2,1)S(1)} copy-done((bf16[2,384,384,1]{2,1,0,3:T(8,128)(2,1)S(1)}, bf16[2,384,384,1]{2,1,0,3:T(8,128)(2,1)}, u32[]{:S(2)}) %copy-start.4) | copy-done | bytes 589848
  2.4 0.8 %convolution_bitcast_fusion.1 = f32[2,2,384,384]{3,2,0,1:T(8,128)S(1)} fusion(bf16[2,384,384,1]{2,1,0,3:T(8,128)(2,1)S(1)} %copy-done.4, bf16[1,384,384]{2,1,0:T(8,128)(2,1)S(1)} %get-tuple-element.12, bf16[1,384,384]{2,1,0:T(8,128)(2,1)S(1)} %get-tuple-element.11), kind=kOutput, calls=%fused_computation.13 | convolution fusion | flops 454164480 | bytes 3538944 | tf_op jit(solution)/shard_map/bij,ajk->abik/dot_general | solution.py:84
  3.3 0.9 %copy-done.2 = bf16[2,384,384]{2,1,0:T(8,128)(2,1)S(1)} copy-done((bf16[2,384,384]{2,1,0:T(8,128)(2,1)S(1)}, bf16[2,384,384]{2,1,0:T(8,128)(2,1)}, u32[]{:S(2)}) %copy-start.2) | copy-done | bytes 589848
  4.4 0.5 copy-done.13
  5.3 0.4 fusion.30
  5.7 0.4 fusion.29
  6.3 0.4 fusion.24
  6.7 0.4 convolution_convert_fusion.3
  7.1 0.8 %convolution_convert_fusion.2 = bf16[768,384]{1,0:T(8,128)(2,1)S(1)} fusion(bf16[768,384]{1,0:T(8,128)(2,1)S(1)} %bitcast.231, bf16[384,384]{1,0:T(8,128)(2,1)S(1)} %get-tuple-element.14, bf16[384,384]{1,0:T(8,128)(2,1)S(1)} %fusion.74, bf16[384,384]{1,0:T(8,128)(2,1)S(1)} %get-tuple-element.13), kind=kOutput, calls=%fused_computation.16 | convolution fusion | flops 457998336 | bytes 2064384 | tf_op jit(solution)/shard_map/dot_general | solution.py:93
  7.9 0.9 %fusion.5 = f32[2,6,128]{2,0,1:T(2,128)S(1)} fusion(bf16[2,384,384,1]{2,1,0,3:T(8,128)(2,1)S(1)} %bitcast.240, f32[6,384,128]{1,2,0:T(8,128)S(1)} %fusion.24, bf16[6,128,384]{2,1,0:T(8,128)(2,1)S(1)} %convolution_convert_fusion.3), kind=kOutput, calls=%fused_computation.8 | convolution fusion | flops 454162944 | bytes 2365440 | tf_op jit(solution)/shard_map/pik,gjk->pgij/dot_general | solution.py:96
  8.8 0.6 %bitcast_subtract_fusion = f32[2,6,128]{2,0,1:T(2,128)} fusion(f32[2,6,128]{2,0,1:T(2,128)S(1)} %fusion.5, f32[1,1,2,6,128]{4,2,3,1,0:T(2,128)S(1)} %copy-done.10), kind=kLoop, calls=%fused_computation.106 | loop fusion | flops 1536 | bytes 18432 | tf_op jit(solution)/shard_map/sub | solution.py:98
  9.4 1.6 %collective-permute-start.5 = (f32[2,6,128]{2,0,1:T(2,128)}, f32[2,6,128]{2,0,1:T(2,128)}, u32[]{:S(2)}, u32[]{:S(2)}) collective-permute-start(f32[2,6,128]{2,0,1:T(2,128)} %bitcast_subtract_fusion), channel_id=1, source_target_pairs={{0,1},{1,2},{2,3},{3,0},{4,5},{5,6},{6,7},{7,4},{8,9},{9,10},{10,1... | collective-permute-start | bytes 18440 | tf_op jit(solution)/shard_map/ppermute | solution.py:49
  11.0 2.6 %collective-permute-start.6 = (f32[2,6,128]{2,0,1:T(2,128)}, f32[2,6,128]{2,0,1:T(2,128)}, u32[]{:S(2)}, u32[]{:S(2)}) collective-permute-start(f32[2,6,128]{2,0,1:T(2,128)} %bitcast_subtract_fusion), channel_id=1, source_target_pairs={{0,2},{1,3},{2,0},{3,1},{4,6},{5,7},{6,4},{7,5},{8,10},{9,11},{10,... | collective-permute-start | bytes 18440 | tf_op jit(solution)/shard_map/ppermute | solution.py:49
  13.6 1.3 %collective-permute-start.7 = (f32[2,6,128]{2,0,1:T(2,128)}, f32[2,6,128]{2,0,1:T(2,128)}, u32[]{:S(2)}, u32[]{:S(2)}) collective-permute-start(f32[2,6,128]{2,0,1:T(2,128)} %bitcast_subtract_fusion), channel_id=1, source_target_pairs={{0,3},{1,0},{2,1},{3,2},{4,7},{5,4},{6,5},{7,6},{8,11},{9,8},{10,9... | collective-permute-start | bytes 18440 | tf_op jit(solution)/shard_map/ppermute | solution.py:49
  14.9 1.9 %collective-permute-start = (bf16[2,384,384]{2,1,0:T(8,128)(2,1)S(1)}, bf16[2,384,384]{2,1,0:T(8,128)(2,1)S(1)}, u32[]{:S(2)}, u32[]{:S(2)}) collective-permute-start(bf16[2,384,384]{2,1,0:T(8,128)(2,1)S(1)} %bitcast.227), channel_id=1, source_target_pairs={{0,4},{4,8},{8,12},{1,5},{5,9},{9,13},{2,6},{6,10},{10,14},{3,7},{... | collective-permute-start | bytes 1769480 | tf_op jit(solution)/shard_map/ppermute | solution.py:145
  16.9 3.6 %collective-permute-start.1 = (bf16[2,384,384]{2,1,0:T(8,128)(2,1)S(1)}, bf16[2,384,384]{2,1,0:T(8,128)(2,1)S(1)}, u32[]{:S(2)}, u32[]{:S(2)}) collective-permute-start(bf16[2,384,384]{2,1,0:T(8,128)(2,1)S(1)} %bitcast.228), channel_id=1, source_target_pairs={{4,0},{8,4},{12,8},{5,1},{9,5},{13,9},{6,2},{10,6},{14,10},{7,3},{... | collective-permute-start | bytes 1769480 | tf_op jit(solution)/shard_map/ppermute | solution.py:146
  20.6 0.8 %bitcast_convert_fusion = f32[6,128,128]{2,1,0:T(8,128)} fusion(bf16[1,6,128,128]{3,1,2,0:T(8,128)(2,1)S(1)} %fusion.30), kind=kLoop, calls=%fused_computation.93 | loop fusion | flops 98304 | bytes 589824 | tf_op jit(solution)/shard_map/convert_element_type | solution.py:103
  21.3 1.1 %fusion.26 = bf16[2,96,6,128,1,1]{3,1,2,0,5,4:T(8,128)(2,1)} fusion(s32[6,128]{1,0:T(8,128)S(1)} %iota_add_fusion, bf16[2,384,384]{2,1,0:T(8,128)(2,1)S(1)} %copy-done.2, s32[]{:T(128)S(6)} %select_n.28), kind=kOutput, calls=%fused_computation.36 | convolution fusion | flops 113688576 | bytes 446468 | tf_op jit(solution)/shard_map/aij,gjr->aigr/dot_general | solution.py:108
  22.5 0.8 %dynamic-slice_bitcast_fusion.2 = (bf16[2,96,384]{2,1,0:T(8,128)(2,1)}, bf16[2,96,384]{2,1,0:T(8,128)(2,1)}, bf16[2,96,384]{2,1,0:T(8,128)(2,1)}) fusion(bf16[1,2,384,384]{3,2,1,0:T(8,128)(2,1)S(1)} %copy-done.1, s32[]{:T(128)S(6)} %select_n.30, s32[]{:T(128)S(6)} %select_n.32, s32[]{:T(128)S(6)} %select_n.34), kind=kLoop, calls=%fused_computation.101 | loop fusion | bytes 884748 | tf_op jit(solution)/shard_map/dynamic_slice | solution.py:56
  23.3 0.5 collective-permute-start.4
  23.8 1.6 %collective-permute-start.2 = (bf16[2,96,384]{2,1,0:T(8,128)(2,1)}, bf16[2,96,384]{2,1,0:T(8,128)(2,1)}, u32[]{:S(2)}, u32[]{:S(2)}) collective-permute-start(bf16[2,96,384]{2,1,0:T(8,128)(2,1)} %get-tuple-element.15), channel_id=1, source_target_pairs={{0,1},{1,2},{2,3},{3,0},{4,5},{5,6},{6,7},{7,4},{8,9},{9,10},{10,1... | collective-permute-start | bytes 442376 | tf_op jit(solution)/shard_map/ppermute | solution.py:49
  25.7 0.7 %pad_maximum_fusion.2 = f32[4,2,6,128]{3,1,2,0:T(2,128)S(1)} fusion(f32[1,2,6,128]{3,1,2,0:T(2,128)} %bitcast.38, f32[1,2,6,128]{3,1,2,0:T(2,128)} %bitcast.37, f32[1,2,6,128]{3,1,2,0:T(2,128)} %bitcast.36, f32[1,2,6,128]{3,1,2,0:T(2,128)S(1)} %bitcast_subtract_fusion.1), kind=kLoop, calls=%fused_computation.105 | loop fusion | flops 18432 | bytes 49152 | tf_op jit(solution)/shard_map/stack | solution.py:179
  26.5 4.7 %fusion.8 = f32[2,2,4,96,384]{4,3,0,1,2:T(8,128)} fusion(bf16[2,96,6,128,1,1]{3,1,2,0,5,4:T(8,128)(2,1)} %fusion.26, f32[4,2,6,128]{3,2,1,0:T(8,128)S(1)} %copy.23, f32[6,128,128]{2,1,0:T(8,128)S(1)} %copy-done.9, bf16[6,128,384]{2,1,0:T(8,128)(2,1)S(1)} %copy-done.6), kind=kOutput, calls=%fused_computation.11 | convolution fusion | flops 1513881600 | bytes 3661824 | tf_op jit(solution)/shard_map/aigr,cbgrk->abcik/dot_general | solution.py:111
  31.2 1.8 %copy.24 = f32[2,2,4,96,384]{4,3,2,1,0:T(8,128)S(1)} copy(f32[2,2,4,96,384]{4,3,0,1,2:T(8,128)} %fusion.8) | data formatting | bytes 4718592 | tf_op jit(solution)/shard_map/aigr,cbgrk->abcik/transpose | solution.py:111
  33.1 4.9 %fusion.6 = bf16[4,96,384,2]{2,3,1,0:T(2,128)(2,1)S(1)} fusion(f32[2,4,1,1]{1,0,3,2:T(2,128)S(1)} %copy-done.12, f32[4,4,96,384]{3,2,1,0:T(8,128)S(1)} %bitcast.229), kind=kOutput, calls=%fused_computation.9 | convolution fusion | flops 14155776 | bytes 2949152 | tf_op jit(solution)/shard_map/oq,qcik->ocik/dot_general | solution.py:113
  37.9 0.8 %convolution_bitcast_fusion = f32[2,2,4,96,384]{4,3,0,2,1:T(8,128)S(1)} fusion(bf16[2,384,384,1,1]{2,1,0,4,3:T(8,128)(2,1)S(1)} %copy-done.3, bf16[4,96,384,2]{2,3,1,0:T(2,128)(2,1)S(1)} %fusion.6), kind=kOutput, calls=%fused_computation.12 | convolution fusion | flops 452984832 | bytes 3538944 | tf_op jit(solution)/shard_map/bcij,ajk->abcik/dot_general | solution.py:117
  38.8 1.2 %maximum_convert_fusion = f32[4,2,96,384]{3,2,0,1:T(8,128)S(1)} fusion(bf16[1,2,96,384]{3,2,0,1:T(8,128)(2,1)} %bitcast.10, bf16[1,2,96,384]{3,2,0,1:T(8,128)(2,1)} %bitcast.8, bf16[1,2,96,384]{3,2,0,1:T(8,128)(2,1)} %bitcast.6, bf16[1,2,96,384]{3,2,0,1:T(8,128)(2,1)S(1)} %constant_dynamic-slice_fusion), kind=kLoop, calls=%fused_computation.70 | loop fusion | flops 1179648 | bytes 1769472 | tf_op jit(solution)/shard_map/convert_element_type | solution.py:119
  40.5 0.4 fusion.44
  40.9 0.5 subtract_bitcast_fusion
  41.4 16.6 %all_gather.3 = bf16[2,384,384]{2,1,0:T(8,128)(2,1)S(1)} all-gather(bf16[2,96,384]{2,1,0:T(8,128)(2,1)S(1)} %pad_maximum_fusion.1), channel_id=1, replica_groups=mesh['grp'=2,'frame'=4,'coil'=4] {'coil'}, dimensions={1}, use_global_device_ids=true | all-gather | bytes 737280 | tf_op jit(solution)/shard_map/all_gather | solution.py:186
  57.9 1.3 %fusion.22 = f32[1,2,384,384]{3,2,1,0:T(8,128)} fusion(f32[1,2,384,384]{3,2,1,0:T(8,128)S(1)} %subtract_bitcast_fusion, bf16[1,2,384,384]{3,2,1,0:T(8,128)(2,1)S(1)} %copy-done, bf16[2,384,384]{2,1,0:T(8,128)(2,1)S(1)} %all_gather.3), kind=kLoop, calls=%fused_computation.27 | loop fusion | flops 1474560 | bytes 3538944 | tf_op jit(solution)/shard_map/sub | solution.py:187
  (51 shorter events, 2.0 us)
Async XLA Ops:
  0.0 1.2 %copy-start.1 = (bf16[1,2,384,384]{3,2,1,0:T(8,128)(2,1)S(1)}, bf16[1,2,384,384]{3,2,1,0:T(8,128)(2,1)}, u32[]{:S(2)}) copy-start(bf16[1,2,384,384]{3,2,1,0:T(8,128)(2,1)} %param.11) | copy-start | bytes 1769476
  1.3 1.1 %copy-start.4 = (bf16[2,384,384,1]{2,1,0,3:T(8,128)(2,1)S(1)}, bf16[2,384,384,1]{2,1,0,3:T(8,128)(2,1)}, u32[]{:S(2)}) copy-start(bf16[2,384,384,1]{2,1,0,3:T(8,128)(2,1)} %constant.62) | copy-start | bytes 1769476
  3.2 1.1 %copy-start.2 = (bf16[2,384,384]{2,1,0:T(8,128)(2,1)S(1)}, bf16[2,384,384]{2,1,0:T(8,128)(2,1)}, u32[]{:S(2)}) copy-start(bf16[2,384,384]{2,1,0:T(8,128)(2,1)} %constant.54.clone) | copy-start | bytes 1769476
  4.2 0.7 %copy-start.13 = (s32[1,6]{1,0:T(1,128)S(1)}, s32[1,6]{1,0:T(1,128)}, u32[]{:S(2)}) copy-start(s32[1,6]{1,0:T(1,128)} %param.14) | copy-start | bytes 76
  4.2 1.1 %copy-start.7 = (bf16[16,128,128]{2,1,0:T(8,128)(2,1)S(1)}, bf16[16,128,128]{2,1,0:T(8,128)(2,1)}, u32[]{:S(2)}) copy-start(bf16[16,128,128]{2,1,0:T(8,128)(2,1)} %param.16) | copy-start | bytes 1572868
  4.2 1.1 %copy-start.11 = (s32[1,6]{1,0:T(1,128)S(1)}, s32[1,6]{1,0:T(1,128)}, u32[]{:S(2)}) copy-start(s32[1,6]{1,0:T(1,128)} %param.13) | copy-start | bytes 76
  4.2 1.5 %copy-start.8 = (bf16[16,128,128]{2,1,0:T(8,128)(2,1)S(1)}, bf16[16,128,128]{2,1,0:T(8,128)(2,1)}, u32[]{:S(2)}) copy-start(bf16[16,128,128]{2,1,0:T(8,128)(2,1)} %param.17) | copy-start | bytes 1572868
  4.3 1.8 %copy-start.14 = (s32[1,6]{1,0:T(1,128)S(1)}, s32[1,6]{1,0:T(1,128)}, u32[]{:S(2)}) copy-start(s32[1,6]{1,0:T(1,128)} %param.15) | copy-start | bytes 76
  7.1 0.8 %copy-start.5 = (bf16[6,128,384]{2,1,0:T(8,128)(2,1)}, bf16[6,128,384]{2,1,0:T(8,128)(2,1)S(1)}, u32[]{:S(2)}) copy-start(bf16[6,128,384]{2,1,0:T(8,128)(2,1)S(1)} %convolution_convert_fusion.3) | copy-start | bytes 1769476
  7.9 0.9 %copy-start.10 = (f32[1,1,2,6,128]{4,2,3,1,0:T(2,128)S(1)}, f32[1,1,2,6,128]{4,2,3,1,0:T(2,128)}, u32[]{:S(2)}) copy-start(f32[1,1,2,6,128]{4,2,3,1,0:T(2,128)} %param.12) | copy-start | bytes 18436
  7.9 7.0 %copy-start = (bf16[1,2,384,384]{3,2,1,0:T(8,128)(2,1)S(1)}, bf16[1,2,384,384]{3,2,1,0:T(8,128)(2,1)}, u32[]{:S(2)}) copy-start(bf16[1,2,384,384]{3,2,1,0:T(8,128)(2,1)} %param.10) | copy-start | bytes 1769476
  9.4 13.9 %collective-permute-start.5 = (f32[2,6,128]{2,0,1:T(2,128)}, f32[2,6,128]{2,0,1:T(2,128)}, u32[]{:S(2)}, u32[]{:S(2)}) collective-permute-start(f32[2,6,128]{2,0,1:T(2,128)} %bitcast_subtract_fusion), channel_id=1, source_target_pairs={{0,1},{1,2},{2,3},{3,0},{4,5},{5,6},{6,7},{7,4},{8,9},{9,10},{10,1... | collective-permute-start | bytes 18440 | tf_op jit(solution)/shard_map/ppermute | solution.py:49
  11.0 12.8 %collective-permute-start.6 = (f32[2,6,128]{2,0,1:T(2,128)}, f32[2,6,128]{2,0,1:T(2,128)}, u32[]{:S(2)}, u32[]{:S(2)}) collective-permute-start(f32[2,6,128]{2,0,1:T(2,128)} %bitcast_subtract_fusion), channel_id=1, source_target_pairs={{0,2},{1,3},{2,0},{3,1},{4,6},{5,7},{6,4},{7,5},{8,10},{9,11},{10,... | collective-permute-start | bytes 18440 | tf_op jit(solution)/shard_map/ppermute | solution.py:49
  13.6 11.8 %collective-permute-start.7 = (f32[2,6,128]{2,0,1:T(2,128)}, f32[2,6,128]{2,0,1:T(2,128)}, u32[]{:S(2)}, u32[]{:S(2)}) collective-permute-start(f32[2,6,128]{2,0,1:T(2,128)} %bitcast_subtract_fusion), channel_id=1, source_target_pairs={{0,3},{1,0},{2,1},{3,2},{4,7},{5,4},{6,5},{7,6},{8,11},{9,8},{10,9... | collective-permute-start | bytes 18440 | tf_op jit(solution)/shard_map/ppermute | solution.py:49
  14.9 25.3 %collective-permute-start = (bf16[2,384,384]{2,1,0:T(8,128)(2,1)S(1)}, bf16[2,384,384]{2,1,0:T(8,128)(2,1)S(1)}, u32[]{:S(2)}, u32[]{:S(2)}) collective-permute-start(bf16[2,384,384]{2,1,0:T(8,128)(2,1)S(1)} %bitcast.227), channel_id=1, source_target_pairs={{0,4},{4,8},{8,12},{1,5},{5,9},{9,13},{2,6},{6,10},{10,14},{3,7},{... | collective-permute-start | bytes 1769480 | tf_op jit(solution)/shard_map/ppermute | solution.py:145
  16.9 23.4 %collective-permute-start.1 = (bf16[2,384,384]{2,1,0:T(8,128)(2,1)S(1)}, bf16[2,384,384]{2,1,0:T(8,128)(2,1)S(1)}, u32[]{:S(2)}, u32[]{:S(2)}) collective-permute-start(bf16[2,384,384]{2,1,0:T(8,128)(2,1)S(1)} %bitcast.228), channel_id=1, source_target_pairs={{4,0},{8,4},{12,8},{5,1},{9,5},{13,9},{6,2},{10,6},{14,10},{7,3},{... | collective-permute-start | bytes 1769480 | tf_op jit(solution)/shard_map/ppermute | solution.py:146
  21.3 5.1 %copy-start.6 = (bf16[6,128,384]{2,1,0:T(8,128)(2,1)S(1)}, bf16[6,128,384]{2,1,0:T(8,128)(2,1)}, u32[]{:S(2)}) copy-start(bf16[6,128,384]{2,1,0:T(8,128)(2,1)} %copy-done.5) | copy-start | bytes 1769476
  22.5 4.0 %copy-start.9 = (f32[6,128,128]{2,1,0:T(8,128)S(1)}, f32[6,128,128]{2,1,0:T(8,128)}, u32[]{:S(2)}) copy-start(f32[6,128,128]{2,1,0:T(8,128)} %bitcast_convert_fusion) | copy-start | bytes 1179652
  23.3 15.4 %collective-permute-start.4 = (bf16[2,96,384]{2,1,0:T(8,128)(2,1)}, bf16[2,96,384]{2,1,0:T(8,128)(2,1)}, u32[]{:S(2)}, u32[]{:S(2)}) collective-permute-start(bf16[2,96,384]{2,1,0:T(8,128)(2,1)} %get-tuple-element.17), channel_id=1, source_target_pairs={{0,3},{1,0},{2,1},{3,2},{4,7},{5,4},{6,5},{7,6},{8,11},{9,8},{10,9... | collective-permute-start | bytes 442376 | tf_op jit(solution)/shard_map/ppermute | solution.py:49
  23.8 14.9 %collective-permute-start.2 = (bf16[2,96,384]{2,1,0:T(8,128)(2,1)}, bf16[2,96,384]{2,1,0:T(8,128)(2,1)}, u32[]{:S(2)}, u32[]{:S(2)}) collective-permute-start(bf16[2,96,384]{2,1,0:T(8,128)(2,1)} %get-tuple-element.15), channel_id=1, source_target_pairs={{0,1},{1,2},{2,3},{3,0},{4,5},{5,6},{6,7},{7,4},{8,9},{9,10},{10,1... | collective-permute-start | bytes 442376 | tf_op jit(solution)/shard_map/ppermute | solution.py:49
  25.4 13.4 %collective-permute-start.3 = (bf16[2,96,384]{2,1,0:T(8,128)(2,1)}, bf16[2,96,384]{2,1,0:T(8,128)(2,1)}, u32[]{:S(2)}, u32[]{:S(2)}) collective-permute-start(bf16[2,96,384]{2,1,0:T(8,128)(2,1)} %get-tuple-element.16), channel_id=1, source_target_pairs={{0,2},{1,3},{2,0},{3,1},{4,6},{5,7},{6,4},{7,5},{8,10},{9,11},{10,... | collective-permute-start | bytes 442376 | tf_op jit(solution)/shard_map/ppermute | solution.py:49
  31.2 1.9 %copy-start.12 = (f32[2,4,1,1]{1,0,3,2:T(2,128)S(1)}, f32[2,4,1,1]{1,0,3,2:T(2,128)}, u32[]{:S(2)}) copy-start(f32[2,4,1,1]{1,0,3,2:T(2,128)} %constant.63) | copy-start | bytes 100
  33.0 4.9 %copy-start.3 = (bf16[2,384,384,1,1]{2,1,0,4,3:T(8,128)(2,1)S(1)}, bf16[2,384,384,1,1]{2,1,0,4,3:T(8,128)(2,1)}, u32[]{:S(2)}) copy-start(bf16[2,384,384,1,1]{2,1,0,4,3:T(8,128)(2,1)} %constant.64) | copy-start | bytes 1769476

commit v12 on v10

--- a/solution.py
+++ b/solution.py
@@ -50,10 +50,11 @@
 
 
 def exchange_rows(coil_map, rows, coil_count, coil_index):
-    received = [lax.dynamic_slice_in_dim(coil_map, coil_index * rows, rows, axis=1)]
+    wide = coil_map.astype(jnp.float32)
+    received = [lax.dynamic_slice_in_dim(wide, coil_index * rows, rows, axis=1)]
     for shift in range(1, coil_count):
         target = (coil_index + shift) % coil_count
-        block = lax.dynamic_slice_in_dim(coil_map, target * rows, rows, axis=1)
+        block = lax.dynamic_slice_in_dim(wide, target * rows, rows, axis=1)
         received.append(rotated(block, coil_count, shift))
     return jnp.stack(received)
 
@@ -109,9 +110,7 @@
         "aij,gjr->aigr", row_table, row_select, preferred_element_type=jnp.float32
     ).astype(jnp.bfloat16)
     products = jnp.einsum("aigr,cbgrk->abcik", table_at, placed, preferred_element_type=jnp.float32)
-    pairs = products.reshape((4,) + products.shape[2:])
-    signs = jnp.array([-1.0, 1.0], jnp.float32).reshape((2,) + (1,) * (pairs.ndim - 1))
-    half_back = (pairs[:2] + signs * jnp.flip(pairs, 0)[:2]).astype(jnp.bfloat16)
+    half_back = combine_parts(products, -1.0).astype(jnp.bfloat16)
     products = jnp.einsum("bcij,ajk->abcik", half_back, transform, preferred_element_type=jnp.float32)
     coil_back = combine_parts(products, -1.0)
     maps = map_rows.astype(jnp.float32)

time: 57.5 us -> 70.6 us (1.23)
  waiting for transfers between devices: 4.28 us -> 8.99 us
  blocking collectives: 16.7 us -> 20.4 us
  matrix products: 10.6 us -> 13.5 us
  other arithmetic: 6.9 us -> 9.6 us
  local copies, waits for them, and re-layouts: 6.46 us -> 3.86 us
  starting transfers between devices: 11.9 us -> 13.5 us
    ppermute x6, waiting for transfers between devices: 4.27 us -> 8.99 us  [rotated(): lax.ppermute(block, 'coil', [(i, (i + shift) % coil_count) for i in range...]
    all_gather x1, blocking collectives: 16.7 us -> 20.4 us  [body(): lax.all_gather(grad_rows, 'coil', axis=1, tiled=True).astype(jnp.float32)]
    dot_general x1, matrix products: 1.1 us -> 3.5 us  [backward_rows(): jnp.einsum('cpgrj,gjk->cpgrk', spread, col_placed, preferred_element_type...]
    add x1 -> x2, other arithmetic: 0.06 us -> 1.86 us  [combine_parts(): real_part = products[0, 0] + direction * products[1, 1]]
    ppermute x6, starting transfers between devices: 9.26 us -> 10.9 us  [rotated(): lax.ppermute(block, 'coil', [(i, (i + shift) % coil_count) for i in range...]
    slice x1 -> x0, local copies, waits for them, and re-layouts: 1.5 us -> none  [backward_rows(): jnp.flip(pairs, 0)[:2]]
    unnamed x28 -> x22, local copies, waits for them, and re-layouts: 4.09 us -> 2.72 us
    another operation x1 -> x2, other arithmetic: 0.18 us -> 1.32 us  [the longest x1 1.13 us: exchange_rows(): return jnp.stack(received)]
  transfers between devices with their start and end apart: 8 -> 8, of which waited for: 1 -> 1; matrix products, arithmetic and copies ran while one was open for 19% -> 20% of each run, Pallas kernels for 0% -> 0%
where the time goes in v12:
time: 70.6 us; the launch traced here: 70.1 us
  blocking collectives  20.4 us (29%)
  matrix products  13.5 us (19%)
  starting transfers between devices  13.5 us (19%)
  other arithmetic  9.6 us (14%)
  waiting for transfers between devices  8.99 us (13%)
  local copies, waits for them, and re-layouts  3.86 us (5%)
    all_gather x1, blocking collectives, body(): lax.all_gather(grad_rows, 'coil', axis=1, tiled=True).astype(jnp.float32)  20.4 us
    ppermute x6, starting transfers between devices, rotated(): lax.ppermute(block, 'coil', [(i, (i + shift) % coil_count) for i in range...  10.9 us
    ppermute x6, waiting for transfers between devices, rotated(): lax.ppermute(block, 'coil', [(i, (i + shift) % coil_count) for i in range...  8.99 us
    dot_general x1, matrix products, backward_rows(): jnp.einsum('aigr,cbgrk->abcik', table_at, placed, preferred_element_type=...  5.15 us
    dot_general x1, matrix products, backward_rows(): jnp.einsum('cpgrj,gjk->cpgrk', spread, col_placed, preferred_element_type...  3.5 us
    unnamed x22, local copies, waits for them, and re-layouts  2.72 us
    add x2, other arithmetic, combine_parts(): real_part = products[0, 0] + direction * products[1, 1]  1.86 us
    broadcast_in_dim x1, other arithmetic, tv_single(): (normed_change(image, earlier, has_earlier) - normed_change(later, image,...  1.53 us
  transfers between devices with their start and end apart: 8, of which 1 were waited for; matrix products, arithmetic and copies ran while one was open for 20% of the time, Pallas kernels for 0%

profile of v12, /device:TPU:0, one launch (start us, length us, event | category | flops | bytes accessed | tf_op | source)
XLA Modules:
  0.0 70.1 jit_solution(4747520003353055886)
XLA Ops:
  0.0 1.2 %convert_element_type.75 = f32[1,2,384,384]{3,2,1,0:T(8,128)S(1)} convert(bf16[1,2,384,384]{3,2,1,0:T(8,128)(2,1)} %param.10) | non-fusion elementwise | flops 294912 | bytes 1769472 | tf_op jit(solution)/shard_map/convert_element_type | solution.py:53
  1.5 0.9 %copy-done.4 = bf16[2,384,384,1]{2,1,0,3:T(8,128)(2,1)S(1)} copy-done((bf16[2,384,384,1]{2,1,0,3:T(8,128)(2,1)S(1)}, bf16[2,384,384,1]{2,1,0,3:T(8,128)(2,1)}, u32[]{:S(2)}) %copy-start.4) | copy-done | bytes 589848
  2.4 0.8 %convolution_bitcast_fusion.1 = f32[2,2,384,384]{3,2,0,1:T(8,128)S(1)} fusion(bf16[2,384,384,1]{2,1,0,3:T(8,128)(2,1)S(1)} %copy-done.4, bf16[1,384,384]{2,1,0:T(8,128)(2,1)S(1)} %get-tuple-element.14, bf16[1,384,384]{2,1,0:T(8,128)(2,1)S(1)} %get-tuple-element.13), kind=kOutput, calls=%fused_computation.10 | convolution fusion | flops 454164480 | bytes 3538944 | tf_op jit(solution)/shard_map/bij,ajk->abik/dot_general | solution.py:85
  3.3 0.9 %copy-done.1 = bf16[2,384,384]{2,1,0:T(8,128)(2,1)S(1)} copy-done((bf16[2,384,384]{2,1,0:T(8,128)(2,1)S(1)}, bf16[2,384,384]{2,1,0:T(8,128)(2,1)}, u32[]{:S(2)}) %copy-start.1) | copy-done | bytes 589848
  4.4 0.5 copy-done.9
  5.0 0.3 copy-done.5
  5.3 0.4 fusion.23
  5.7 0.4 fusion.22
  6.3 0.4 fusion.17
  6.7 0.4 convolution_convert_fusion.3
  7.1 0.8 %convolution_convert_fusion.2 = bf16[768,384]{1,0:T(8,128)(2,1)S(1)} fusion(bf16[768,384]{1,0:T(8,128)(2,1)S(1)} %bitcast.196, bf16[384,384]{1,0:T(8,128)(2,1)S(1)} %get-tuple-element.20, bf16[384,384]{1,0:T(8,128)(2,1)S(1)} %fusion.77, bf16[384,384]{1,0:T(8,128)(2,1)S(1)} %get-tuple-element.19), kind=kOutput, calls=%fused_computation.13 | convolution fusion | flops 457998336 | bytes 2064384 | tf_op jit(solution)/shard_map/dot_general | solution.py:94
  7.9 0.9 %fusion.2 = f32[2,6,128]{2,0,1:T(2,128)S(1)} fusion(bf16[2,384,384,1]{2,1,0,3:T(8,128)(2,1)S(1)} %bitcast.209, f32[6,384,128]{1,2,0:T(8,128)S(1)} %fusion.17, bf16[6,128,384]{2,1,0:T(8,128)(2,1)S(1)} %convolution_convert_fusion.3), kind=kOutput, calls=%fused_computation.7 | convolution fusion | flops 454162944 | bytes 2365440 | tf_op jit(solution)/shard_map/pik,gjk->pgij/dot_general | solution.py:97
  8.8 3.1 %collective-permute-start.5 = (f32[2,6,128]{2,0,1:T(2,128)S(1)}, f32[2,6,128]{2,0,1:T(2,128)S(1)}, u32[]{:S(2)}, u32[]{:S(2)}) collective-permute-start(f32[2,6,128]{2,0,1:T(2,128)S(1)} %bitcast_subtract_fusion), channel_id=1, source_target_pairs={{0,1},{1,2},{2,3},{3,0},{4,5},{5,6},{6,7},{7,4},{8,9},{9,10},{10,1... | collective-permute-start | bytes 18440 | tf_op jit(solution)/shard_map/ppermute | solution.py:49
  11.9 2.6 %collective-permute-start.6 = (f32[2,6,128]{2,0,1:T(2,128)S(1)}, f32[2,6,128]{2,0,1:T(2,128)S(1)}, u32[]{:S(2)}, u32[]{:S(2)}) collective-permute-start(f32[2,6,128]{2,0,1:T(2,128)S(1)} %bitcast_subtract_fusion), channel_id=1, source_target_pairs={{0,2},{1,3},{2,0},{3,1},{4,6},{5,7},{6,4},{7,5},{8,10},{9,11},{10,... | collective-permute-start | bytes 18440 | tf_op jit(solution)/shard_map/ppermute | solution.py:49
  14.5 1.3 %collective-permute-start.7 = (f32[2,6,128]{2,0,1:T(2,128)S(1)}, f32[2,6,128]{2,0,1:T(2,128)S(1)}, u32[]{:S(2)}, u32[]{:S(2)}) collective-permute-start(f32[2,6,128]{2,0,1:T(2,128)S(1)} %bitcast_subtract_fusion), channel_id=1, source_target_pairs={{0,3},{1,0},{2,1},{3,2},{4,7},{5,4},{6,5},{7,6},{8,11},{9,8},{10,9... | collective-permute-start | bytes 18440 | tf_op jit(solution)/shard_map/ppermute | solution.py:49
  15.8 1.3 %collective-permute-start = (bf16[2,384,384]{2,1,0:T(8,128)(2,1)S(1)}, bf16[2,384,384]{2,1,0:T(8,128)(2,1)S(1)}, u32[]{:S(2)}, u32[]{:S(2)}) collective-permute-start(bf16[2,384,384]{2,1,0:T(8,128)(2,1)S(1)} %bitcast.194), channel_id=1, source_target_pairs={{0,4},{4,8},{8,12},{1,5},{5,9},{9,13},{2,6},{6,10},{10,14},{3,7},{... | collective-permute-start | bytes 1769480 | tf_op jit(solution)/shard_map/ppermute | solution.py:142
  17.2 1.3 %collective-permute-start.1 = (bf16[2,384,384]{2,1,0:T(8,128)(2,1)S(1)}, bf16[2,384,384]{2,1,0:T(8,128)(2,1)}, u32[]{:S(2)}, u32[]{:S(2)}) collective-permute-start(bf16[2,384,384]{2,1,0:T(8,128)(2,1)S(1)} %bitcast.195), channel_id=1, source_target_pairs={{4,0},{8,4},{12,8},{5,1},{9,5},{13,9},{6,2},{10,6},{14,10},{7,3},{... | collective-permute-start | bytes 1769480 | tf_op jit(solution)/shard_map/ppermute | solution.py:143
  18.6 1.1 %constant_dynamic-slice_fusion = (f32[1,2,96,384]{3,2,1,0:T(8,128)}, f32[2,96,384]{2,1,0:T(8,128)}, f32[2,96,384]{2,1,0:T(8,128)}, f32[2,96,384]{2,1,0:T(8,128)}) fusion(f32[1,2,384,384]{3,2,1,0:T(8,128)S(1)} %convert_element_type.75, s32[]{:T(128)S(6)} %select_n.28, s32[]{:T(128)S(6)} %select_n.34, s32[]{:T(128)S(6)} %select_n.32, s32[]{:T(128)S(6)} %select_n.30), kind=kLoop, calls=%fused_computation.118 | loop fusion | bytes 2359312 | tf_op jit(solution)/shard_map/dynamic_slice | solution.py:54
  19.6 0.7 collective-permute-start.2
  20.3 0.3 collective-permute-start.3
  20.7 2.9 %collective-permute-start.4 = (f32[2,96,384]{2,1,0:T(8,128)}, f32[2,96,384]{2,1,0:T(8,128)}, u32[]{:S(2)}, u32[]{:S(2)}) collective-permute-start(f32[2,96,384]{2,1,0:T(8,128)} %get-tuple-element.16), channel_id=1, source_target_pairs={{0,3},{1,0},{2,1},{3,2},{4,7},{5,4},{6,5},{7,6},{8,11},{9,8},{10,9... | collective-permute-start | bytes 884744 | tf_op jit(solution)/shard_map/ppermute | solution.py:49
  23.6 3.5 %convert_bitcast_fusion = bf16[4,2,6,128,384,1]{4,3,2,1,0,5:T(8,128)(2,1)} fusion(f32[4,2,6,128]{3,2,1,0:T(8,128)S(1)} %copy.14, f32[6,128,128]{2,1,0:T(8,128)S(1)} %bitcast_convert_fusion, bf16[6,128,384]{2,1,0:T(8,128)(2,1)S(1)} %convolution_convert_fusion.3), kind=kOutput, calls=%fused_computation.4 | convolution fusion | flops 607911936 | bytes 5726208 | tf_op jit(solution)/shard_map/cpgrj,gjk->cpgrk/dot_general | solution.py:105
  27.1 5.1 %fusion.3 = f32[2,2,4,96,384]{4,3,2,1,0:T(8,128)} fusion(bf16[4,2,6,128,384,1]{4,3,2,1,0,5:T(8,128)(2,1)} %convert_bitcast_fusion, s32[6,128]{1,0:T(8,128)S(1)} %iota_add_fusion, bf16[2,384,384]{2,1,0:T(8,128)(2,1)} %constant.52.clone, s32[]{:T(128)S(6)} %select_n.28), kind=kOutput, calls=%fused_computation.8 | convolution fusion | flops 1019658240 | bytes 7228420 | tf_op jit(solution)/shard_map/aigr,cbgrk->abcik/dot_general | solution.py:112
  32.2 1.8 %fusion.60 = (bf16[1,4,96,384]{3,2,1,0:T(8,128)(2,1)S(1)}, bf16[1,4,96,384]{3,2,1,0:T(8,128)(2,1)S(1)}) fusion(f32[2,2,4,96,384]{4,3,2,1,0:T(8,128)} %fusion.3), kind=kLoop, calls=%fused_computation.92 | loop fusion | flops 884736 | bytes 2949120 | tf_op jit(solution)/shard_map/add | solution.py:43
  34.0 0.8 %convolution_bitcast_fusion = f32[2,2,4,96,384]{4,3,2,1,0:T(8,128)S(1)} fusion(bf16[2,384,384,1,1]{2,1,4,3,0:T(8,128)(2,1)S(1)} %copy-done.3, bf16[1,4,96,384]{3,2,1,0:T(8,128)(2,1)S(1)} %get-tuple-element.12, bf16[1,4,96,384]{3,2,1,0:T(8,128)(2,1)S(1)} %get-tuple-element.11), kind=kOutput, calls=%fused_computation.9 | convolution fusion | flops 454164480 | bytes 3538944 | tf_op jit(solution)/shard_map/bcij,ajk->abcik/dot_general | solution.py:114
  34.8 9.0 %collective-permute-done.3 = f32[2,96,384]{2,1,0:T(8,128)} collective-permute-done((f32[2,96,384]{2,1,0:T(8,128)}, f32[2,96,384]{2,1,0:T(8,128)}, u32[]{:S(2)}, u32[]{:S(2)}) %collective-permute-start.3) | collective-permute-done | bytes 294944 | tf_op jit(solution)/shard_map/ppermute | solution.py:49
  43.8 1.1 %pad_maximum_fusion = f32[4,2,96,384]{3,2,1,0:T(8,128)S(1)} fusion(f32[1,2,96,384]{3,2,1,0:T(8,128)} %bitcast.9, f32[1,2,96,384]{3,2,1,0:T(8,128)} %bitcast.7, f32[1,2,96,384]{3,2,1,0:T(8,128)S(1)} %bitcast.199, f32[1,2,96,384]{3,2,1,0:T(8,128)S(1)} %copy-done.2), kind=kLoop, calls=%fused_computation.16 | loop fusion | flops 884736 | bytes 2359296 | tf_op jit(solution)/shard_map/stack | solution.py:59
  45.3 1.3 %convert_subtract_fusion.1 = (f32[2,384,384]{2,1,0:T(8,128)S(1)}, f32[2,384,384]{2,1,0:T(8,128)S(1)}) fusion(bf16[2,384,384]{2,1,0:T(8,128)(2,1)S(1)} %collective-permute-done, bf16[1,2,384,384]{3,2,1,0:T(8,128)(2,1)S(1)} %copy-done, bf16[2,384,384]{2,1,0:T(8,128)(2,1)} %collective-permute-done.1), kind=kLoop, calls=%fused_computation.32 | loop fusion | flops 1474560 | bytes 4128768 | tf_op jit(solution)/shard_map/sub | solution.py:134
  46.5 0.4 fusion.38
  47.0 1.5 %subtract_bitcast_fusion = f32[1,2,384,384]{3,2,1,0:T(8,128)S(1)} fusion(f32[384,384]{1,0:T(8,128)S(1)} %get-tuple-element.23, f32[]{:T(128)S(6)} %convert_element_type.73, f32[384,384]{1,0:T(8,128)S(1)} %get-tuple-element.24, f32[]{:T(128)S(6)} %convert_element_type.70, bf16[2,384,384]{2,1,0:T(8,128)(2,1)S(1)} %collective-permute-done, ...), kind=kLoop, calls=%fused_computation.30 | loop fusion | flops 2949120 | bytes 4128776 | tf_op jit(solution)/shard_map/broadcast_in_dim | solution.py:146
  48.5 20.4 %all_gather.3 = bf16[2,384,384]{2,1,0:T(8,128)(2,1)S(1)} all-gather(bf16[2,96,384]{2,1,0:T(8,128)(2,1)S(1)} %pad_maximum_fusion.2), channel_id=1, replica_groups=mesh['grp'=2,'frame'=4,'coil'=4] {'coil'}, dimensions={1}, use_global_device_ids=true | all-gather | bytes 737280 | tf_op jit(solution)/shard_map/all_gather | solution.py:183
  68.9 1.3 %fusion.15 = f32[1,2,384,384]{3,2,1,0:T(8,128)} fusion(f32[1,2,384,384]{3,2,1,0:T(8,128)S(1)} %subtract_bitcast_fusion, bf16[1,2,384,384]{3,2,1,0:T(8,128)(2,1)S(1)} %copy-done, bf16[2,384,384]{2,1,0:T(8,128)(2,1)S(1)} %all_gather.3), kind=kLoop, calls=%fused_computation.25 | loop fusion | flops 1474560 | bytes 3538944 | tf_op jit(solution)/shard_map/sub | solution.py:184
  (41 shorter events, 1.2 us)
Async XLA Ops:
  0.0 1.2 %copy-start = (bf16[1,2,384,384]{3,2,1,0:T(8,128)(2,1)S(1)}, bf16[1,2,384,384]{3,2,1,0:T(8,128)(2,1)}, u32[]{:S(2)}) copy-start(bf16[1,2,384,384]{3,2,1,0:T(8,128)(2,1)} %param.9) | copy-start | bytes 1769476
  1.3 1.1 %copy-start.4 = (bf16[2,384,384,1]{2,1,0,3:T(8,128)(2,1)S(1)}, bf16[2,384,384,1]{2,1,0,3:T(8,128)(2,1)}, u32[]{:S(2)}) copy-start(bf16[2,384,384,1]{2,1,0,3:T(8,128)(2,1)} %constant.59) | copy-start | bytes 1769476
  3.2 1.1 %copy-start.1 = (bf16[2,384,384]{2,1,0:T(8,128)(2,1)S(1)}, bf16[2,384,384]{2,1,0:T(8,128)(2,1)}, u32[]{:S(2)}) copy-start(bf16[2,384,384]{2,1,0:T(8,128)(2,1)} %constant.52.clone) | copy-start | bytes 1769476
  4.2 0.7 copy-start.9
  4.2 1.1 %copy-start.5 = (bf16[16,128,128]{2,1,0:T(8,128)(2,1)S(1)}, bf16[16,128,128]{2,1,0:T(8,128)(2,1)}, u32[]{:S(2)}) copy-start(bf16[16,128,128]{2,1,0:T(8,128)(2,1)} %param.15) | copy-start | bytes 1572868
  4.2 1.1 %copy-start.8 = (s32[1,6]{1,0:T(1,128)S(1)}, s32[1,6]{1,0:T(1,128)}, u32[]{:S(2)}) copy-start(s32[1,6]{1,0:T(1,128)} %param.12) | copy-start | bytes 76
  4.2 1.5 %copy-start.6 = (bf16[16,128,128]{2,1,0:T(8,128)(2,1)S(1)}, bf16[16,128,128]{2,1,0:T(8,128)(2,1)}, u32[]{:S(2)}) copy-start(bf16[16,128,128]{2,1,0:T(8,128)(2,1)} %param.16) | copy-start | bytes 1572868
  4.3 1.8 %copy-start.10 = (s32[1,6]{1,0:T(1,128)S(1)}, s32[1,6]{1,0:T(1,128)}, u32[]{:S(2)}) copy-start(s32[1,6]{1,0:T(1,128)} %param.14) | copy-start | bytes 76
  7.9 0.9 %copy-start.7 = (f32[1,1,2,6,128]{4,2,3,1,0:T(2,128)S(1)}, f32[1,1,2,6,128]{4,2,3,1,0:T(2,128)}, u32[]{:S(2)}) copy-start(f32[1,1,2,6,128]{4,2,3,1,0:T(2,128)} %param.11) | copy-start | bytes 18436
  8.8 10.8 %collective-permute-start.5 = (f32[2,6,128]{2,0,1:T(2,128)S(1)}, f32[2,6,128]{2,0,1:T(2,128)S(1)}, u32[]{:S(2)}, u32[]{:S(2)}) collective-permute-start(f32[2,6,128]{2,0,1:T(2,128)S(1)} %bitcast_subtract_fusion), channel_id=1, source_target_pairs={{0,1},{1,2},{2,3},{3,0},{4,5},{5,6},{6,7},{7,4},{8,9},{9,10},{10,1... | collective-permute-start | bytes 18440 | tf_op jit(solution)/shard_map/ppermute | solution.py:49
  11.9 8.4 %collective-permute-start.6 = (f32[2,6,128]{2,0,1:T(2,128)S(1)}, f32[2,6,128]{2,0,1:T(2,128)S(1)}, u32[]{:S(2)}, u32[]{:S(2)}) collective-permute-start(f32[2,6,128]{2,0,1:T(2,128)S(1)} %bitcast_subtract_fusion), channel_id=1, source_target_pairs={{0,2},{1,3},{2,0},{3,1},{4,6},{5,7},{6,4},{7,5},{8,10},{9,11},{10,... | collective-permute-start | bytes 18440 | tf_op jit(solution)/shard_map/ppermute | solution.py:49
  14.5 6.2 %collective-permute-start.7 = (f32[2,6,128]{2,0,1:T(2,128)S(1)}, f32[2,6,128]{2,0,1:T(2,128)S(1)}, u32[]{:S(2)}, u32[]{:S(2)}) collective-permute-start(f32[2,6,128]{2,0,1:T(2,128)S(1)} %bitcast_subtract_fusion), channel_id=1, source_target_pairs={{0,3},{1,0},{2,1},{3,2},{4,7},{5,4},{6,5},{7,6},{8,11},{9,8},{10,9... | collective-permute-start | bytes 18440 | tf_op jit(solution)/shard_map/ppermute | solution.py:49
  15.8 29.4 %collective-permute-start = (bf16[2,384,384]{2,1,0:T(8,128)(2,1)S(1)}, bf16[2,384,384]{2,1,0:T(8,128)(2,1)S(1)}, u32[]{:S(2)}, u32[]{:S(2)}) collective-permute-start(bf16[2,384,384]{2,1,0:T(8,128)(2,1)S(1)} %bitcast.194), channel_id=1, source_target_pairs={{0,4},{4,8},{8,12},{1,5},{5,9},{9,13},{2,6},{6,10},{10,14},{3,7},{... | collective-permute-start | bytes 1769480 | tf_op jit(solution)/shard_map/ppermute | solution.py:142
  17.2 28.1 %collective-permute-start.1 = (bf16[2,384,384]{2,1,0:T(8,128)(2,1)S(1)}, bf16[2,384,384]{2,1,0:T(8,128)(2,1)}, u32[]{:S(2)}, u32[]{:S(2)}) collective-permute-start(bf16[2,384,384]{2,1,0:T(8,128)(2,1)S(1)} %bitcast.195), channel_id=1, source_target_pairs={{4,0},{8,4},{12,8},{5,1},{9,5},{13,9},{6,2},{10,6},{14,10},{7,3},{... | collective-permute-start | bytes 1769480 | tf_op jit(solution)/shard_map/ppermute | solution.py:143
  19.6 15.2 %collective-permute-start.2 = (f32[2,96,384]{2,1,0:T(8,128)}, f32[2,96,384]{2,1,0:T(8,128)S(1)}, u32[]{:S(2)}, u32[]{:S(2)}) collective-permute-start(f32[2,96,384]{2,1,0:T(8,128)} %get-tuple-element.18), channel_id=1, source_target_pairs={{0,1},{1,2},{2,3},{3,0},{4,5},{5,6},{6,7},{7,4},{8,9},{9,10},{10,1... | collective-permute-start | bytes 884744 | tf_op jit(solution)/shard_map/ppermute | solution.py:49
  20.3 23.5 %collective-permute-start.3 = (f32[2,96,384]{2,1,0:T(8,128)}, f32[2,96,384]{2,1,0:T(8,128)}, u32[]{:S(2)}, u32[]{:S(2)}) collective-permute-start(f32[2,96,384]{2,1,0:T(8,128)} %get-tuple-element.17), channel_id=1, source_target_pairs={{0,2},{1,3},{2,0},{3,1},{4,6},{5,7},{6,4},{7,5},{8,10},{9,11},{10,... | collective-permute-start | bytes 884744 | tf_op jit(solution)/shard_map/ppermute | solution.py:49
  20.7 23.1 %collective-permute-start.4 = (f32[2,96,384]{2,1,0:T(8,128)}, f32[2,96,384]{2,1,0:T(8,128)}, u32[]{:S(2)}, u32[]{:S(2)}) collective-permute-start(f32[2,96,384]{2,1,0:T(8,128)} %get-tuple-element.16), channel_id=1, source_target_pairs={{0,3},{1,0},{2,1},{3,2},{4,7},{5,4},{6,5},{7,6},{8,11},{9,8},{10,9... | collective-permute-start | bytes 884744 | tf_op jit(solution)/shard_map/ppermute | solution.py:49
  32.2 1.8 %copy-start.3 = (bf16[2,384,384,1,1]{2,1,4,3,0:T(8,128)(2,1)S(1)}, bf16[2,384,384,1,1]{2,1,4,3,0:T(8,128)(2,1)}, u32[]{:S(2)}) copy-start(bf16[2,384,384,1,1]{2,1,4,3,0:T(8,128)(2,1)} %constant.60) | copy-start | bytes 1769476
  34.0 9.8 %copy-start.2 = (f32[1,2,96,384]{3,2,1,0:T(8,128)S(1)}, f32[1,2,96,384]{3,2,1,0:T(8,128)}, u32[]{:S(2)}) copy-start(f32[1,2,96,384]{3,2,1,0:T(8,128)} %get-tuple-element.15) | copy-start | bytes 884740
